TPU v7x, 32 devices: a whole 2x2x4 slice. The times are simulated.
32 devices in a mesh: hours: 2 (over y), pair: 4 (over z), win: 2 (over x), band: 2 (over core).
Axes of the slice: x: 2, y: 2, z: 4, core: 2. Of those that a mesh axis runs over, the one named last changes fastest.
Arguments:
- records: bfloat16 [256, 3, 32, 512], P(('hours', 'win'), None, 'pair'), parts along dimension 0, may hold values from -180 to 180
- valid_mask: int32 [256, 32], P(('hours', 'win'), 'pair'), parts along dimension 0, may hold values from 0 to 1, as said below
- round_keys: int32 [4], replicated, may hold values from 0 to 3, as said below
Outputs:
- correlations: float32 [4, 64, 3, 24, 256], P(None, ('hours', 'pair', 'win', 'band')), parts along dimension 1
There are 2 independent parts, one for each index of `hours`. A program takes and returns all parts, laid end to end along the dimension named above; an argument that names none is the same for every part. Nothing has to cross between parts.
Inputs may be any that keep to these rules, and one draw needn't show every extreme that they name: `valid_mask`: 1 where the window holds usable data at that station, else 0. `round_keys`: distinct; in round r every block p is paired with block p XOR round_keys[r], and 0 pairs a block with itself.
All inputs are finite; a program needn't handle non-finite values.
Results may differ from a plain program's by a relative error of at most 0.005.
Values may be sent and summed in bfloat16 or wider, within the bound.
No kernel may reach another device: no remote copies, remote signals or barrier semaphores. Data moves between devices by JAX's collectives and lax.ppermute only.
A program may use at most 192 MiB of HBM per device.

v0:
```python
import math

import jax
import jax.numpy as jnp
from jax import lax
from jax.sharding import PartitionSpec as P

FREQ = 128
NLAG = 256
ROUNDS = 4


def dft_table(sample_points, bin_count, first_bin):
    sample_moments = jnp.arange(sample_points, dtype=jnp.int32)
    spectral_bin_index = first_bin + 1 + jnp.arange(bin_count, dtype=jnp.int32)
    phase_turns = jnp.mod(sample_moments[:, None] * spectral_bin_index[None, :], sample_points)
    phases = phase_turns.astype(jnp.float32) * (2.0 * math.pi / sample_points)
    hanning_taper = 0.5 - 0.5 * jnp.cos(
        sample_moments.astype(jnp.float32) * (2.0 * math.pi / sample_points)
    )
    weight = (hanning_taper * math.sqrt(8.0 / (3.0 * sample_points)))[:, None]
    return jnp.concatenate([weight * jnp.cos(phases), -(weight * jnp.sin(phases))], axis=1).astype(
        jnp.bfloat16
    )


def lag_table(sample_points, bin_count, first_bin, lag_count, all_bins):
    spectral_bin_index = first_bin + 1 + jnp.arange(bin_count, dtype=jnp.int32)
    shifts = jnp.arange(lag_count, dtype=jnp.int32) - lag_count // 2
    phase_turns = jnp.mod(spectral_bin_index[:, None] * shifts[None, :], sample_points)
    phases = phase_turns.astype(jnp.float32) * (2.0 * math.pi / sample_points)
    lag_scale = 1.0 / math.sqrt(all_bins)
    return jnp.concatenate([jnp.cos(phases) * lag_scale, -(jnp.sin(phases) * lag_scale)], axis=0)


def whiten(spectra, validity):
    bin_count = spectra.shape[-1] // 2
    real_part = spectra[..., :bin_count]
    imag_part = spectra[..., bin_count:]
    band_power = jnp.mean(real_part * real_part + imag_part * imag_part, axis=1)
    amplitude = jnp.sqrt(jnp.maximum(band_power, 0.25))
    factor = validity[:, :, None] / amplitude
    factor = jnp.concatenate([factor, factor], axis=-1)
    return (spectra * factor[:, None]).astype(jnp.bfloat16)


def cross_spectra(own_block, partner):
    window_count, comp_count, station_count, twice_values = own_block.shape
    bin_count = twice_values // 2
    lanes = jnp.arange(twice_values, dtype=jnp.int32)
    lower = lanes < bin_count
    signs = jnp.where(lower, -1.0, 1.0).astype(partner.dtype)
    turned = jnp.roll(partner, bin_count, axis=-1) * signs
    direct = jnp.einsum("waik,wbjk->iabjk", own_block, partner, preferred_element_type=jnp.float32)
    rotated = jnp.einsum("waik,wbjk->iabjk", own_block, turned, preferred_element_type=jnp.float32)
    real_both = direct + jnp.roll(direct, bin_count, axis=-1)
    imag_both = rotated + jnp.roll(rotated, bin_count, axis=-1)
    product = jnp.where(lower, real_both, imag_both)
    return product.reshape(station_count, comp_count, comp_count * station_count, twice_values)


def to_lags(stacked_result, lag_rows):
    leading = stacked_result.shape[:-1]
    flattened = stacked_result.reshape(-1, stacked_result.shape[-1])
    lagged = jnp.dot(
        flattened, lag_rows, precision=lax.Precision.HIGHEST, preferred_element_type=jnp.float32
    )
    return lagged.reshape(leading + (lag_rows.shape[1],))


def body(records, valid_mask, round_keys):
    window_count, comp_count, station_count, sample_points = records.shape
    frequency_band_count = lax.axis_size("band")
    bin_count = FREQ // frequency_band_count
    band_index = lax.axis_index("band")
    dft_rows = dft_table(sample_points, bin_count, band_index * bin_count)
    spectra = jnp.einsum("wcsn,nk->wcsk", records, dft_rows, preferred_element_type=jnp.float32)
    validity = valid_mask.astype(jnp.float32)
    whitened = whiten(spectra, validity)
    valid_wire = validity.astype(jnp.bfloat16)
    lag_rows = lag_table(sample_points, bin_count, band_index * bin_count, NLAG, FREQ)
    my_rows = station_count // (lax.axis_size("win") * frequency_band_count)
    partner_list = jnp.bitwise_xor(lax.axis_index("pair"), round_keys)
    initial = (
        jnp.zeros((ROUNDS,) + whitened.shape, jnp.bfloat16),
        jnp.zeros((ROUNDS,) + valid_wire.shape, jnp.bfloat16),
    )
    shard_piece = (
        lax.all_gather(whitened[None], "pair", axis=0, tiled=True),
        lax.all_gather(valid_wire[None], "pair", axis=0, tiled=True),
    )
    held = shard_piece[0].shape[0]
    inside = jnp.logical_and(partner_list >= 0, partner_list < held)
    position = jnp.clip(partner_list, 0, held - 1)
    chosen_spectra = jnp.take(shard_piece[0], position, axis=0)
    chosen_valid = jnp.take(shard_piece[1], position, axis=0)
    kept_spectra = jnp.where(inside[:, None, None, None, None], chosen_spectra, initial[0])
    kept_valid = jnp.where(inside[:, None, None], chosen_valid, initial[1])
    results = []
    for round_index in range(ROUNDS):
        partner_spectra = kept_spectra[round_index]
        partner_valid = kept_valid[round_index]
        term = cross_spectra(whitened, partner_spectra)
        local_counts = jnp.einsum("wi,wj->ij", validity, partner_valid.astype(jnp.float32))
        summed = lax.psum_scatter(
            to_lags(term, lag_rows), ("win", "band"), scatter_dimension=0, tiled=True
        )
        totals = lax.psum(local_counts, "win")
        first_row = (lax.axis_index("win") * frequency_band_count + band_index) * my_rows
        row_counts = lax.dynamic_slice_in_dim(totals, first_row, my_rows, 0)
        divisor = jnp.tile(jnp.maximum(row_counts, 1.0), (1, comp_count))
        results.append(summed / divisor[:, None, :, None])
    return jnp.stack(results)


def solution(mesh):
    placed = (P(("hours", "win"), None, "pair", None), P(("hours", "win"), "pair"), P())
    return jax.shard_map(
        body,
        mesh=mesh,
        in_specs=placed,
        out_specs=P(None, ("hours", "pair", "win", "band"), None, None, None),
        check_vma=False,
    )
```

profile of v0, /device:TPU:0, one launch (start us, length us, event | category | flops | bytes accessed | tf_op | source)
XLA Modules:
  0.0 239.5 jit_solution(13563093318808857216)
XLA Ops:
  6.6 0.8 convert_bitcast_fusion
  7.4 0.6 multiply_convert_fusion.1
  8.0 0.7 fusion.6
  8.7 0.3 fusion.10
  9.0 0.1 rsqrt_multiply_fusion
  9.1 0.1 pad_maximum_fusion.1
  9.3 0.8 multiply_convert_fusion
  10.3 0.4 copy.120
  10.8 0.3 cosine_multiply_fusion
  11.1 38.9 %all-gather.5.cloned.1.call-done = bf16[256,3,8,128]{3,0,2,1:T(8,128)(2,1)} async-done(((bf16[64,3,8,128]{3,0,2,1:T(8,128)(2,1)}), bf16[256,3,8,128]{3,0,2,1:T(8,128)(2,1)}) %all-gather.5.cloned.1.call-update) | async-done | bytes 1572880 | tf_op jit(solution)/shard_map/all_gather | solution.py:89
  50.0 2.4 %copy.100 = bf16[4,64,3,8,128]{4,3,2,1,0:T(8,128)(2,1)S(1)} copy(bf16[4,64,3,8,128]{4,1,0,3,2:T(8,128)(2,1)} %bitcast.141) | data formatting | bytes 3145728 | tf_op jit(solution)/shard_map/all_gather | solution.py:89
  52.5 1.9 gather_fusion
  54.4 4.9 %copy.101 = bf16[4,64,3,8,128]{1,3,2,4,0:T(8,128)(2,1)} copy(bf16[4,64,3,8,128]{4,3,2,1,0:T(8,128)(2,1)} %gather_fusion) | data formatting | bytes 3145728 | tf_op jit(solution)/shard_map/jit(_take)/gather | solution.py:95
  59.2 2.3 select_select_fusion
  61.5 0.5 slice_bitcast_fusion.3
  62.1 3.1 %convolution_bitcast_fusion.1 = f32[8,3,3,8,128]{0,3,1,2,4:T(8,128)S(1)} fusion(bf16[64,3,8,128,1]{0,2,1,4,3:T(8,128)(2,1)S(1)} %copy.120, bf16[4,64,3,8,128]{1,3,2,4,0:T(8,128)(2,1)S(1)} %select_select_fusion), kind=kOutput, calls=%fused_computation.16 | convolution fusion | flops 9437184 | bytes 1867776 | tf_op jit(solution)/shard_map/waik,wbjk->iabjk/dot_general | solution.py:54
  65.2 5.3 %convolution_bitcast_fusion.7 = f32[8,3,3,8,128]{0,3,1,2,4:T(8,128)} fusion(bf16[64,3,8,128,1]{0,2,1,4,3:T(8,128)(2,1)S(1)} %copy.120, bf16[4,64,3,8,128]{1,3,2,4,0:T(8,128)(2,1)S(1)} %select_select_fusion), kind=kOutput, calls=%fused_computation.22 | convolution fusion | flops 9437184 | bytes 1867776 | tf_op jit(solution)/shard_map/waik,wbjk->iabjk/dot_general | solution.py:54
  70.4 3.1 %convolution_bitcast_fusion.5 = f32[8,3,3,8,128]{0,3,1,2,4:T(8,128)S(1)} fusion(bf16[64,3,8,128,1]{0,2,1,4,3:T(8,128)(2,1)S(1)} %copy.120, bf16[4,64,3,8,128]{1,3,2,4,0:T(8,128)(2,1)S(1)} %select_select_fusion), kind=kOutput, calls=%fused_computation.20 | convolution fusion | flops 9437184 | bytes 1867776 | tf_op jit(solution)/shard_map/waik,wbjk->iabjk/dot_general | solution.py:54
  73.5 5.3 %convolution_bitcast_fusion.3 = f32[8,3,3,8,128]{0,3,1,2,4:T(8,128)} fusion(bf16[64,3,8,128,1]{0,2,1,4,3:T(8,128)(2,1)S(1)} %copy.120, bf16[4,64,3,8,128]{1,3,2,4,0:T(8,128)(2,1)S(1)} %select_select_fusion), kind=kOutput, calls=%fused_computation.18 | convolution fusion | flops 9437184 | bytes 1867776 | tf_op jit(solution)/shard_map/waik,wbjk->iabjk/dot_general | solution.py:54
  78.9 2.4 %fusion.74 = (f32[8,3,3,8,64]{0,3,1,2,4:T(8,128)}, f32[8,3,3,8,64]{0,3,1,2,4:T(8,128)}) fusion(f32[8,3,3,8,128]{0,3,1,2,4:T(8,128)S(1)} %convolution_bitcast_fusion.5), kind=kLoop, calls=%fused_computation.142 | loop fusion | bytes 589824 | tf_op jit(solution)/shard_map/jit(_roll_static)/slice | solution.py:56
  81.3 2.5 %fusion.78 = (f32[8,3,3,8,64]{0,3,1,2,4:T(8,128)}, f32[8,3,3,8,64]{0,3,1,2,4:T(8,128)}) fusion(f32[8,3,3,8,128]{0,3,1,2,4:T(8,128)S(1)} %convolution_bitcast_fusion.1), kind=kLoop, calls=%fused_computation.146 | loop fusion | bytes 589824 | tf_op jit(solution)/shard_map/jit(_roll_static)/slice | solution.py:56
  83.8 0.3 fusion.79
  84.1 3.1 %convolution_bitcast_fusion.4 = f32[8,3,3,8,128]{0,3,1,2,4:T(8,128)S(1)} fusion(bf16[64,3,8,128,1]{0,2,1,4,3:T(8,128)(2,1)S(1)} %copy.120, bf16[64,3,8,64]{0,2,1,3:T(8,128)(2,1)S(1)} %get-tuple-element.49, bf16[64,3,8,64]{0,2,1,3:T(8,128)(2,1)S(1)} %get-tuple-element.50, bf16[128]{0:T(256)(128)(2,1)S(1)} %select_convert_fusion), kind=kOutput, calls=%fused_computation.19 | convolution fusion | flops 10616832 | bytes 1081600 | tf_op jit(solution)/shard_map/waik,wbjk->iabjk/dot_general | solution.py:55
  87.2 2.6 %fusion.73 = (f32[8,3,3,8,64]{0,3,1,2,4:T(8,128)}, f32[8,3,3,8,64]{0,3,1,2,4:T(8,128)}) fusion(f32[8,3,3,8,128]{0,3,1,2,4:T(8,128)S(1)} %convolution_bitcast_fusion.4), kind=kLoop, calls=%fused_computation.141 | loop fusion | bytes 589824 | tf_op jit(solution)/shard_map/jit(_roll_static)/slice | solution.py:57
  89.8 0.9 copy-done.3
  90.7 9.5 %fusion.1 = f32[8,3,3,8,128]{0,3,1,2,4:T(8,128)} fusion(f32[8,3,3,8,128]{0,3,1,2,4:T(8,128)} %copy-done.2, f32[8,3,3,8,64]{0,3,1,2,4:T(8,128)} %get-tuple-element.18, f32[8,3,3,8,64]{0,3,1,2,4:T(8,128)} %get-tuple-element.17, f32[8,3,3,8,128]{0,3,1,2,4:T(8,128)} %copy-done.3, f32[8,3,3,8,64]{0,3,1,2,4:T(8,128)} %get-tuple-element.16, ...), kind=kLoop, calls=%fused_computation.6 | loop fusion | flops 368640 | bytes 1474688 | tf_op jit(solution)/shard_map/jit(_where)/select_n | solution.py:58
  100.2 4.4 %copy.108 = f32[8,3,3,8,128]{4,3,2,1,0:T(8,128)} copy(f32[8,3,3,8,128]{0,3,1,2,4:T(8,128)} %fusion.1) | data formatting | bytes 589824 | tf_op jit(solution)/shard_map/jit(_where)/select_n | solution.py:58
  104.7 2.4 fusion.43
  107.1 0.3 fusion.81
  107.4 2.9 %convolution_bitcast_fusion = f32[8,3,3,8,128]{0,3,1,2,4:T(8,128)S(1)} fusion(bf16[64,3,8,128,1]{0,2,1,4,3:T(8,128)(2,1)S(1)} %copy.120, bf16[64,3,8,64]{0,2,1,3:T(8,128)(2,1)S(1)} %get-tuple-element.51, bf16[64,3,8,64]{0,2,1,3:T(8,128)(2,1)S(1)} %get-tuple-element.52, bf16[128]{0:T(256)(128)(2,1)S(1)} %select_convert_fusion), kind=kOutput, calls=%fused_computation.15 | convolution fusion | flops 10616832 | bytes 1081600 | tf_op jit(solution)/shard_map/waik,wbjk->iabjk/dot_general | solution.py:55
  110.3 2.7 %fusion.77 = (f32[8,3,3,8,64]{0,3,1,2,4:T(8,128)}, f32[8,3,3,8,64]{0,3,1,2,4:T(8,128)}) fusion(f32[8,3,3,8,128]{0,3,1,2,4:T(8,128)S(1)} %convolution_bitcast_fusion), kind=kLoop, calls=%fused_computation.145 | loop fusion | bytes 589824 | tf_op jit(solution)/shard_map/jit(_roll_static)/slice | solution.py:57
  113.0 0.9 copy-done.5
  113.8 2.9 %convolution_bitcast_fusion.6 = f32[8,3,3,8,128]{0,3,1,2,4:T(8,128)S(1)} fusion(bf16[64,3,8,128,1]{0,2,1,4,3:T(8,128)(2,1)S(1)} %copy.120, bf16[64,3,8,64]{0,2,1,3:T(8,128)(2,1)S(1)} %get-tuple-element.32, bf16[64,3,8,64]{0,2,1,3:T(8,128)(2,1)S(1)} %get-tuple-element.31, bf16[128]{0:T(256)(128)(2,1)S(1)} %select_convert_fusion), kind=kOutput, calls=%fused_computation.21 | convolution fusion | flops 10616832 | bytes 1081600 | tf_op jit(solution)/shard_map/waik,wbjk->iabjk/dot_general | solution.py:55
  116.7 2.6 %fusion.71 = (f32[8,3,3,8,64]{0,3,1,2,4:T(8,128)}, f32[8,3,3,8,64]{0,3,1,2,4:T(8,128)}) fusion(f32[8,3,3,8,128]{0,3,1,2,4:T(8,128)S(1)} %convolution_bitcast_fusion.6), kind=kLoop, calls=%fused_computation.139 | loop fusion | bytes 589824 | tf_op jit(solution)/shard_map/jit(_roll_static)/slice | solution.py:57
  119.3 1.0 copy-done.6
  120.3 2.9 %convolution_bitcast_fusion.2 = f32[8,3,3,8,128]{0,3,1,2,4:T(8,128)S(1)} fusion(bf16[64,3,8,128,1]{0,2,1,4,3:T(8,128)(2,1)S(1)} %copy.120, bf16[64,3,8,64]{0,2,1,3:T(8,128)(2,1)S(1)} %get-tuple-element.36, bf16[64,3,8,64]{0,2,1,3:T(8,128)(2,1)S(1)} %get-tuple-element.35, bf16[128]{0:T(256)(128)(2,1)S(1)} %select_convert_fusion), kind=kOutput, calls=%fused_computation.17 | convolution fusion | flops 10616832 | bytes 1081600 | tf_op jit(solution)/shard_map/waik,wbjk->iabjk/dot_general | solution.py:55
  123.2 2.2 copy-done.7
  125.4 2.5 %fusion.75 = (f32[8,3,3,8,64]{0,3,1,2,4:T(8,128)}, f32[8,3,3,8,64]{0,3,1,2,4:T(8,128)}) fusion(f32[8,3,3,8,128]{0,3,1,2,4:T(8,128)S(1)} %convolution_bitcast_fusion.2), kind=kLoop, calls=%fused_computation.143 | loop fusion | bytes 589824 | tf_op jit(solution)/shard_map/jit(_roll_static)/slice | solution.py:57
  127.9 3.8 %fusion.72 = (f32[8,3,3,8,64]{0,3,1,2,4:T(8,128)}, f32[8,3,3,8,64]{0,3,1,2,4:T(8,128)}, f32[8,3,3,8,64]{0,3,1,2,4:T(8,128)}, f32[8,3,3,8,64]{0,3,1,2,4:T(8,128)}) fusion(f32[8,3,3,8,128]{0,3,1,2,4:T(8,128)S(1)} %bitcast.138, f32[8,3,3,8,128]{0,3,1,2,4:T(8,128)S(1)} %bitcast.140), kind=kLoop, calls=%fused_computation.140 | loop fusion | bytes 1179648 | tf_op jit(solution)/shard_map/jit(_roll_static)/slice | solution.py:56
  131.7 24.2 %fusion = (f32[8,3,3,8,128]{0,3,1,2,4:T(8,128)}, f32[8,3,3,8,128]{0,3,1,2,4:T(8,128)}, f32[8,3,3,8,128]{0,3,1,2,4:T(8,128)}) fusion(f32[8,3,3,8,128]{0,3,1,2,4:T(8,128)} %convolution_bitcast_fusion.7, f32[8,3,3,8,64]{0,3,1,2,4:T(8,128)} %get-tuple-element.14, f32[8,3,3,8,64]{0,3,1,2,4:T(8,128)} %get-tuple-element.13, f32[8,3,3,8,128]{0,3,1,2,4:T(8,128)} %copy-done.6, ...), kind=kLoop, calls=%fused_computation.3 | loop fusion | flops 1105920 | bytes 4423808 | tf_op jit(solution)/shard_map/jit(_where)/select_n | solution.py:58
  155.9 3.7 %copy.104 = f32[8,3,3,8,128]{4,3,2,1,0:T(8,128)S(1)} copy(f32[8,3,3,8,128]{0,3,1,2,4:T(8,128)} %get-tuple-element.45) | data formatting | bytes 589824 | tf_op jit(solution)/shard_map/jit(_where)/select_n | solution.py:58
  159.6 1.4 fusion.45
  161.1 0.3 reduce-scatter.9.cloned.1.call-start
  161.4 3.7 %copy.112 = f32[8,3,3,8,128]{4,3,2,1,0:T(8,128)S(1)} copy(f32[8,3,3,8,128]{0,3,1,2,4:T(8,128)} %get-tuple-element.46) | data formatting | bytes 589824 | tf_op jit(solution)/shard_map/jit(_where)/select_n | solution.py:58
  165.1 1.5 fusion.41
  166.7 11.9 %all-gather.2 = bf16[4,64,8]{1,2,0:T(8,128)(2,1)S(1)} all-gather(bf16[1,64,8]{1,2,0:T(8,128)(2,1)S(1)} %get-tuple-element.39), channel_id=3, replica_groups=mesh['hours'=2,'pair'=4,'win'=2,'band'=2] {'pair'}, dimensions={0}, use_global_device_ids=true | all-gather | bytes 5120 | tf_op jit(solution)/shard_map/all_gather | solution.py:90
  178.6 0.6 gather_fusion.1
  179.2 0.1 convolution_bitcast_fusion.8
  179.4 0.1 convolution_bitcast_fusion.9
  179.5 3.9 %copy.116 = f32[8,3,3,8,128]{4,3,2,1,0:T(8,128)S(1)} copy(f32[8,3,3,8,128]{0,3,1,2,4:T(8,128)} %get-tuple-element.47) | data formatting | bytes 589824 | tf_op jit(solution)/shard_map/jit(_where)/select_n | solution.py:58
  183.4 1.4 fusion.39
  184.8 0.1 convolution_bitcast_fusion.10
  184.9 0.1 convolution_bitcast_fusion.11
  185.1 8.0 %all-reduce = (f32[8,8]{0,1:T(8,128)S(1)}, f32[8,8]{0,1:T(8,128)S(1)}, f32[8,8]{0,1:T(8,128)S(1)}, f32[8,8]{0,1:T(8,128)S(1)}) all-reduce(f32[8,8]{0,1:T(8,128)S(1)} %convolution_bitcast_fusion.8, f32[8,8]{0,1:T(8,128)S(1)} %convolution_bitcast_fusion.9, ...), channel_id=1, replica_groups=mesh['hours'=2,'pair'=4,'win'=2,'band'=2] {'win'}, use_global_device_ids=true, to_apply=%region_8.9 | all-reduce | flops 256 | bytes 2048 | tf_op jit(solution)/shard_map/psum | solution.py:108
  193.6 0.1 tile.33
  193.7 0.1 tile.37
  193.8 0.1 tile.39
  193.9 1.0 divide_bitcast_fusion.2
  195.0 1.0 divide_bitcast_fusion.3
  196.0 10.7 %reduce-scatter.9.cloned.1.call-done = f32[2,3,24,256]{3,2,1,0:T(8,128)} async-done(((f32[8,3,24,256]{3,2,1,0:T(8,128)}), f32[2,3,24,256]{3,2,1,0:T(8,128)}) %reduce-scatter.9.cloned.1.call-update) | async-done | bytes 147472 | tf_op jit(solution)/shard_map/reduce_scatter | solution.py:105
  206.7 1.0 divide_bitcast_fusion.1
  207.7 23.4 %reduce-scatter.11.cloned.1.call-done = f32[2,3,24,256]{3,2,1,0:T(8,128)} async-done(((f32[8,3,24,256]{3,2,1,0:T(8,128)}), f32[2,3,24,256]{3,2,1,0:T(8,128)}) %reduce-scatter.11.cloned.1.call-update) | async-done | bytes 147472 | tf_op jit(solution)/shard_map/reduce_scatter | solution.py:105
  231.1 1.0 divide_bitcast_fusion
  232.1 0.9 pad_maximum_fusion
  (57 shorter events, 1.1 us)
Async XLA Ops:
  6.5 1.5 copy-start
  6.5 43.5 %all-gather.5.cloned.1.call-start = ((), (), s32[]{:S(2)}) async-start(), calls=%async_computation.8 | async-start | bytes 1966080 | tf_op jit(solution)/shard_map/all_gather | solution.py:89
  9.0 1.8 copy-start.9
  10.1 183.8 %reduce-scatter.7.cloned.1.call-start = ((), (), s32[]{:S(2)}) async-start(), calls=%async_computation.5 | async-start | bytes 737280 | tf_op jit(solution)/shard_map/reduce_scatter | solution.py:105
  65.2 16.1 %copy-start.4 = (f32[8,3,3,8,128]{0,3,1,2,4:T(8,128)}, f32[8,3,3,8,128]{0,3,1,2,4:T(8,128)S(1)}, u32[]{:S(2)}) copy-start(f32[8,3,3,8,128]{0,3,1,2,4:T(8,128)S(1)} %convolution_bitcast_fusion.1) | copy-start | bytes 884740
  73.5 5.3 %copy-start.2 = (f32[8,3,3,8,128]{0,3,1,2,4:T(8,128)}, f32[8,3,3,8,128]{0,3,1,2,4:T(8,128)S(1)}, u32[]{:S(2)}) copy-start(f32[8,3,3,8,128]{0,3,1,2,4:T(8,128)S(1)} %convolution_bitcast_fusion.5) | copy-start | bytes 884740
  87.2 3.6 %copy-start.3 = (f32[8,3,3,8,128]{0,3,1,2,4:T(8,128)}, f32[8,3,3,8,128]{0,3,1,2,4:T(8,128)S(1)}, u32[]{:S(2)}) copy-start(f32[8,3,3,8,128]{0,3,1,2,4:T(8,128)S(1)} %convolution_bitcast_fusion.4) | copy-start | bytes 884740
  107.1 87.9 %reduce-scatter.5.cloned.1.call-start = ((), (), s32[]{:S(2)}) async-start(), calls=%async_computation.4 | async-start | bytes 737280 | tf_op jit(solution)/shard_map/reduce_scatter | solution.py:105
  110.3 3.5 %copy-start.5 = (f32[8,3,3,8,128]{0,3,1,2,4:T(8,128)}, f32[8,3,3,8,128]{0,3,1,2,4:T(8,128)S(1)}, u32[]{:S(2)}) copy-start(f32[8,3,3,8,128]{0,3,1,2,4:T(8,128)S(1)} %convolution_bitcast_fusion) | copy-start | bytes 884740
  116.7 3.6 %copy-start.6 = (f32[8,3,3,8,128]{0,3,1,2,4:T(8,128)}, f32[8,3,3,8,128]{0,3,1,2,4:T(8,128)S(1)}, u32[]{:S(2)}) copy-start(f32[8,3,3,8,128]{0,3,1,2,4:T(8,128)S(1)} %convolution_bitcast_fusion.6) | copy-start | bytes 884740
  120.3 7.5 %slice-start = ((s8[4718592]{0:T(1024)(128)(4,1)}), s8[4194304]{0:T(1024)(128)(4,1)S(1)}, s32[]{:S(2)}) async-start(s8[4718592]{0:T(1024)(128)(4,1)} %bitcast.137), calls=%async_computation.9 | async-start | bytes 8388608
  120.3 7.6 %slice-start.2 = ((s8[4718592]{0:T(1024)(128)(4,1)}), s8[4194304]{0:T(1024)(128)(4,1)S(1)}, s32[]{:S(2)}) async-start(s8[4718592]{0:T(1024)(128)(4,1)} %bitcast.139), calls=%async_computation.11 | async-start | bytes 8388608
  123.2 2.2 copy-start.7
  125.4 2.5 %slice-start.1 = ((s8[4718592]{0:T(1024)(128)(4,1)}), s8[524288]{0:T(1024)(128)(4,1)S(1)}, s32[]{:S(2)}) async-start(s8[4718592]{0:T(1024)(128)(4,1)} %bitcast.137), calls=%async_computation.10 | async-start | bytes 1048576
  125.4 2.5 %slice-start.3 = ((s8[4718592]{0:T(1024)(128)(4,1)}), s8[524288]{0:T(1024)(128)(4,1)S(1)}, s32[]{:S(2)}) async-start(s8[4718592]{0:T(1024)(128)(4,1)} %bitcast.139), calls=%async_computation.12 | async-start | bytes 1048576
  161.1 45.6 %reduce-scatter.9.cloned.1.call-start = ((), (), s32[]{:S(2)}) async-start(), calls=%async_computation.6 | async-start | bytes 737280 | tf_op jit(solution)/shard_map/reduce_scatter | solution.py:105
  161.4 17.9 %copy-start.8 = (s32[64,8]{0,1:T(8,128)S(1)}, s32[64,8]{0,1:T(8,128)}, u32[]{:S(2)}) copy-start(s32[64,8]{0,1:T(8,128)} %param.4) | copy-start | bytes 6148
  166.6 64.5 %reduce-scatter.11.cloned.1.call-start = ((), (), s32[]{:S(2)}) async-start(), calls=%async_computation.7 | async-start | bytes 737280 | tf_op jit(solution)/shard_map/reduce_scatter | solution.py:105
  179.5 53.5 %copy-start.1 = (bf16[64,3,8,512]{3,2,1,0:T(8,128)(2,1)S(1)}, bf16[64,3,8,512]{3,2,1,0:T(8,128)(2,1)}, u32[]{:S(2)}) copy-start(bf16[64,3,8,512]{3,2,1,0:T(8,128)(2,1)} %param.3) | copy-start | bytes 4718596
Sparse Core Ops, SparseCore 0:
  10.3 39.7 all-gather.4
  107.2 20.8 reduce-scatter.6
  161.2 20.9 reduce-scatter.4
  184.6 22.0 reduce-scatter.8
  209.0 22.0 reduce-scatter.10
where the time goes:
time: 240 us
  waiting for transfers between devices  73.2 us (30%)
  local copies, waits for them, and re-layouts  51.8 us (22%)
  other arithmetic  44.4 us (18%)
  matrix products  36.4 us (15%)
  blocking collectives  20 us (8%)
  between operations  13.5 us (6%)
    all_gather x1, waiting for transfers between devices, body(): lax.all_gather(whitened[None], 'pair', axis=0, tiled=True)  38.9 us
    reduce_scatter x4, waiting for transfers between devices, body(): lax.psum_scatter(to_lags(term, lag_rows), ('win', 'band'), scatter_dimens...  34.2 us
    select_n x2, other arithmetic, cross_spectra(): product = jnp.where(lower, real_both, imag_both)  33.7 us
    dot_general x4, matrix products, cross_spectra(): jnp.einsum('waik,wbjk->iabjk', own_block, partner, preferred_element_type...  16.7 us
    select_n x4, local copies, waits for them, and re-layouts, cross_spectra(): product = jnp.where(lower, real_both, imag_both)  15.7 us
    all_gather x1, blocking collectives, body(): lax.all_gather(valid_wire[None], 'pair', axis=0, tiled=True)  11.9 us
    dot_general x4, matrix products, cross_spectra(): jnp.einsum('waik,wbjk->iabjk', own_block, turned, preferred_element_type=...  11.7 us
    slice x4, local copies, waits for them, and re-layouts, cross_spectra(): imag_both = rotated + jnp.roll(rotated, bin_count, axis=-1)  10.3 us
  transfers between devices with their start and end apart: 5, of which 3 were waited for; matrix products, arithmetic and copies ran while one was open for 28% of the time, Pallas kernels for 0%

commit v1 on v0

v1 whole, which is shorter than its diff:
```python
import math

import jax
import jax.numpy as jnp
from jax import lax
from jax.sharding import PartitionSpec as P

FREQ = 128
NLAG = 256
ROUNDS = 4


def dft_table(sample_points, bin_count, first_bin):
    sample_moments = jnp.arange(sample_points, dtype=jnp.int32)
    spectral_bin_index = first_bin + 1 + jnp.arange(bin_count, dtype=jnp.int32)
    phase_turns = jnp.mod(sample_moments[:, None] * spectral_bin_index[None, :], sample_points)
    phases = phase_turns.astype(jnp.float32) * (2.0 * math.pi / sample_points)
    hanning_taper = 0.5 - 0.5 * jnp.cos(
        sample_moments.astype(jnp.float32) * (2.0 * math.pi / sample_points)
    )
    weight = (hanning_taper * math.sqrt(8.0 / (3.0 * sample_points)))[:, None]
    return jnp.concatenate([weight * jnp.cos(phases), -(weight * jnp.sin(phases))], axis=1).astype(
        jnp.bfloat16
    )


def lag_table(sample_points, bin_count, first_bin, lag_count, all_bins):
    spectral_bin_index = first_bin + 1 + jnp.arange(bin_count, dtype=jnp.int32)
    shifts = jnp.arange(lag_count, dtype=jnp.int32) - lag_count // 2
    phase_turns = jnp.mod(spectral_bin_index[:, None] * shifts[None, :], sample_points)
    phases = phase_turns.astype(jnp.float32) * (2.0 * math.pi / sample_points)
    lag_scale = 1.0 / math.sqrt(all_bins)
    return jnp.concatenate([jnp.cos(phases) * lag_scale, -(jnp.sin(phases) * lag_scale)], axis=0)


def whiten(spectra, validity):
    bin_count = spectra.shape[-1] // 2
    real_part = spectra[..., :bin_count]
    imag_part = spectra[..., bin_count:]
    band_power = jnp.mean(real_part * real_part + imag_part * imag_part, axis=1)
    amplitude = jnp.sqrt(jnp.maximum(band_power, 0.25))
    factor = validity[:, :, None] / amplitude
    factor = jnp.concatenate([factor, factor], axis=-1)
    return (spectra * factor[:, None]).astype(jnp.bfloat16)


def body(records, valid_mask, round_keys):
    window_count, comp_count, station_count, sample_points = records.shape
    bands = lax.axis_size("band")
    wins = lax.axis_size("win")
    band_index = lax.axis_index("band")
    win_index = lax.axis_index("win")
    pair_index = lax.axis_index("pair")
    nb = FREQ // bands
    rounds = round_keys.shape[0]

    mask_all = lax.all_gather(valid_mask, ("pair", "win"), axis=0, tiled=False)
    mask_all = mask_all.reshape(lax.axis_size("pair"), wins * window_count, station_count)

    dft_rows = dft_table(sample_points, nb, band_index * nb)
    spectra = jnp.einsum("wcsn,nk->wcsk", records, dft_rows, preferred_element_type=jnp.float32)
    validity = valid_mask.astype(jnp.float32)
    whitened = whiten(spectra, validity)

    gathered = lax.all_gather(whitened, "pair", axis=0, tiled=False)
    partner_list = jnp.bitwise_xor(pair_index, round_keys)
    partners = jnp.take(gathered, partner_list, axis=0, mode="clip")

    own = whitened.reshape(window_count, comp_count, station_count, 2, nb)
    other = partners.reshape(rounds, window_count, comp_count, station_count, 2, nb)
    prod = jnp.einsum(
        "waitf,rwbjuf->iarbjtuf", own, other, preferred_element_type=jnp.float32
    )
    real = prod[..., 0, 0, :] + prod[..., 1, 1, :]
    imag = prod[..., 1, 0, :] - prod[..., 0, 1, :]
    cross = jnp.stack([real, imag], axis=-2)

    summed = lax.psum_scatter(cross, "win", scatter_dimension=0, tiled=True)
    per_band = summed.shape[0] // bands
    summed = summed.reshape((bands, per_band) + summed.shape[1:])
    swapped = lax.all_to_all(summed, "band", split_axis=0, concat_axis=0, tiled=True)
    stacked = jnp.moveaxis(swapped, 0, -3)
    stacked = stacked.reshape(stacked.shape[:-3] + (bands * 2 * nb,))

    own_mask = mask_all[pair_index].astype(jnp.float32)
    first_row = (win_index * bands + band_index) * per_band
    own_mask = lax.dynamic_slice_in_dim(own_mask, first_row, per_band, axis=1)
    partner_mask = jnp.take(mask_all, partner_list, axis=0, mode="clip").astype(jnp.float32)
    counts = jnp.einsum("wi,rwj->irj", own_mask, partner_mask)
    divisor = jnp.maximum(counts, 1.0)[:, None, :, None, :, None]
    stacked = stacked / divisor

    full_lag = lag_table(sample_points, FREQ, 0, NLAG, FREQ)
    full_lag = full_lag.reshape(2, bands, nb, NLAG).transpose(1, 0, 2, 3).reshape(-1, NLAG)
    lagged = jnp.einsum(
        "iarbje,el->riabjl",
        stacked,
        full_lag,
        precision=lax.Precision.HIGHEST,
        preferred_element_type=jnp.float32,
    )
    return lagged.reshape(rounds, per_band, comp_count, comp_count * station_count, NLAG)


def solution(mesh):
    placed = (P(("hours", "win"), None, "pair", None), P(("hours", "win"), "pair"), P())
    return jax.shard_map(
        body,
        mesh=mesh,
        in_specs=placed,
        out_specs=P(None, ("hours", "pair", "win", "band"), None, None, None),
        check_vma=False,
    )
```

time: 240 us -> 174 us (0.72)
  waiting for transfers between devices: 73.2 us -> 38.7 us
  matrix products: 36.4 us -> 18 us
  other arithmetic: 44.4 us -> 27.9 us
  blocking collectives: 20 us -> 35.1 us
  local copies, waits for them, and re-layouts: 51.8 us -> 40.3 us
    select_n x4 -> x0, other arithmetic: 36.1 us -> none  [the longest x2 33.7 us: cross_spectra(): product = jnp.where(lower, real_both, imag_both)]
    reduce_scatter x4 -> x1, waiting for transfers between devices: 34.2 us -> 1.95 us  [body(): summed = lax.psum_scatter(cross, 'win', scatter_dimension=0, tiled=True)]
    add x0 -> x2, other arithmetic: none -> 21 us  [the longest x1 21 us: body(): real = prod[..., 0, 0, :] + prod[..., 1, 1, :]]
    reshape x0 -> x7, local copies, waits for them, and re-layouts: none -> 20.4 us  [the longest x2 16.4 us: body(): partners.reshape(rounds, window_count, comp_count, station_count, 2, nb)]
    slice x9 -> x0, local copies, waits for them, and re-layouts: 19.6 us -> none  [the longest x4 10.3 us: cross_spectra(): imag_both = rotated + jnp.roll(rotated, bin_count, axis=-1)]
    all_gather x1, blocking collectives: 11.9 us -> 30.9 us  [body(): mask_all = lax.all_gather(valid_mask, ('pair', 'win'), axis=0, tiled=False)]
    dot_general x16 -> x3, matrix products: 35.7 us -> 17.3 us  [the longest x1 16 us: body(): jnp.einsum('waitf,rwbjuf->iarbjtuf', own, other, preferred_element_type=j...]
    select_n x4 -> x0, local copies, waits for them, and re-layouts: 15.7 us -> none  [cross_spectra(): product = jnp.where(lower, real_both, imag_both)]
  transfers between devices with their start and end apart: 5 -> 2, of which waited for: 3 -> 2; matrix products, arithmetic and copies ran while one was open for 28% -> 3% of each run, Pallas kernels for 0% -> 0%
where the time goes in v1:
time: 174 us
  local copies, waits for them, and re-layouts  40.3 us (23%)
  waiting for transfers between devices  38.7 us (22%)
  blocking collectives  35.1 us (20%)
  other arithmetic  27.9 us (16%)
  matrix products  18 us (10%)
  between operations  13.6 us (8%)
    all_gather x1, waiting for transfers between devices, body(): gathered = lax.all_gather(whitened, 'pair', axis=0, tiled=False)  36.7 us
    all_gather x1, blocking collectives, body(): mask_all = lax.all_gather(valid_mask, ('pair', 'win'), axis=0, tiled=False)  30.9 us
    add x1, other arithmetic, body(): real = prod[..., 0, 0, :] + prod[..., 1, 1, :]  21 us
    reshape x2, local copies, waits for them, and re-layouts, body(): partners.reshape(rounds, window_count, comp_count, station_count, 2, nb)  16.4 us
    dot_general x1, matrix products, body(): jnp.einsum('waitf,rwbjuf->iarbjtuf', own, other, preferred_element_type=j...  16 us
    sub x1, local copies, waits for them, and re-layouts, body(): imag = prod[..., 1, 0, :] - prod[..., 0, 1, :]  5.61 us
    add x1, local copies, waits for them, and re-layouts, body(): real = prod[..., 0, 0, :] + prod[..., 1, 1, :]  5.6 us
    all_to_all x1, blocking collectives, body(): lax.all_to_all(summed, 'band', split_axis=0, concat_axis=0, tiled=True)  4.21 us
  transfers between devices with their start and end apart: 2, of which 2 were waited for; matrix products, arithmetic and copies ran while one was open for 3% of the time, Pallas kernels for 0%

profile of v1, /device:TPU:0, one launch (start us, length us, event | category | flops | bytes accessed | tf_op | source)
XLA Modules:
  0.0 173.6 jit_solution(16270902631576337646)
XLA Ops:
  6.5 0.0 copy-start
  6.5 0.0 all-gather.5.cloned.1.call-start
  6.6 0.6 multiply_convert_fusion.1
  7.2 0.7 copy-done
  7.9 0.0 copy-start.2
  7.9 0.7 fusion.4
  8.6 0.3 fusion.10
  8.9 0.0 copy-done.2
  8.9 0.1 rsqrt_multiply_fusion
  9.1 0.1 pad_maximum_fusion.2
  9.2 0.8 multiply_convert_fusion
  10.1 0.0 copy-start.3
  10.1 0.0 all-gather.5.cloned.1.call-update
  10.1 0.0 reduce-scatter.2.cloned.1.call-start
  10.1 2.1 %reshape.85 = bf16[64,3,8,2,64]{4,3,0,2,1:T(2,128)(2,1)S(1)} reshape(bf16[64,3,8,128]{3,0,2,1:T(8,128)(2,1)} %multiply_convert_fusion) | data formatting | bytes 786432 | tf_op jit(solution)/shard_map/reshape | solution.py:69
  12.3 0.9 copy.60
  13.2 0.0 copy-done.3
  13.3 36.7 %all-gather.5.cloned.1.call-done = bf16[256,3,8,128]{3,0,2,1:T(8,128)(2,1)} async-done(((bf16[64,3,8,128]{3,0,2,1:T(8,128)(2,1)}), bf16[256,3,8,128]{3,0,2,1:T(8,128)(2,1)}) %all-gather.5.cloned.1.call-update) | async-done | bytes 1572880 | tf_op jit(solution)/shard_map/all_gather | solution.py:65
  50.0 2.4 %copy.48 = bf16[4,64,3,8,128]{4,3,2,1,0:T(8,128)(2,1)S(1)} copy(bf16[4,64,3,8,128]{4,1,0,3,2:T(8,128)(2,1)} %bitcast.60) | data formatting | bytes 3145728 | tf_op jit(solution)/shard_map/all_gather | solution.py:65
  52.4 1.9 %gather_fusion = bf16[4,64,3,8,128]{4,3,2,1,0:T(8,128)(2,1)} fusion(bf16[4,64,3,8,128]{4,3,2,1,0:T(8,128)(2,1)S(1)} %copy.48, s32[1024]{0:T(1024)S(1)} %pad_clamp_fusion), kind=kCustom, calls=%fused_computation | custom fusion | bytes 3145744 | tf_op jit(solution)/shard_map/jit(_take)/gather | solution.py:67
  54.3 6.5 %reshape.84 = bf16[4,64,3,8,2,64]{5,4,3,2,1,0:T(2,128)(2,1)} reshape(bf16[4,64,3,8,128]{4,3,2,1,0:T(8,128)(2,1)} %gather_fusion) | data formatting | bytes 3145728 | tf_op jit(solution)/shard_map/reshape | solution.py:70
  60.8 9.9 %copy.59 = bf16[4,64,3,8,2,64,1,1]{1,3,7,6,4,2,0,5:T(8,128)(2,1)} copy(bf16[4,64,3,8,2,64,1,1]{5,4,3,2,1,0,7,6:T(2,128)(2,1)} %bitcast.58) | data formatting | bytes 3145728 | tf_op jit(solution)/shard_map/reshape | solution.py:70
  70.7 16.0 %convolution_bitcast_fusion = f32[8,3,4,3,8,2,2,64]{0,4,5,1,6,3,2,7:T(8,128)} fusion(bf16[4,64,3,8,2,64,1,1]{1,3,7,6,4,2,0,5:T(8,128)(2,1)} %copy.59, bf16[64,3,8,2,64,1,1,1]{0,2,3,1,7,6,5,4:T(8,128)(2,1)S(1)} %copy.60), kind=kOutput, calls=%fused_computation.2 | convolution fusion | flops 75497472 | bytes 4325376 | tf_op jit(solution)/shard_map/waitf,rwbjuf->iarbjtuf/dot_general | solution.py:71
  86.7 21.0 %fusion.1 = (f32[8,3,4,3,8,1,64]{0,4,1,3,2,6,5:T(8,128)}, f32[8,3,4,3,8,1,64]{0,4,1,3,2,6,5:T(8,128)}) fusion(f32[8,3,4,3,8,2,2,64]{0,4,5,1,6,3,2,7:T(8,128)} %convolution_bitcast_fusion), kind=kLoop, calls=%fused_computation.6 | loop fusion | flops 294912 | bytes 3538944 | tf_op jit(solution)/shard_map/add | solution.py:74
  107.7 5.6 %copy.51 = f32[8,3,4,3,8,1,64]{6,4,5,3,2,1,0:T(8,128)S(1)} copy(f32[8,3,4,3,8,1,64]{0,4,1,3,2,6,5:T(8,128)} %get-tuple-element.5) | data formatting | bytes 1179648 | tf_op jit(solution)/shard_map/add | solution.py:74
  113.3 5.6 %copy.52 = f32[8,3,4,3,8,1,64]{6,4,5,3,2,1,0:T(8,128)S(1)} copy(f32[8,3,4,3,8,1,64]{0,4,1,3,2,6,5:T(8,128)} %get-tuple-element.6) | data formatting | bytes 1179648 | tf_op jit(solution)/shard_map/sub | solution.py:75
  118.9 1.6 pad_maximum_fusion
  120.6 0.0 reduce-scatter.2.cloned.1.call-update
  120.6 30.9 %all-gather.2 = s32[8,64,8]{1,2,0:T(8,128)S(1)} all-gather(s32[1,64,8]{1,2,0:T(8,128)S(1)} %bitcast.63), channel_id=3, replica_groups=mesh['hours'=2,'pair'=4,'win'=2,'band'=2] {'pair','win'}, dimensions={0}, use_global_device_ids=true | all-gather | bytes 18432 | tf_op jit(solution)/shard_map/all_gather | solution.py:57
  151.5 0.1 reshape.87
  151.6 0.5 gather_fusion.1
  152.2 0.1 convolution_maximum_fusion
  152.3 0.6 cosine_multiply_fusion
  153.0 2.0 %reduce-scatter.2.cloned.1.call-done = f32[4,3,4,3,8,2,64]{6,4,5,3,2,1,0:T(8,128)} async-done(((f32[8,3,4,3,8,2,64]{6,4,5,3,2,1,0:T(8,128)}), f32[4,3,4,3,8,2,64]{6,4,5,3,2,1,0:T(8,128)}) %reduce-scatter.2.cloned.1.call-update) | async-done | bytes 589840 | tf_op jit(solution)/shard_map/reduce_scatter | solution.py:78
  154.9 1.8 %reshape.119 = f32[2,1,73728]{2,1,0:T(1,128)S(1)} reshape(f32[2,2,3,4,3,2,8,64]{7,6,5,4,3,2,1,0:T(8,128)} %bitcast.61) | data formatting | bytes 1179648
  156.8 4.2 %all_to_all.5 = f32[2,1,73728]{2,1,0:T(1,128)S(1)} all-to-all(f32[2,1,73728]{2,1,0:T(1,128)S(1)} %reshape.119), channel_id=1, replica_groups=mesh['hours'=2,'pair'=4,'win'=2,'band'=2] {'band'}, dimensions={0} | all-to-all | bytes 1179648 | tf_op jit(solution)/shard_map/all_to_all | solution.py:81
  161.0 0.5 broadcast.80
  161.5 2.5 %reduce = f32[2,73728]{1,0:T(2,128)S(1)} reduce(f32[2,1,73728]{2,1,0:T(1,128)S(1)} %all_to_all.5, f32[]{:T(128)} %broadcast.80), dimensions={1}, to_apply=%all_to_all.3.reduce_sub_computation | reduce | bytes 1179652 | tf_op jit(solution)/shard_map/all_to_all | solution.py:81
  164.0 0.7 reshape.120
  164.7 0.0 copy-start.1
  164.7 1.2 convolution_bitcast_fusion.1
  165.9 0.9 copy.57
  166.7 0.0 copy-done.1
  (12 shorter events, 0.1 us)
Async XLA Ops:
  6.5 1.4 copy-start
  6.5 43.4 %all-gather.5.cloned.1.call-start = ((), (), s32[]{:S(2)}) async-start(), calls=%async_computation.3 | async-start | bytes 1966080 | tf_op jit(solution)/shard_map/all_gather | solution.py:65
  7.9 1.0 copy-start.2
  10.1 3.2 %copy-start.3 = (s32[4]{0:T(128)S(1)}, s32[4]{0:T(128)}, u32[]{:S(2)}) copy-start(s32[4]{0:T(128)} %param.5) | copy-start | bytes 52
  10.1 144.9 %reduce-scatter.2.cloned.1.call-start = ((), (), s32[]{:S(2)}) async-start(), calls=%async_computation.2 | async-start | bytes 3538944 | tf_op jit(solution)/shard_map/reduce_scatter | solution.py:78
  164.7 2.1 %copy-start.1 = (bf16[64,3,8,512]{3,2,1,0:T(8,128)(2,1)S(1)}, bf16[64,3,8,512]{3,2,1,0:T(8,128)(2,1)}, u32[]{:S(2)}) copy-start(bf16[64,3,8,512]{3,2,1,0:T(8,128)(2,1)} %param.3) | copy-start | bytes 4718596
Sparse Core Ops, SparseCore 0:
  10.2 39.7 all-gather.4
  120.7 34.1 reduce-scatter.1

commit v2 on v1

v2 whole, which is shorter than its diff:
```python
import math

import jax
import jax.numpy as jnp
from jax import lax
from jax.sharding import PartitionSpec as P

FREQ = 128
NLAG = 256
ROUNDS = 4


def dft_table(sample_points, bin_count, first_bin):
    sample_moments = jnp.arange(sample_points, dtype=jnp.int32)
    spectral_bin_index = first_bin + 1 + jnp.arange(bin_count, dtype=jnp.int32)
    phase_turns = jnp.mod(sample_moments[:, None] * spectral_bin_index[None, :], sample_points)
    phases = phase_turns.astype(jnp.float32) * (2.0 * math.pi / sample_points)
    hanning_taper = 0.5 - 0.5 * jnp.cos(
        sample_moments.astype(jnp.float32) * (2.0 * math.pi / sample_points)
    )
    weight = (hanning_taper * math.sqrt(8.0 / (3.0 * sample_points)))[:, None]
    return jnp.concatenate([weight * jnp.cos(phases), -(weight * jnp.sin(phases))], axis=1).astype(
        jnp.bfloat16
    )


def lag_table(sample_points, bin_count, first_bin, lag_count, all_bins):
    spectral_bin_index = first_bin + 1 + jnp.arange(bin_count, dtype=jnp.int32)
    shifts = jnp.arange(lag_count, dtype=jnp.int32) - lag_count // 2
    phase_turns = jnp.mod(spectral_bin_index[:, None] * shifts[None, :], sample_points)
    phases = phase_turns.astype(jnp.float32) * (2.0 * math.pi / sample_points)
    lag_scale = 1.0 / math.sqrt(all_bins)
    return jnp.concatenate([jnp.cos(phases) * lag_scale, -(jnp.sin(phases) * lag_scale)], axis=0)


def whiten_t(spectra_t, validity_t):
    bin_count = spectra_t.shape[0] // 2
    real_part = spectra_t[:bin_count]
    imag_part = spectra_t[bin_count:]
    band_power = jnp.mean(real_part * real_part + imag_part * imag_part, axis=1)
    amplitude = jnp.sqrt(jnp.maximum(band_power, 0.25))
    factor = validity_t[None] / amplitude
    split = spectra_t.reshape((2, bin_count) + spectra_t.shape[1:])
    return (split * factor[None, :, None]).astype(jnp.bfloat16)


def body(records, valid_mask, round_keys):
    window_count, comp_count, station_count, sample_points = records.shape
    bands = lax.axis_size("band")
    band_index = lax.axis_index("band")
    pair_index = lax.axis_index("pair")
    nb = FREQ // bands
    rounds = round_keys.shape[0]
    rows = 2 * comp_count * station_count

    dft_rows = dft_table(sample_points, nb, band_index * nb)
    spectra_t = jnp.einsum("wcsn,nk->kcsw", records, dft_rows, preferred_element_type=jnp.float32)
    validity_t = valid_mask.astype(jnp.float32).T
    whitened = whiten_t(spectra_t, validity_t)
    own = whitened.transpose(1, 0, 2, 3, 4).reshape(nb, rows, window_count)

    vslab = jnp.zeros((1, rows, window_count), jnp.bfloat16)
    vslab = vslab.at[0, :station_count].set(validity_t.astype(jnp.bfloat16))
    payload = jnp.concatenate([own, vslab], axis=0)

    gathered = lax.all_gather(payload, "pair", axis=0, tiled=False)
    partner_list = jnp.bitwise_xor(pair_index, round_keys)
    partners = jnp.take(gathered, partner_list, axis=0, mode="clip")
    partner_valid = partners[:, nb, :station_count, :].astype(jnp.float32)
    rhs = partners[:, :nb].transpose(1, 0, 2, 3).reshape(nb, rounds * rows, window_count)

    prod = jnp.einsum("fxw,fyw->fxy", own, rhs, preferred_element_type=jnp.float32)
    prod = prod.reshape(nb, 2, comp_count, station_count, rounds, 2, comp_count, station_count)
    real = prod[:, 0, :, :, :, 0] + prod[:, 1, :, :, :, 1]
    imag = prod[:, 1, :, :, :, 0] - prod[:, 0, :, :, :, 1]
    cross = jnp.stack([real, imag], axis=0)
    cross = cross.transpose(3, 2, 4, 5, 6, 0, 1)
    per_station = comp_count * rounds * comp_count * station_count
    cross = cross.reshape(station_count, per_station, 2 * nb)

    counts = jnp.einsum("iw,rjw->irj", validity_t, partner_valid)
    counts = counts.reshape(station_count, 1, rounds * station_count)
    counts = jnp.pad(counts, ((0, 0), (0, 0), (0, 2 * nb - rounds * station_count)))
    ext = jnp.concatenate([cross, counts], axis=1)

    summed = lax.psum_scatter(ext, "win", scatter_dimension=0, tiled=True)
    per_band = summed.shape[0] // bands
    summed = summed.reshape((bands, per_band) + summed.shape[1:])
    swapped = lax.all_to_all(summed, "band", split_axis=0, concat_axis=0, tiled=True)
    totals = swapped[0, :, per_station, : rounds * station_count]
    totals = totals.reshape(per_band, 1, rounds, 1, station_count, 1)
    spec = swapped[:, :, :per_station, :].transpose(1, 2, 0, 3)
    spec = spec.reshape(per_band, comp_count, rounds, comp_count, station_count, bands * 2 * nb)
    stacked = spec / jnp.maximum(totals, 1.0)

    full_lag = lag_table(sample_points, FREQ, 0, NLAG, FREQ)
    full_lag = full_lag.reshape(2, bands, nb, NLAG).transpose(1, 0, 2, 3).reshape(-1, NLAG)
    lagged = jnp.einsum(
        "iarbje,el->riabjl",
        stacked,
        full_lag,
        precision=lax.Precision.HIGHEST,
        preferred_element_type=jnp.float32,
    )
    return lagged.reshape(rounds, per_band, comp_count, comp_count * station_count, NLAG)


def solution(mesh):
    placed = (P(("hours", "win"), None, "pair", None), P(("hours", "win"), "pair"), P())
    return jax.shard_map(
        body,
        mesh=mesh,
        in_specs=placed,
        out_specs=P(None, ("hours", "pair", "win", "band"), None, None, None),
        check_vma=False,
    )
```

time: 174 us -> 162 us (0.931)
  waiting for transfers between devices: 38.7 us -> 87.2 us
  blocking collectives: 35.1 us -> 4.21 us
  other arithmetic: 27.9 us -> 12.7 us
  matrix products: 18 us -> 7.14 us
  local copies, waits for them, and re-layouts: 40.3 us -> 36.7 us
    all_gather x1 -> x0, blocking collectives: 30.9 us -> none  [body(): mask_all = lax.all_gather(valid_mask, ('pair', 'win'), axis=0, tiled=False)]
    all_gather x1, waiting for transfers between devices: 36.7 us -> 66.9 us  [body(): gathered = lax.all_gather(payload, 'pair', axis=0, tiled=False)]
    reduce_scatter x1, waiting for transfers between devices: 1.95 us -> 20.3 us  [body(): summed = lax.psum_scatter(ext, 'win', scatter_dimension=0, tiled=True)]
    add x1, other arithmetic: 21 us -> 2.88 us  [body(): real = prod[:, 0, :, :, :, 0] + prod[:, 1, :, :, :, 1]]
    dot_general x3, matrix products: 16.8 us -> 6.49 us  [the longest x1 5.67 us: body(): jnp.einsum('fxw,fyw->fxy', own, rhs, preferred_element_type=jnp.float32)]
    reshape x6 -> x5, local copies, waits for them, and re-layouts: 19.5 us -> 11.7 us  [the longest x1 5.47 us: body(): partners[:, :nb].transpose(1, 0, 2, 3)]
    sub x1 -> x0, local copies, waits for them, and re-layouts: 5.61 us -> none  [body(): imag = prod[..., 1, 0, :] - prod[..., 0, 1, :]]
    add x1 -> x0, local copies, waits for them, and re-layouts: 5.6 us -> none  [body(): real = prod[..., 0, 0, :] + prod[..., 1, 1, :]]
  transfers between devices with their start and end apart: 2 -> 2, of which waited for: 2 -> 2; matrix products, arithmetic and copies ran while one was open for 3% -> 0% of each run, Pallas kernels for 0% -> 0%
where the time goes in v2:
time: 162 us
  waiting for transfers between devices  87.2 us (54%)
  local copies, waits for them, and re-layouts  36.7 us (23%)
  between operations  13.6 us (8%)
  other arithmetic  12.7 us (8%)
  matrix products  7.14 us (4%)
  blocking collectives  4.21 us (3%)
    all_gather x1, waiting for transfers between devices, body(): gathered = lax.all_gather(payload, 'pair', axis=0, tiled=False)  66.9 us
    reduce_scatter x1, waiting for transfers between devices, body(): summed = lax.psum_scatter(ext, 'win', scatter_dimension=0, tiled=True)  20.3 us
    all_gather x1, local copies, waits for them, and re-layouts, body(): gathered = lax.all_gather(payload, 'pair', axis=0, tiled=False)  6.44 us
    dot_general x1, matrix products, body(): jnp.einsum('fxw,fyw->fxy', own, rhs, preferred_element_type=jnp.float32)  5.67 us
    dot_general x1, local copies, waits for them, and re-layouts, body(): jnp.einsum('fxw,fyw->fxy', own, rhs, preferred_element_type=jnp.float32)  5.54 us
    reshape x1, local copies, waits for them, and re-layouts, body(): partners[:, :nb].transpose(1, 0, 2, 3)  5.47 us
    gather x1, local copies, waits for them, and re-layouts, body(): partners = jnp.take(gathered, partner_list, axis=0, mode='clip')  4.49 us
    all_to_all x1, blocking collectives, body(): lax.all_to_all(summed, 'band', split_axis=0, concat_axis=0, tiled=True)  4.21 us
  transfers between devices with their start and end apart: 2, of which 2 were waited for; matrix products, arithmetic and copies ran while one was open for 0% of the time, Pallas kernels for 0%

profile of v2, /device:TPU:0, one launch (start us, length us, event | category | flops | bytes accessed | tf_op | source)
XLA Modules:
  0.0 161.7 jit_solution(15183028539613251417)
XLA Ops:
  6.5 0.0 copy-start
  6.5 0.0 all-gather.3.cloned.1.call-start
  6.6 0.6 multiply_convert_fusion.1
  7.2 0.7 copy-done
  7.9 0.7 fusion.3
  8.6 0.3 fusion.12
  8.9 0.0 copy-start.1
  8.9 2.0 %reshape.147 = f32[2,64,3,8,64]{1,0,4,3,2:T(2,128)} reshape(f32[128,3,8,64]{0,3,2,1:T(8,128)S(1)} %fusion.3) | data formatting | bytes 1572864 | tf_op jit(solution)/shard_map/reshape | solution.py:43
  11.0 0.0 copy-done.1
  11.0 0.1 rsqrt_multiply_fusion
  11.1 2.3 %fusion.10 = bf16[64,2,3,8,64]{0,1,4,3,2:T(2,128)(2,1)S(1)} fusion(f32[2,64,3,8,64]{1,0,4,3,2:T(2,128)} %reshape.147, f32[64,8,64]{0,2,1:T(8,128)S(1)} %rsqrt_multiply_fusion), kind=kLoop, calls=%fused_computation.19 | loop fusion | flops 393216 | bytes 1310720 | tf_op jit(solution)/shard_map/transpose | solution.py:60
  13.4 1.0 copy.61
  14.4 0.0 copy-start.2
  14.4 1.1 fusion.9
  15.5 0.0 all-gather.3.cloned.1.call-update
  15.5 0.2 reduce-scatter.2.cloned.1.call-start
  15.7 0.0 copy-done.2
  15.8 66.9 %all-gather.3.cloned.1.call-done = bf16[260,48,64]{2,1,0:T(8,128)(2,1)} async-done(((bf16[65,48,64]{2,1,0:T(8,128)(2,1)}), bf16[260,48,64]{2,1,0:T(8,128)(2,1)}) %all-gather.3.cloned.1.call-update) | async-done | bytes 1597456 | tf_op jit(solution)/shard_map/all_gather | solution.py:66
  82.6 6.4 %copy.63 = bf16[4,65,48,64]{1,3,2,0:T(8,128)(2,1)} copy(bf16[4,65,48,64]{3,2,1,0:T(8,128)(2,1)} %bitcast.76) | data formatting | bytes 3194880 | tf_op jit(solution)/shard_map/all_gather | solution.py:66
  89.1 4.5 %gather_fusion = bf16[4,65,48,64]{1,3,2,0:T(8,128)(2,1)} fusion(bf16[4,65,48,64]{1,3,2,0:T(8,128)(2,1)} %copy.63, s32[1024]{0:T(1024)S(1)} %pad_clamp_fusion), kind=kCustom, calls=%fused_computation | custom fusion | bytes 3194896 | tf_op jit(solution)/shard_map/jit(_take)/gather | solution.py:68
  93.5 1.2 slice.72
  94.8 5.5 %copy.77 = bf16[64,192,64]{2,1,0:T(8,128)(2,1)} copy(bf16[64,192,64]{0,2,1:T(8,128)(2,1)} %bitcast.73) | data formatting | bytes 3145728 | tf_op jit(solution)/shard_map/reshape | solution.py:70
  100.3 5.7 %fusion.29 = f32[64,48,192]{2,1,0:T(8,128)} fusion(bf16[64,48,64]{2,1,0:T(8,128)(2,1)S(1)} %bitcast.75, bf16[64,192,64]{2,1,0:T(8,128)(2,1)} %copy.77), kind=kOutput, calls=%fused_computation.65 | convolution fusion | flops 75497472 | bytes 4325376 | tf_op jit(solution)/shard_map/fxw,fyw->fxy/dot_general | solution.py:72
  105.9 5.5 %copy.66 = f32[64,48,192]{0,2,1:T(8,128)} copy(f32[64,48,192]{2,1,0:T(8,128)} %fusion.29) | data formatting | bytes 4718592 | tf_op jit(solution)/shard_map/fxw,fyw->fxy/dot_general | solution.py:72
  111.5 1.8 %fusion.6 = f32[1,64,3,8,4,3,8]{1,6,5,4,3,2,0:T(8,128)S(1)} fusion(f32[64,2,3,8,4,2,3,8]{0,7,6,5,4,3,2,1:T(8,128)} %bitcast.71), kind=kLoop, calls=%fused_computation.12 | loop fusion | flops 147456 | bytes 1769472 | tf_op jit(solution)/shard_map/sub | solution.py:75
  113.3 2.9 %fusion.8 = f32[1,64,3,8,4,3,8]{1,6,5,4,3,2,0:T(8,128)} fusion(f32[64,2,3,8,4,2,3,8]{0,7,6,5,4,3,2,1:T(8,128)} %bitcast.72), kind=kLoop, calls=%fused_computation.15 | loop fusion | flops 147456 | bytes 1769472 | tf_op jit(solution)/shard_map/add | solution.py:74
  116.2 0.3 copy.88
  116.5 0.1 convolution_bitcast_fusion.1
  116.6 0.1 copy.71
  116.6 1.5 maximum_bitcast_fusion
  118.2 3.3 %copy.69 = f32[8,3,4,3,8,2,64]{6,5,4,3,2,1,0:T(2,128)} copy(f32[8,3,4,3,8,2,64]{6,4,3,2,0,1,5:T(8,128)S(1)} %maximum_bitcast_fusion) | data formatting | bytes 2359296 | tf_op jit(solution)/shard_map/transpose | solution.py:77
  121.5 2.7 %reshape.152 = f32[8,288,128]{2,1,0:T(8,128)S(1)} reshape(f32[8,3,4,3,8,2,64]{6,5,4,3,2,1,0:T(2,128)} %copy.69) | data formatting | bytes 2359296 | tf_op jit(solution)/shard_map/reshape | solution.py:79
  124.2 1.1 select_maximum_fusion
  125.3 0.0 reduce-scatter.2.cloned.1.call-update
  125.4 0.6 cosine_multiply_fusion
  126.0 20.3 %reduce-scatter.2.cloned.1.call-done = f32[4,289,128]{2,1,0:T(8,128)} async-done(((f32[8,289,128]{2,1,0:T(8,128)}), f32[4,289,128]{2,1,0:T(8,128)}) %reduce-scatter.2.cloned.1.call-update) | async-done | bytes 591888 | tf_op jit(solution)/shard_map/reduce_scatter | solution.py:86
  146.3 1.4 copy.72
  147.7 4.2 %all_to_all.5 = f32[2,2,289,128]{3,1,2,0:T(2,128)S(1)} all-to-all(f32[2,2,289,128]{3,1,2,0:T(2,128)S(1)} %copy.72), channel_id=1, replica_groups=mesh['hours'=2,'pair'=4,'win'=2,'band'=2] {'band'}, dimensions={0} | all-to-all | bytes 1183744 | tf_op jit(solution)/shard_map/all_to_all | solution.py:89
  151.9 0.1 copy.90
  152.0 0.4 fusion.13
  152.4 0.5 copy.74
  152.9 0.5 div.41
  153.4 0.7 convolution_bitcast_fusion
  154.0 0.9 copy.75
  (11 shorter events, 0.1 us)
Async XLA Ops:
  6.5 1.4 copy-start
  6.5 76.1 %all-gather.3.cloned.1.call-start = ((), (), s32[]{:S(2)}) async-start(), calls=%async_computation.3 | async-start | bytes 3993600 | tf_op jit(solution)/shard_map/all_gather | solution.py:66
  8.9 2.1 %copy-start.1 = (s32[64,8]{0,1:T(8,128)S(1)}, s32[64,8]{0,1:T(8,128)}, u32[]{:S(2)}) copy-start(s32[64,8]{0,1:T(8,128)} %param.6) | copy-start | bytes 6148
  14.4 1.3 copy-start.2
  15.5 130.8 %reduce-scatter.2.cloned.1.call-start = ((), (), s32[]{:S(2)}) async-start(), calls=%async_computation.2 | async-start | bytes 1818624 | tf_op jit(solution)/shard_map/reduce_scatter | solution.py:86
Sparse Core Ops, SparseCore 0:
  15.6 66.9 all-gather.2
  125.5 20.8 reduce-scatter.1

commit v3 on v1

--- a/solution.py
+++ b/solution.py
@@ -47,48 +47,64 @@
 def body(records, valid_mask, round_keys):
     window_count, comp_count, station_count, sample_points = records.shape
     bands = lax.axis_size("band")
-    wins = lax.axis_size("win")
     band_index = lax.axis_index("band")
-    win_index = lax.axis_index("win")
     pair_index = lax.axis_index("pair")
     nb = FREQ // bands
+    lanes = 2 * nb
     rounds = round_keys.shape[0]
-
-    mask_all = lax.all_gather(valid_mask, ("pair", "win"), axis=0, tiled=False)
-    mask_all = mask_all.reshape(lax.axis_size("pair"), wins * window_count, station_count)
+    rows = window_count * comp_count * station_count
+    half = nb // 2
 
     dft_rows = dft_table(sample_points, nb, band_index * nb)
     spectra = jnp.einsum("wcsn,nk->wcsk", records, dft_rows, preferred_element_type=jnp.float32)
     validity = valid_mask.astype(jnp.float32)
-    whitened = whiten(spectra, validity)
+    whitened = whiten(spectra, validity).reshape(rows, lanes)
 
-    gathered = lax.all_gather(whitened, "pair", axis=0, tiled=False)
+    vrows = -(-window_count * station_count // lanes)
+    vflat = validity.astype(jnp.bfloat16).reshape(-1)
+    vflat = jnp.pad(vflat, (0, vrows * lanes - vflat.shape[0])).reshape(vrows, lanes)
+    payload = jnp.concatenate([whitened, vflat], axis=0)
+
+    gathered = lax.all_gather(payload, "pair", axis=0, tiled=False)
     partner_list = jnp.bitwise_xor(pair_index, round_keys)
     partners = jnp.take(gathered, partner_list, axis=0, mode="clip")
+    partner_valid = partners[:, rows:].reshape(rounds, -1)[:, : window_count * station_count]
+    partner_valid = partner_valid.reshape(rounds, window_count, station_count).astype(jnp.float32)
 
-    own = whitened.reshape(window_count, comp_count, station_count, 2, nb)
-    other = partners.reshape(rounds, window_count, comp_count, station_count, 2, nb)
-    prod = jnp.einsum(
-        "waitf,rwbjuf->iarbjtuf", own, other, preferred_element_type=jnp.float32
+    spec = partners[:, :rows].reshape(
+        rounds, window_count, comp_count, station_count, 2, half, 2
     )
-    real = prod[..., 0, 0, :] + prod[..., 1, 1, :]
-    imag = prod[..., 1, 0, :] - prod[..., 0, 1, :]
-    cross = jnp.stack([real, imag], axis=-2)
+    rhs = spec.transpose(5, 0, 4, 2, 3, 6, 1).reshape(half, rounds * 2 * comp_count * station_count, 2 * window_count)
+    mine = whitened.reshape(window_count, comp_count, station_count, 2, half, 2)
+    mine = mine.transpose(4, 5, 3, 1, 2, 0)
+    parity = jnp.arange(2)
+    pick = (parity[:, None] == parity[None, :]).astype(jnp.bfloat16)
+    lhs = mine[:, :, :, :, :, None, :] * pick[None, :, None, None, None, :, None]
+    lhs = lhs.reshape(half, 2 * 2 * comp_count * station_count, 2 * window_count)
 
-    summed = lax.psum_scatter(cross, "win", scatter_dimension=0, tiled=True)
+    prod = jnp.einsum("gxk,gyk->gxy", lhs, rhs, preferred_element_type=jnp.float32)
+    prod = prod.reshape(half, 2, 2, comp_count, station_count, rounds, 2, comp_count, station_count)
+    real = prod[:, :, 0, :, :, :, 0] + prod[:, :, 1, :, :, :, 1]
+    imag = prod[:, :, 1, :, :, :, 0] - prod[:, :, 0, :, :, :, 1]
+    cross = jnp.stack([real, imag], axis=0)
+    cross = cross.transpose(4, 3, 5, 6, 7, 0, 1, 2)
+    per_station = comp_count * rounds * comp_count * station_count
+    cross = cross.reshape(station_count, per_station, lanes)
+
+    counts = jnp.einsum("wi,rwj->irj", validity, partner_valid)
+    counts = counts.reshape(station_count, 1, rounds * station_count)
+    counts = jnp.pad(counts, ((0, 0), (0, 0), (0, lanes - rounds * station_count)))
+    ext = jnp.concatenate([cross, counts], axis=1)
+
+    summed = lax.psum_scatter(ext, "win", scatter_dimension=0, tiled=True)
     per_band = summed.shape[0] // bands
     summed = summed.reshape((bands, per_band) + summed.shape[1:])
     swapped = lax.all_to_all(summed, "band", split_axis=0, concat_axis=0, tiled=True)
-    stacked = jnp.moveaxis(swapped, 0, -3)
-    stacked = stacked.reshape(stacked.shape[:-3] + (bands * 2 * nb,))
-
-    own_mask = mask_all[pair_index].astype(jnp.float32)
-    first_row = (win_index * bands + band_index) * per_band
-    own_mask = lax.dynamic_slice_in_dim(own_mask, first_row, per_band, axis=1)
-    partner_mask = jnp.take(mask_all, partner_list, axis=0, mode="clip").astype(jnp.float32)
-    counts = jnp.einsum("wi,rwj->irj", own_mask, partner_mask)
-    divisor = jnp.maximum(counts, 1.0)[:, None, :, None, :, None]
-    stacked = stacked / divisor
+    totals = swapped[0, :, per_station, : rounds * station_count]
+    totals = totals.reshape(per_band, 1, rounds, 1, station_count, 1)
+    spec = swapped[:, :, :per_station, :].transpose(1, 2, 0, 3)
+    spec = spec.reshape(per_band, comp_count, rounds, comp_count, station_count, bands * lanes)
+    stacked = spec / jnp.maximum(totals, 1.0)
 
     full_lag = lag_table(sample_points, FREQ, 0, NLAG, FREQ)
     full_lag = full_lag.reshape(2, bands, nb, NLAG).transpose(1, 0, 2, 3).reshape(-1, NLAG)

time: 174 us -> 261 us (1.50)
  local copies, waits for them, and re-layouts: 40.3 us -> 157 us
  blocking collectives: 35.1 us -> 4.21 us
  waiting for transfers between devices: 38.7 us -> 60.3 us
  matrix products: 18 us -> 4.35 us
  other arithmetic: 27.9 us -> 18.7 us
    transpose x0 -> x4, local copies, waits for them, and re-layouts: none -> 68.2 us  [the longest x1 42.5 us: body(): spec.transpose(5, 0, 4, 2, 3, 6, 1)]
    reshape x6, local copies, waits for them, and re-layouts: 19.5 us -> 70.1 us  [the longest x1 41.1 us: body(): partners[:, :rows]]
    all_gather x1 -> x0, blocking collectives: 30.9 us -> none  [body(): mask_all = lax.all_gather(valid_mask, ('pair', 'win'), axis=0, tiled=False)]
    reduce_scatter x1, waiting for transfers between devices: 1.95 us -> 24.5 us  [body(): summed = lax.psum_scatter(ext, 'win', scatter_dimension=0, tiled=True)]
    add x1, other arithmetic: 21 us -> 4.32 us  [body(): real = prod[:, :, 0, :, :, :, 0] + prod[:, :, 1, :, :, :, 1]]
    dot_general x2, matrix products: 16.1 us -> 3.01 us  [the longest x1 2.82 us: body(): jnp.einsum('gxk,gyk->gxy', lhs, rhs, preferred_element_type=jnp.float32)]
    dot_general x0 -> x1, local copies, waits for them, and re-layouts: none -> 7.13 us  [body(): jnp.einsum('gxk,gyk->gxy', lhs, rhs, preferred_element_type=jnp.float32)]
    sub x1 -> x0, local copies, waits for them, and re-layouts: 5.61 us -> none  [body(): imag = prod[..., 1, 0, :] - prod[..., 0, 1, :]]
  transfers between devices with their start and end apart: 2 -> 2, of which waited for: 2 -> 2; matrix products, arithmetic and copies ran while one was open for 3% -> 2% of each run, Pallas kernels for 0% -> 0%
where the time goes in v3:
time: 261 us; the launch traced here: 258 us
  local copies, waits for them, and re-layouts  157 us (60%)
  waiting for transfers between devices  60.3 us (23%)
  other arithmetic  18.7 us (7%)
  between operations  13.7 us (5%)
  matrix products  4.35 us (2%)
  blocking collectives  4.21 us (2%)
    transpose x1, local copies, waits for them, and re-layouts, body(): spec.transpose(5, 0, 4, 2, 3, 6, 1)  42.5 us
    reshape x1, local copies, waits for them, and re-layouts, body(): partners[:, :rows]  41.1 us
    all_gather x1, waiting for transfers between devices, body(): gathered = lax.all_gather(payload, 'pair', axis=0, tiled=False)  35.8 us
    transpose x1, local copies, waits for them, and re-layouts, body(): cross = cross.transpose(4, 3, 5, 6, 7, 0, 1, 2)  25.6 us
    reduce_scatter x1, waiting for transfers between devices, body(): summed = lax.psum_scatter(ext, 'win', scatter_dimension=0, tiled=True)  24.5 us
    reshape x1, local copies, waits for them, and re-layouts, body(): cross = cross.reshape(station_count, per_station, lanes)  21.7 us
    dot_general x1, local copies, waits for them, and re-layouts, body(): jnp.einsum('gxk,gyk->gxy', lhs, rhs, preferred_element_type=jnp.float32)  7.13 us
    reshape x1, local copies, waits for them, and re-layouts, body(): spec.transpose(5, 0, 4, 2, 3, 6, 1)  5.41 us
  transfers between devices with their start and end apart: 2, of which 2 were waited for; matrix products, arithmetic and copies ran while one was open for 2% of the time, Pallas kernels for 0%

profile of v3, /device:TPU:0, one launch (start us, length us, event | category | flops | bytes accessed | tf_op | source)
XLA Modules:
  0.0 258.3 jit_solution(3313028280856023153)
XLA Ops:
  6.5 0.0 copy-start
  6.5 0.0 all-gather.4.cloned.1.call-start
  6.6 0.8 fusion.28
  7.4 0.1 copy.70
  7.5 0.1 reshape.127
  7.6 0.6 multiply_convert_fusion.1
  8.2 0.0 copy-done
  8.2 0.7 fusion.5
  8.9 0.3 fusion.9
  9.2 0.1 rsqrt_multiply_fusion
  9.3 0.1 pad_maximum_fusion.1
  9.5 0.1 multiply_convert_fusion
  9.6 0.3 copy.69
  9.8 0.8 maximum_bitcast_fusion.1
  10.6 0.0 all-gather.4.cloned.1.call-update
  10.6 0.2 reduce-scatter.2.cloned.1.call-start
  10.9 0.4 copy.67
  11.3 0.1 copy.68
  11.5 1.7 mul.163
  13.1 0.0 copy-start.4
  13.2 1.5 mul.164
  14.7 0.1 mul.165
  14.8 0.1 mul.166
  14.9 0.0 copy-done.4
  14.9 35.8 %all-gather.4.cloned.1.call-done = bf16[4,1540,128]{2,1,0:T(8,128)(2,1)} async-done(((bf16[1,1540,128]{2,1,0:T(8,128)(2,1)}), bf16[4,1540,128]{2,1,0:T(8,128)(2,1)}) %all-gather.4.cloned.1.call-update) | async-done | bytes 1576976 | tf_op jit(solution)/shard_map/all_gather | solution.py:68
  50.7 2.3 gather_fusion
  53.0 1.3 slice.44
  54.2 1.7 copy.71
  55.9 41.1 %reshape.128 = bf16[4,64,3,8,2,32,2]{3,2,1,6,5,4,0:T(4,128)(2,1)} reshape(bf16[4,1536,128]{1,2,0:T(8,128)(2,1)S(1)} %copy.71) | data formatting | bytes 3145728 | tf_op jit(solution)/shard_map/reshape | solution.py:74
  97.1 42.5 %copy.72 = bf16[32,4,2,3,8,2,64]{6,5,4,3,2,1,0:T(2,128)(2,1)} copy(bf16[32,4,2,3,8,2,64]{4,3,6,5,0,2,1:T(4,128)(2,1)} %bitcast.61) | data formatting | bytes 3145728 | tf_op jit(solution)/shard_map/transpose | solution.py:77
  139.5 0.0 copy-start.2
  139.5 5.4 %reshape.129 = bf16[32,192,128]{2,1,0:T(8,128)(2,1)S(1)} reshape(bf16[32,4,2,3,8,2,64]{6,5,4,3,2,1,0:T(2,128)(2,1)} %copy.72) | data formatting | bytes 3145728 | tf_op jit(solution)/shard_map/reshape | solution.py:77
  144.9 0.0 copy-done.2
  145.0 2.8 %fusion.10 = f32[32,96,192]{2,1,0:T(8,128)} fusion(bf16[32,192,128]{2,1,0:T(8,128)(2,1)S(1)} %reshape.129, bf16[32,96,128]{2,1,0:T(8,128)(2,1)S(1)} %copy-done.2, bf16[96,128]{1,0:T(8,128)(2,1)S(1)} %mul.166), kind=kOutput, calls=%fused_computation.19 | convolution fusion | flops 151388160 | bytes 4743168 | tf_op jit(solution)/shard_map/gxk,gyk->gxy/dot_general | solution.py:85
  147.8 7.1 %copy.73 = f32[32,96,192]{0,2,1:T(8,128)} copy(f32[32,96,192]{2,1,0:T(8,128)} %fusion.10) | data formatting | bytes 4718592 | tf_op jit(solution)/shard_map/gxk,gyk->gxy/dot_general | solution.py:85
  154.9 4.2 %fusion = f32[1,32,2,3,8,4,3,8]{1,7,6,5,4,3,2,0:T(8,128)} fusion(f32[32,2,2,3,8,4,2,3,8]{0,8,7,6,5,4,3,2,1:T(8,128)} %bitcast.62), kind=kLoop, calls=%fused_computation.3 | loop fusion | flops 147456 | bytes 1769472 | tf_op jit(solution)/shard_map/sub | solution.py:88
  159.1 0.0 copy-start.3
  159.1 4.3 %fusion.2 = f32[1,32,2,3,8,4,3,8]{1,7,6,5,4,3,2,0:T(8,128)} fusion(f32[32,2,2,3,8,4,2,3,8]{0,8,7,6,5,4,3,2,1:T(8,128)} %bitcast.63), kind=kLoop, calls=%fused_computation.6 | loop fusion | flops 147456 | bytes 1769472 | tf_op jit(solution)/shard_map/add | solution.py:87
  163.5 0.1 reshape_reshape.7
  163.6 0.0 copy-done.3
  163.6 0.2 convolution_bitcast_fusion.1
  163.8 0.3 copy.78
  164.0 5.0 %maximum_bitcast_fusion = f32[8,3,4,3,8,2,32,2]{6,4,3,2,0,1,7,5:T(8,128)} fusion(f32[1,32,2,3,8,4,3,8]{1,7,6,5,4,3,2,0:T(8,128)} %fusion, f32[1,32,2,3,8,4,3,8]{1,7,6,5,4,3,2,0:T(8,128)} %fusion.2), kind=kLoop, calls=%fused_computation.1 | loop fusion | flops 294912 | bytes 2359296 | tf_op jit(solution)/shard_map/transpose | solution.py:90
  169.1 25.6 %copy.76 = f32[8,3,4,3,8,2,32,2]{4,3,2,1,7,6,5,0:T(4,128)} copy(f32[8,3,4,3,8,2,32,2]{6,4,3,2,0,1,7,5:T(8,128)} %maximum_bitcast_fusion) | data formatting | bytes 2359296 | tf_op jit(solution)/shard_map/transpose | solution.py:90
  194.7 21.7 %reshape.131 = f32[8,288,128]{1,2,0:T(8,128)S(1)} reshape(f32[8,3,4,3,8,2,32,2]{4,3,2,1,7,6,5,0:T(4,128)} %copy.76) | data formatting | bytes 2359296 | tf_op jit(solution)/shard_map/reshape | solution.py:92
  216.4 1.3 select_maximum_fusion
  217.7 0.0 reduce-scatter.2.cloned.1.call-update
  217.7 0.6 cosine_multiply_fusion
  218.4 24.5 %reduce-scatter.2.cloned.1.call-done = f32[4,289,128]{1,2,0:T(8,128)} async-done(((f32[8,289,128]{1,2,0:T(8,128)}), f32[4,289,128]{1,2,0:T(8,128)}) %reduce-scatter.2.cloned.1.call-update) | async-done | bytes 591888 | tf_op jit(solution)/shard_map/reduce_scatter | solution.py:99
  242.9 1.4 copy.80
  244.3 4.2 %all_to_all.5 = f32[2,2,289,128]{3,1,2,0:T(2,128)S(1)} all-to-all(f32[2,2,289,128]{3,1,2,0:T(2,128)S(1)} %copy.80), channel_id=1, replica_groups=mesh['hours'=2,'pair'=4,'win'=2,'band'=2] {'band'}, dimensions={0} | all-to-all | bytes 1183744 | tf_op jit(solution)/shard_map/all_to_all | solution.py:102
  248.5 0.1 copy.94
  248.6 0.4 fusion.12
  249.0 0.5 copy.82
  249.4 0.5 div.41
  249.9 0.0 copy-start.1
  249.9 0.7 convolution_bitcast_fusion
  250.6 0.9 copy.83
  251.5 0.0 copy-done.1
  (12 shorter events, 0.1 us)
Async XLA Ops:
  6.5 1.7 copy-start
  6.5 44.1 %all-gather.4.cloned.1.call-start = ((), (), s32[]{:S(2)}) async-start(), calls=%async_computation.3 | async-start | bytes 1976320 | tf_op jit(solution)/shard_map/all_gather | solution.py:68
  10.6 232.2 %reduce-scatter.2.cloned.1.call-start = ((), (), s32[]{:S(2)}) async-start(), calls=%async_computation.2 | async-start | bytes 2359296 | tf_op jit(solution)/shard_map/reduce_scatter | solution.py:99
  13.1 1.7 copy-start.4
  139.5 5.4 %copy-start.2 = (bf16[32,96,128]{2,1,0:T(8,128)(2,1)S(1)}, bf16[32,96,128]{2,1,0:T(8,128)(2,1)}, u32[]{:S(2)}) copy-start(bf16[32,96,128]{2,1,0:T(8,128)(2,1)} %mul.164) | copy-start | bytes 2359300
  159.1 4.4 %copy-start.3 = (s32[64,8]{0,1:T(8,128)S(1)}, s32[64,8]{0,1:T(8,128)}, u32[]{:S(2)}) copy-start(s32[64,8]{0,1:T(8,128)} %param.4) | copy-start | bytes 6148
  249.9 1.5 copy-start.1
Sparse Core Ops, SparseCore 0:
  10.8 39.8 all-gather.3
  217.8 24.9 reduce-scatter.1

commit v4 on v3

--- a/solution.py
+++ b/solution.py
@@ -3,6 +3,8 @@
 import jax
 import jax.numpy as jnp
 from jax import lax
+from jax.experimental import pallas as pl
+from jax.experimental.pallas import tpu as pltpu
 from jax.sharding import PartitionSpec as P
 
 FREQ = 128
@@ -44,6 +46,57 @@
     return (spectra * factor[:, None]).astype(jnp.bfloat16)
 
 
+def cross_kernel(own_ref, part_ref, out_ref):
+    window_count = own_ref.shape[0]
+    station_count = own_ref.shape[2]
+    lanes = own_ref.shape[3]
+    nb = lanes // 2
+    lower = lax.broadcasted_iota(jnp.int32, (station_count, station_count, lanes), 2) < nb
+    for b in range(part_ref.shape[2]):
+
+        def step(w, carry):
+            direct, turned = carry
+            a_rows = own_ref[w, 0]
+            b_rows = part_ref[0, w, b]
+            b_turn = pltpu.roll(b_rows, nb, 1)
+            direct = direct + a_rows[:, None, :] * b_rows[None, :, :]
+            turned = turned + a_rows[:, None, :] * b_turn[None, :, :]
+            return direct, turned
+
+        zero = jnp.zeros((station_count, station_count, lanes), jnp.float32)
+        direct, turned = lax.fori_loop(0, window_count, step, (zero, zero), unroll=4)
+        real = direct + pltpu.roll(direct, nb, 2)
+        imag = turned - pltpu.roll(turned, nb, 2)
+        out_ref[:, 0, 0, b] = jnp.where(lower, real, imag)
+
+
+def cross_products(own, partners):
+    rounds, window_count, comp_count, station_count, lanes = partners.shape
+    flops = 4 * rounds * window_count * comp_count * comp_count * station_count * station_count * lanes
+    return pl.pallas_call(
+        cross_kernel,
+        grid=(comp_count, rounds),
+        in_specs=[
+            pl.BlockSpec((window_count, 1, station_count, lanes), lambda a, r: (0, a, 0, 0)),
+            pl.BlockSpec(
+                (1, window_count, comp_count, station_count, lanes), lambda a, r: (r, 0, 0, 0, 0)
+            ),
+        ],
+        out_specs=pl.BlockSpec(
+            (station_count, 1, 1, comp_count, station_count, lanes),
+            lambda a, r: (0, a, r, 0, 0, 0),
+        ),
+        out_shape=jax.ShapeDtypeStruct(
+            (station_count, comp_count, rounds, comp_count, station_count, lanes), jnp.float32
+        ),
+        cost_estimate=pl.CostEstimate(
+            flops=flops,
+            transcendentals=0,
+            bytes_accessed=4 * (own.size * rounds + partners.size + station_count * comp_count * rounds * comp_count * station_count * lanes),
+        ),
+    )(own, partners)
+
+
 def body(records, valid_mask, round_keys):
     window_count, comp_count, station_count, sample_points = records.shape
     bands = lax.axis_size("band")
@@ -53,41 +106,27 @@
     lanes = 2 * nb
     rounds = round_keys.shape[0]
     rows = window_count * comp_count * station_count
-    half = nb // 2
 
     dft_rows = dft_table(sample_points, nb, band_index * nb)
     spectra = jnp.einsum("wcsn,nk->wcsk", records, dft_rows, preferred_element_type=jnp.float32)
     validity = valid_mask.astype(jnp.float32)
-    whitened = whiten(spectra, validity).reshape(rows, lanes)
+    whitened = whiten(spectra, validity)
 
     vrows = -(-window_count * station_count // lanes)
     vflat = validity.astype(jnp.bfloat16).reshape(-1)
     vflat = jnp.pad(vflat, (0, vrows * lanes - vflat.shape[0])).reshape(vrows, lanes)
-    payload = jnp.concatenate([whitened, vflat], axis=0)
+    payload = jnp.concatenate([whitened.reshape(rows, lanes), vflat], axis=0)
 
     gathered = lax.all_gather(payload, "pair", axis=0, tiled=False)
     partner_list = jnp.bitwise_xor(pair_index, round_keys)
     partners = jnp.take(gathered, partner_list, axis=0, mode="clip")
     partner_valid = partners[:, rows:].reshape(rounds, -1)[:, : window_count * station_count]
     partner_valid = partner_valid.reshape(rounds, window_count, station_count).astype(jnp.float32)
+    partner_spec = partners[:, :rows].astype(jnp.float32).reshape(
+        rounds, window_count, comp_count, station_count, lanes
+    )
 
-    spec = partners[:, :rows].reshape(
-        rounds, window_count, comp_count, station_count, 2, half, 2
-    )
-    rhs = spec.transpose(5, 0, 4, 2, 3, 6, 1).reshape(half, rounds * 2 * comp_count * station_count, 2 * window_count)
-    mine = whitened.reshape(window_count, comp_count, station_count, 2, half, 2)
-    mine = mine.transpose(4, 5, 3, 1, 2, 0)
-    parity = jnp.arange(2)
-    pick = (parity[:, None] == parity[None, :]).astype(jnp.bfloat16)
-    lhs = mine[:, :, :, :, :, None, :] * pick[None, :, None, None, None, :, None]
-    lhs = lhs.reshape(half, 2 * 2 * comp_count * station_count, 2 * window_count)
-
-    prod = jnp.einsum("gxk,gyk->gxy", lhs, rhs, preferred_element_type=jnp.float32)
-    prod = prod.reshape(half, 2, 2, comp_count, station_count, rounds, 2, comp_count, station_count)
-    real = prod[:, :, 0, :, :, :, 0] + prod[:, :, 1, :, :, :, 1]
-    imag = prod[:, :, 1, :, :, :, 0] - prod[:, :, 0, :, :, :, 1]
-    cross = jnp.stack([real, imag], axis=0)
-    cross = cross.transpose(4, 3, 5, 6, 7, 0, 1, 2)
+    cross = cross_products(whitened.astype(jnp.float32), partner_spec)
     per_station = comp_count * rounds * comp_count * station_count
     cross = cross.reshape(station_count, per_station, lanes)
 

time: 261 us -> 149 us (0.57); the launches traced: 258 us -> 149 us
  local copies, waits for them, and re-layouts: 157 us -> 7.29 us
  Pallas kernels: 0 us -> 51.6 us
  other arithmetic: 18.7 us -> 10.4 us
  matrix products: 4.35 us -> 1.41 us
    reshape x3 -> x0, local copies, waits for them, and re-layouts: 68.3 us -> none  [the longest x1 41.1 us: body(): partners[:, :rows]]
    transpose x3 -> x0, local copies, waits for them, and re-layouts: 68.2 us -> none  [the longest x1 42.5 us: body(): spec.transpose(5, 0, 4, 2, 3, 6, 1)]
    pallas_call x0 -> x1, Pallas kernels: none -> 51.6 us  [cross_products(): pl.pallas_call(cross_kernel, grid=(comp_count, rounds), in_specs=[pl.Bloc...]
    dot_general x1 -> x0, local copies, waits for them, and re-layouts: 7.13 us -> none  [body(): jnp.einsum('gxk,gyk->gxy', lhs, rhs, preferred_element_type=jnp.float32)]
    transpose x1 -> x0, other arithmetic: 5.03 us -> none  [body(): cross = cross.transpose(4, 3, 5, 6, 7, 0, 1, 2)]
    add x1 -> x0, other arithmetic: 4.32 us -> none  [body(): real = prod[:, :, 0, :, :, :, 0] + prod[:, :, 1, :, :, :, 1]]
    sub x1 -> x0, other arithmetic: 4.22 us -> none  [body(): imag = prod[:, :, 1, :, :, :, 0] - prod[:, :, 0, :, :, :, 1]]
    all_gather x1, waiting for transfers between devices: 35.8 us -> 39.9 us  [body(): gathered = lax.all_gather(payload, 'pair', axis=0, tiled=False)]
  transfers between devices with their start and end apart: 2 -> 2, of which waited for: 2 -> 2; matrix products, arithmetic and copies ran while one was open for 2% -> 0% of each run, Pallas kernels for 0% -> 0%
where the time goes in v4:
time: 149 us
  waiting for transfers between devices  60.5 us (41%)
  Pallas kernels  51.6 us (35%)
  between operations  13.6 us (9%)
  other arithmetic  10.4 us (7%)
  local copies, waits for them, and re-layouts  7.29 us (5%)
  blocking collectives  4.21 us (3%)
    pallas_call x1, Pallas kernels, cross_products(): pl.pallas_call(cross_kernel, grid=(comp_count, rounds), in_specs=[pl.Bloc...  51.6 us
    all_gather x1, waiting for transfers between devices, body(): gathered = lax.all_gather(payload, 'pair', axis=0, tiled=False)  39.9 us
    reduce_scatter x1, waiting for transfers between devices, body(): summed = lax.psum_scatter(ext, 'win', scatter_dimension=0, tiled=True)  20.5 us
    all_to_all x1, blocking collectives, body(): lax.all_to_all(summed, 'band', split_axis=0, concat_axis=0, tiled=True)  4.21 us
    reshape x1, other arithmetic, body(): partners[:, :rows].astype(jnp.float32)  3.27 us
  transfers between devices with their start and end apart: 2, of which 2 were waited for; matrix products, arithmetic and copies ran while one was open for 0% of the time, Pallas kernels for 0%

profile of v4, /device:TPU:0, one launch (start us, length us, event | category | flops | bytes accessed | tf_op | source)
XLA Modules:
  0.0 149.1 jit_solution(9471213746321226450)
XLA Ops:
  6.5 0.0 copy-start
  6.5 0.0 all-gather.4.cloned.1.call-start
  6.6 0.8 fusion.18
  7.4 0.1 copy.44
  7.5 0.1 reshape.69
  7.6 0.1 copy.43
  7.7 0.6 multiply_convert_fusion.1
  8.3 0.0 copy-done
  8.3 0.6 convolution_bitcast_fusion
  8.9 0.3 fusion.1
  9.2 0.1 rsqrt_multiply_fusion
  9.3 0.1 pad_maximum_fusion.1
  9.4 0.0 copy-start.2
  9.5 1.0 fusion.17
  10.5 0.8 maximum_bitcast_fusion
  11.2 0.0 all-gather.4.cloned.1.call-update
  11.3 0.0 reduce-scatter.2.cloned.1.call-start
  11.3 0.0 copy-done.2
  11.4 39.9 %all-gather.4.cloned.1.call-done = bf16[4,1540,128]{2,1,0:T(8,128)(2,1)} async-done(((bf16[1,1540,128]{2,1,0:T(8,128)(2,1)}), bf16[4,1540,128]{2,1,0:T(8,128)(2,1)}) %all-gather.4.cloned.1.call-update) | async-done | bytes 1576976 | tf_op jit(solution)/shard_map/all_gather | solution.py:120
  51.3 2.3 %gather_fusion = bf16[4,1540,128]{2,1,0:T(8,128)(2,1)S(1)} fusion(bf16[4,1540,128]{2,1,0:T(8,128)(2,1)} %all-gather.4.cloned.1.call-done, s32[1024]{0:T(1024)S(1)} %pad_clamp_fusion), kind=kCustom, calls=%fused_computation | custom fusion | bytes 3153936 | tf_op jit(solution)/shard_map/jit(_take)/gather | solution.py:122
  53.6 0.0 copy-start.1
  53.6 1.3 slice.28
  54.8 0.1 reshape_reshape.3
  55.0 0.0 copy-done.1
  55.0 0.2 convolution_bitcast_fusion.2
  55.2 0.1 copy.46
  55.2 3.3 %convert.9.part_ref = f32[4,64,3,8,128]{4,3,2,1,0:T(8,128)} convert(bf16[4,64,3,8,128]{4,3,2,1,0:T(8,128)(2,1)} %bitcast.39) | non-fusion elementwise | flops 786432 | bytes 4718592 | tf_op jit(solution)/shard_map/reshape | solution.py:125
  58.5 51.6 %shard_map.37 = f32[8,3,4,3,8,128]{5,4,3,2,1,0:T(8,128)} custom-call(f32[64,3,8,128]{3,2,1,0:T(8,128)} %get-tuple-element.5.own_ref, f32[4,64,3,8,128]{4,3,2,1,0:T(8,128)} %convert.9.part_ref), custom_call_target="tpu_custom_call" | custom-call | flops 75497472 | bytes 7471104 | tf_op jit(solution)/shard_map/pallas_call | solution.py:76
  110.1 2.4 %select_maximum_fusion = f32[8,289,128]{2,1,0:T(8,128)} fusion(f32[8,1,32]{2,1,0:T(1,128)S(1)} %copy.46, f32[8,288,128]{2,1,0:T(8,128)} %bitcast.40), kind=kLoop, calls=%fused_computation.3 | loop fusion | flops 887808 | bytes 2364416 | tf_op jit(solution)/shard_map/concatenate | solution.py:136
  112.5 0.0 reduce-scatter.2.cloned.1.call-update
  112.5 0.6 cosine_multiply_fusion
  113.2 20.5 %reduce-scatter.2.cloned.1.call-done = f32[4,289,128]{2,1,0:T(8,128)} async-done(((f32[8,289,128]{2,1,0:T(8,128)}), f32[4,289,128]{2,1,0:T(8,128)}) %reduce-scatter.2.cloned.1.call-update) | async-done | bytes 591888 | tf_op jit(solution)/shard_map/reduce_scatter | solution.py:138
  133.7 1.4 copy.47
  135.1 4.2 %all_to_all.5 = f32[2,2,289,128]{3,1,2,0:T(2,128)S(1)} all-to-all(f32[2,2,289,128]{3,1,2,0:T(2,128)S(1)} %copy.47), channel_id=1, replica_groups=mesh['hours'=2,'pair'=4,'win'=2,'band'=2] {'band'}, dimensions={0} | all-to-all | bytes 1183744 | tf_op jit(solution)/shard_map/all_to_all | solution.py:141
  139.3 0.1 copy.59
  139.4 0.4 fusion.2
  139.8 0.5 copy.49
  140.2 0.5 div.41
  140.7 0.7 convolution_bitcast_fusion.1
  141.4 0.9 copy.50
  (11 shorter events, 0.1 us)
Async XLA Ops:
  6.5 1.8 %copy-start = (bf16[64,3,8,512]{3,2,1,0:T(8,128)(2,1)S(1)}, bf16[64,3,8,512]{3,2,1,0:T(8,128)(2,1)}, u32[]{:S(2)}) copy-start(bf16[64,3,8,512]{3,2,1,0:T(8,128)(2,1)} %param.3) | copy-start | bytes 4718596
  6.5 44.8 %all-gather.4.cloned.1.call-start = ((), (), s32[]{:S(2)}) async-start(), calls=%async_computation.3 | async-start | bytes 1976320 | tf_op jit(solution)/shard_map/all_gather | solution.py:120
  9.4 1.9 %copy-start.2 = (s32[4]{0:T(128)S(1)}, s32[4]{0:T(128)}, u32[]{:S(2)}) copy-start(s32[4]{0:T(128)} %param.5) | copy-start | bytes 52
  11.3 122.4 %reduce-scatter.2.cloned.1.call-start = ((), (), s32[]{:S(2)}) async-start(), calls=%async_computation.2 | async-start | bytes 1818624 | tf_op jit(solution)/shard_map/reduce_scatter | solution.py:138
  53.6 1.4 copy-start.1
Sparse Core Ops, SparseCore 0:
  11.4 39.8 all-gather.3
  112.6 21.0 reduce-scatter.1

commit v5 on v4

--- a/solution.py
+++ b/solution.py
@@ -49,7 +49,7 @@
 def cross_kernel(own_ref, part_ref, out_ref):
     window_count = own_ref.shape[0]
     station_count = own_ref.shape[2]
-    lanes = own_ref.shape[3]
+    lanes = own_ref.shape[4]
     nb = lanes // 2
     lower = lax.broadcasted_iota(jnp.int32, (station_count, station_count, lanes), 2) < nb
     for b in range(part_ref.shape[2]):
@@ -59,8 +59,8 @@
             a_rows = own_ref[w, 0]
             b_rows = part_ref[0, w, b]
             b_turn = pltpu.roll(b_rows, nb, 1)
-            direct = direct + a_rows[:, None, :] * b_rows[None, :, :]
-            turned = turned + a_rows[:, None, :] * b_turn[None, :, :]
+            direct = direct + a_rows * b_rows[None, :, :]
+            turned = turned + a_rows * b_turn[None, :, :]
             return direct, turned
 
         zero = jnp.zeros((station_count, station_count, lanes), jnp.float32)
@@ -72,12 +72,15 @@
 
 def cross_products(own, partners):
     rounds, window_count, comp_count, station_count, lanes = partners.shape
+    own = jnp.broadcast_to(own[:, :, :, None, :], (window_count, comp_count, station_count, station_count, lanes))
     flops = 4 * rounds * window_count * comp_count * comp_count * station_count * station_count * lanes
     return pl.pallas_call(
         cross_kernel,
         grid=(comp_count, rounds),
         in_specs=[
-            pl.BlockSpec((window_count, 1, station_count, lanes), lambda a, r: (0, a, 0, 0)),
+            pl.BlockSpec(
+                (window_count, 1, station_count, station_count, lanes), lambda a, r: (0, a, 0, 0, 0)
+            ),
             pl.BlockSpec(
                 (1, window_count, comp_count, station_count, lanes), lambda a, r: (r, 0, 0, 0, 0)
             ),
@@ -92,7 +95,7 @@
         cost_estimate=pl.CostEstimate(
             flops=flops,
             transcendentals=0,
-            bytes_accessed=4 * (own.size * rounds + partners.size + station_count * comp_count * rounds * comp_count * station_count * lanes),
+            bytes_accessed=4 * (own.size + partners.size + station_count * comp_count * rounds * comp_count * station_count * lanes),
         ),
     )(own, partners)
 
@@ -135,13 +138,31 @@
     counts = jnp.pad(counts, ((0, 0), (0, 0), (0, lanes - rounds * station_count)))
     ext = jnp.concatenate([cross, counts], axis=1)
 
-    summed = lax.psum_scatter(ext, "win", scatter_dimension=0, tiled=True)
-    per_band = summed.shape[0] // bands
-    summed = summed.reshape((bands, per_band) + summed.shape[1:])
-    swapped = lax.all_to_all(summed, "band", split_axis=0, concat_axis=0, tiled=True)
-    totals = swapped[0, :, per_station, : rounds * station_count]
+    wins = lax.axis_size("win")
+    if wins == 2 and bands == 2:
+        per_band = station_count // (wins * bands)
+        me = lax.axis_index("win") * bands + band_index
+        pieces = []
+        for flip in range(wins * bands):
+            chunk = lax.dynamic_slice_in_dim(ext, (me ^ flip) * per_band, per_band, 0)
+            if flip:
+                perm = [(k, k ^ flip) for k in range(wins * bands)]
+                chunk = lax.ppermute(chunk, ("win", "band"), perm)
+            pieces.append(chunk)
+        same = pieces[0] + pieces[2]
+        other = pieces[1] + pieces[3]
+        first = jnp.where(band_index == 0, same, other)
+        second = jnp.where(band_index == 0, other, same)
+        swapped = jnp.stack([first, second], axis=0)
+        totals = same[:, per_station, : rounds * station_count]
+    else:
+        summed = lax.psum_scatter(ext, "win", scatter_dimension=0, tiled=True)
+        per_band = summed.shape[0] // bands
+        summed = summed.reshape((bands, per_band) + summed.shape[1:])
+        swapped = lax.all_to_all(summed, "band", split_axis=0, concat_axis=0, tiled=True)
+        totals = swapped[0, :, per_station, : rounds * station_count]
     totals = totals.reshape(per_band, 1, rounds, 1, station_count, 1)
-    spec = swapped[:, :, :per_station, :].transpose(1, 2, 0, 3)
+    spec = swapped[:bands, :, :per_station, :].transpose(1, 2, 0, 3)
     spec = spec.reshape(per_band, comp_count, rounds, comp_count, station_count, bands * lanes)
     stacked = spec / jnp.maximum(totals, 1.0)
 

time: 149 us -> 143 us (0.960)
  waiting for transfers between devices: 60.5 us -> 49.2 us
  local copies, waits for them, and re-layouts: 7.29 us -> 12.5 us
  blocking collectives: 4.21 us -> 0 us
  starting transfers between devices: 0.04 us -> 2.14 us
  other arithmetic: 10.4 us -> 12.3 us
    reduce_scatter x1 -> x0, waiting for transfers between devices: 20.5 us -> none  [body(): summed = lax.psum_scatter(ext, 'win', scatter_dimension=0, tiled=True)]
    ppermute x0 -> x3, waiting for transfers between devices: none -> 10.4 us  [body(): chunk = lax.ppermute(chunk, ('win', 'band'), perm)]
    all_to_all x1 -> x0, blocking collectives: 4.21 us -> none  [body(): lax.all_to_all(summed, 'band', split_axis=0, concat_axis=0, tiled=True)]
    broadcast_in_dim x0 -> x1, local copies, waits for them, and re-layouts: none -> 3.54 us  [cross_products(): jnp.broadcast_to(own[:, :, :, None, :], (window_count, comp_count, statio...]
    another operation x1 -> x3, other arithmetic: 0.61 us -> 3.49 us  [the longest x2 2.88 us: body(): swapped = jnp.stack([first, second], axis=0)]
    ppermute x0 -> x3, starting transfers between devices: none -> 2.14 us  [body(): chunk = lax.ppermute(chunk, ('win', 'band'), perm)]
  transfers between devices with their start and end apart: 2 -> 4, of which waited for: 2 -> 3; matrix products, arithmetic and copies ran while one was open for 0% -> 2% of each run, Pallas kernels for 0% -> 0%
where the time goes in v5:
time: 143 us
  Pallas kernels  51.5 us (36%)
  waiting for transfers between devices  49.2 us (34%)
  between operations  13.6 us (10%)
  local copies, waits for them, and re-layouts  12.5 us (9%)
  other arithmetic  12.3 us (9%)
  starting transfers between devices  2.14 us (1%)
  matrix products  1.53 us (1%)
    pallas_call x1, Pallas kernels, cross_products(): pl.pallas_call(cross_kernel, grid=(comp_count, rounds), in_specs=[pl.Bloc...  51.5 us
    all_gather x1, waiting for transfers between devices, body(): gathered = lax.all_gather(payload, 'pair', axis=0, tiled=False)  38.9 us
    ppermute x3, waiting for transfers between devices, body(): chunk = lax.ppermute(chunk, ('win', 'band'), perm)  10.4 us
    broadcast_in_dim x1, local copies, waits for them, and re-layouts, cross_products(): jnp.broadcast_to(own[:, :, :, None, :], (window_count, comp_count, statio...  3.54 us
    reshape x1, other arithmetic, body(): partners[:, :rows].astype(jnp.float32)  3.41 us
    another operation x2, other arithmetic, body(): swapped = jnp.stack([first, second], axis=0)  2.88 us
  transfers between devices with their start and end apart: 4, of which 3 were waited for; matrix products, arithmetic and copies ran while one was open for 2% of the time, Pallas kernels for 0%

profile of v5, /device:TPU:0, one launch (start us, length us, event | category | flops | bytes accessed | tf_op | source)
XLA Modules:
  0.0 142.8 jit_solution(8265359163420904436)
XLA Ops:
  6.5 0.0 copy-start
  6.5 0.0 all-gather.4.cloned.1.call-start
  6.6 0.8 fusion.24
  7.4 0.1 copy.42
  7.5 0.1 reshape.67
  7.6 0.6 multiply_convert_fusion.1
  8.2 0.0 copy-done
  8.2 0.7 fusion.2
  8.9 0.3 fusion.6
  9.2 0.1 rsqrt_multiply_fusion
  9.3 0.1 pad_maximum_fusion.2
  9.5 0.1 multiply_convert_fusion
  9.6 0.0 copy-start.5
  9.6 0.3 copy.41
  9.9 0.8 maximum_bitcast_fusion
  10.6 0.0 all-gather.4.cloned.1.call-update
  10.7 1.1 copy.40
  11.8 0.0 copy-done.5
  11.8 38.9 %all-gather.4.cloned.1.call-done = bf16[4,1540,128]{2,1,0:T(8,128)(2,1)} async-done(((bf16[1,1540,128]{2,1,0:T(8,128)(2,1)}), bf16[4,1540,128]{2,1,0:T(8,128)(2,1)}) %all-gather.4.cloned.1.call-update) | async-done | bytes 1576976 | tf_op jit(solution)/shard_map/all_gather | solution.py:123
  50.7 2.3 %gather_fusion = bf16[4,1540,128]{2,1,0:T(8,128)(2,1)S(1)} fusion(bf16[4,1540,128]{2,1,0:T(8,128)(2,1)} %all-gather.4.cloned.1.call-done, s32[1024]{0:T(1024)S(1)} %pad_clamp_fusion), kind=kCustom, calls=%fused_computation | custom fusion | bytes 3153936 | tf_op jit(solution)/shard_map/jit(_take)/gather | solution.py:125
  53.0 0.0 copy-start.4
  53.0 1.3 slice.28
  54.2 0.1 reshape_reshape.3
  54.4 0.0 copy-done.4
  54.4 0.2 convolution_bitcast_fusion.1
  54.6 0.1 copy.44
  54.6 0.0 copy-start.1
  54.6 3.4 %convert.9.part_ref = f32[4,64,3,8,128]{4,3,2,1,0:T(8,128)} convert(bf16[4,64,3,8,128]{4,3,2,1,0:T(8,128)(2,1)} %bitcast.39) | non-fusion elementwise | flops 786432 | bytes 4718592 | tf_op jit(solution)/shard_map/reshape | solution.py:128
  58.0 0.0 copy-done.1
  58.0 3.5 %broadcast_in_dim.5.own_ref = f32[64,3,8,8,128]{4,3,2,1,0:T(8,128)} broadcast(f32[64,3,8,128]{3,2,1,0:T(8,128)S(1)} %copy-done.1), dimensions={0,1,2,4} | broadcast | bytes 7077888 | tf_op jit(solution)/shard_map/broadcast_in_dim | solution.py:75
  61.6 51.5 %shard_map.37 = f32[8,3,4,3,8,128]{5,4,3,2,1,0:T(8,128)} custom-call(f32[64,3,8,8,128]{4,3,2,1,0:T(8,128)} %broadcast_in_dim.5.own_ref, f32[4,64,3,8,128]{4,3,2,1,0:T(8,128)} %convert.9.part_ref), custom_call_target="tpu_custom_call" | custom-call | flops 75497472 | bytes 10616832 | tf_op jit(solution)/shard_map/pallas_call | solution.py:77
  113.1 1.4 select_maximum_fusion
  114.5 0.9 constant_dynamic-slice_fusion.2
  115.4 1.5 %collective-permute-start = (f32[2,289,128]{2,1,0:T(8,128)}, f32[2,289,128]{2,1,0:T(8,128)S(1)}, u32[]{:S(2)}, u32[]{:S(2)}) collective-permute-start(f32[2,289,128]{2,1,0:T(8,128)} %get-tuple-element.7), channel_id=1, source_target_pairs={{0,2},{1,3},{2,0},{3,1},{4,6},{5,7},{6,4},{7,5},{8,10},{9,11},{10,... | collective-permute-start | bytes 887816 | tf_op jit(solution)/shard_map/ppermute | solution.py:150
  116.9 0.0 collective-permute-start.2
  116.9 0.7 collective-permute-start.1
  117.5 0.6 cosine_multiply_fusion
  118.2 0.7 copy.37
  118.9 6.8 %collective-permute-done = f32[2,289,128]{2,1,0:T(8,128)S(1)} collective-permute-done((f32[2,289,128]{2,1,0:T(8,128)}, f32[2,289,128]{2,1,0:T(8,128)S(1)}, u32[]{:S(2)}, u32[]{:S(2)}) %collective-permute-start) | collective-permute-done | bytes 295968 | tf_op jit(solution)/shard_map/ppermute | solution.py:150
  125.7 0.0 copy-start.2
  125.7 3.6 %collective-permute-done.2 = f32[2,289,128]{2,1,0:T(8,128)S(1)} collective-permute-done((f32[2,289,128]{2,1,0:T(8,128)}, f32[2,289,128]{2,1,0:T(8,128)S(1)}, u32[]{:S(2)}, u32[]{:S(2)}) %collective-permute-start.2) | collective-permute-done | bytes 295968 | tf_op jit(solution)/shard_map/ppermute | solution.py:150
  129.2 0.0 copy-done.2
  129.2 0.0 collective-permute-done.1
  129.2 1.8 %select_bitcast_fusion.1 = (f32[1,2,289,128]{3,2,1,0:T(8,128)}, f32[2,289,128]{2,1,0:T(8,128)S(1)}) fusion(pred[]{:T(512)S(6)} %eq.8, f32[2,289,128]{2,1,0:T(8,128)} %collective-permute-done.1, f32[2,289,128]{2,1,0:T(8,128)S(1)} %collective-permute-done.2, f32[2,289,128]{2,1,0:T(8,128)} %copy-done.2, f32[8,289,128]{2,1,0:T(8,128)S(1)} %select_maximum_fusion, ...), kind=kLoop, calls=%fused_computation.18 | loop fusion | flops 221952 | bytes 1775621 | tf_op jit(solution)/shard_map/stack | solution.py:156
  131.1 0.1 max.24
  131.2 0.1 div.37
  131.3 1.0 select_bitcast_fusion
  132.3 0.0 copy-start.3
  132.4 1.2 fusion.8
  133.5 0.5 copy.45
  134.0 0.5 div.41
  134.5 0.0 copy-done.3
  134.5 0.7 convolution_bitcast_fusion
  135.1 0.9 copy.46
  (10 shorter events, 0.1 us)
Async XLA Ops:
  6.5 1.7 %copy-start = (bf16[64,3,8,512]{3,2,1,0:T(8,128)(2,1)S(1)}, bf16[64,3,8,512]{3,2,1,0:T(8,128)(2,1)}, u32[]{:S(2)}) copy-start(bf16[64,3,8,512]{3,2,1,0:T(8,128)(2,1)} %param.3) | copy-start | bytes 4718596
  6.5 44.2 %all-gather.4.cloned.1.call-start = ((), (), s32[]{:S(2)}) async-start(), calls=%async_computation | async-start | bytes 1976320 | tf_op jit(solution)/shard_map/all_gather | solution.py:123
  9.6 2.2 %copy-start.5 = (s32[4]{0:T(128)S(1)}, s32[4]{0:T(128)}, u32[]{:S(2)}) copy-start(s32[4]{0:T(128)} %param.5) | copy-start | bytes 52
  53.0 1.4 copy-start.4
  54.6 3.4 %copy-start.1 = (f32[64,3,8,128]{3,2,1,0:T(8,128)S(1)}, f32[64,3,8,128]{3,2,1,0:T(8,128)}, u32[]{:S(2)}) copy-start(f32[64,3,8,128]{3,2,1,0:T(8,128)} %copy.40) | copy-start | bytes 2359300
  115.4 10.3 %collective-permute-start = (f32[2,289,128]{2,1,0:T(8,128)}, f32[2,289,128]{2,1,0:T(8,128)S(1)}, u32[]{:S(2)}, u32[]{:S(2)}) collective-permute-start(f32[2,289,128]{2,1,0:T(8,128)} %get-tuple-element.7), channel_id=1, source_target_pairs={{0,2},{1,3},{2,0},{3,1},{4,6},{5,7},{6,4},{7,5},{8,10},{9,11},{10,... | collective-permute-start | bytes 887816 | tf_op jit(solution)/shard_map/ppermute | solution.py:150
  116.9 12.4 %collective-permute-start.2 = (f32[2,289,128]{2,1,0:T(8,128)}, f32[2,289,128]{2,1,0:T(8,128)S(1)}, u32[]{:S(2)}, u32[]{:S(2)}) collective-permute-start(f32[2,289,128]{2,1,0:T(8,128)} %get-tuple-element.8), channel_id=1, source_target_pairs={{0,3},{1,2},{2,1},{3,0},{4,7},{5,6},{6,5},{7,4},{8,11},{9,10},{10,... | collective-permute-start | bytes 887816 | tf_op jit(solution)/shard_map/ppermute | solution.py:150
  116.9 12.4 %collective-permute-start.1 = (f32[2,289,128]{2,1,0:T(8,128)}, f32[2,289,128]{2,1,0:T(8,128)}, u32[]{:S(2)}, u32[]{:S(2)}) collective-permute-start(f32[2,289,128]{2,1,0:T(8,128)} %get-tuple-element.9), channel_id=1, source_target_pairs={{0,1},{1,0},{2,3},{3,2},{4,5},{5,4},{6,7},{7,6},{8,9},{9,8},{10,11... | collective-permute-start | bytes 887816 | tf_op jit(solution)/shard_map/ppermute | solution.py:150
  125.7 3.6 %copy-start.2 = (f32[2,289,128]{2,1,0:T(8,128)}, f32[2,289,128]{2,1,0:T(8,128)S(1)}, u32[]{:S(2)}) copy-start(f32[2,289,128]{2,1,0:T(8,128)S(1)} %collective-permute-done) | copy-start | bytes 887812
  132.3 2.1 %copy-start.3 = (f32[2,2,64,256]{3,2,1,0:T(8,128)S(1)}, f32[2,2,64,256]{3,2,1,0:T(8,128)}, u32[]{:S(2)}) copy-start(f32[2,2,64,256]{3,2,1,0:T(8,128)} %copy.37) | copy-start | bytes 786436
Sparse Core Ops, SparseCore 0:
  10.8 39.8 all-gather.3

commit v6 on v5

--- a/solution.py
+++ b/solution.py
@@ -10,6 +10,7 @@
 FREQ = 128
 NLAG = 256
 ROUNDS = 4
+WSTEP = 4
 
 
 def dft_table(sample_points, bin_count, first_bin):
@@ -54,17 +55,19 @@
     lower = lax.broadcasted_iota(jnp.int32, (station_count, station_count, lanes), 2) < nb
     for b in range(part_ref.shape[2]):
 
-        def step(w, carry):
+        def step(k, carry):
             direct, turned = carry
-            a_rows = own_ref[w, 0]
-            b_rows = part_ref[0, w, b]
-            b_turn = pltpu.roll(b_rows, nb, 1)
-            direct = direct + a_rows * b_rows[None, :, :]
-            turned = turned + a_rows * b_turn[None, :, :]
+            for u in range(WSTEP):
+                w = k * WSTEP + u
+                a_rows = own_ref[w, 0]
+                b_rows = part_ref[0, w, b]
+                b_turn = pltpu.roll(b_rows, nb, 1)
+                direct = direct + a_rows * b_rows[None, :, :]
+                turned = turned + a_rows * b_turn[None, :, :]
             return direct, turned
 
         zero = jnp.zeros((station_count, station_count, lanes), jnp.float32)
-        direct, turned = lax.fori_loop(0, window_count, step, (zero, zero), unroll=4)
+        direct, turned = lax.fori_loop(0, window_count // WSTEP, step, (zero, zero))
         real = direct + pltpu.roll(direct, nb, 2)
         imag = turned - pltpu.roll(turned, nb, 2)
         out_ref[:, 0, 0, b] = jnp.where(lower, real, imag)

time: 143 us -> 143 us (level)
  no operation moved by 1% of the time
where the time goes in v6:
time: 143 us
  Pallas kernels  51.5 us (36%)
  waiting for transfers between devices  49.2 us (34%)
  between operations  13.6 us (10%)
  local copies, waits for them, and re-layouts  12.5 us (9%)
  other arithmetic  12.3 us (9%)
  starting transfers between devices  2.14 us (1%)
  matrix products  1.53 us (1%)
    pallas_call x1, Pallas kernels, cross_products(): pl.pallas_call(cross_kernel, grid=(comp_count, rounds), in_specs=[pl.Bloc...  51.5 us
    all_gather x1, waiting for transfers between devices, body(): gathered = lax.all_gather(payload, 'pair', axis=0, tiled=False)  38.9 us
    ppermute x3, waiting for transfers between devices, body(): chunk = lax.ppermute(chunk, ('win', 'band'), perm)  10.4 us
    broadcast_in_dim x1, local copies, waits for them, and re-layouts, cross_products(): jnp.broadcast_to(own[:, :, :, None, :], (window_count, comp_count, statio...  3.54 us
    reshape x1, other arithmetic, body(): partners[:, :rows].astype(jnp.float32)  3.41 us
    another operation x2, other arithmetic, body(): swapped = jnp.stack([first, second], axis=0)  2.88 us
  transfers between devices with their start and end apart: 4, of which 3 were waited for; matrix products, arithmetic and copies ran while one was open for 2% of the time, Pallas kernels for 0%

profile of v6, /device:TPU:0, one launch (start us, length us, event | category | flops | bytes accessed | tf_op | source)
XLA Modules:
  0.0 142.8 jit_solution(7025350242825497889)
XLA Ops:
  6.5 0.0 copy-start
  6.5 0.0 all-gather.4.cloned.1.call-start
  6.6 0.8 fusion.24
  7.4 0.1 copy.42
  7.5 0.1 reshape.67
  7.6 0.6 multiply_convert_fusion.1
  8.2 0.0 copy-done
  8.2 0.7 fusion.2
  8.9 0.3 fusion.6
  9.2 0.1 rsqrt_multiply_fusion
  9.3 0.1 pad_maximum_fusion.2
  9.5 0.1 multiply_convert_fusion
  9.6 0.0 copy-start.5
  9.6 0.3 copy.41
  9.9 0.8 maximum_bitcast_fusion
  10.6 0.0 all-gather.4.cloned.1.call-update
  10.7 1.1 copy.40
  11.8 0.0 copy-done.5
  11.8 38.9 %all-gather.4.cloned.1.call-done = bf16[4,1540,128]{2,1,0:T(8,128)(2,1)} async-done(((bf16[1,1540,128]{2,1,0:T(8,128)(2,1)}), bf16[4,1540,128]{2,1,0:T(8,128)(2,1)}) %all-gather.4.cloned.1.call-update) | async-done | bytes 1576976 | tf_op jit(solution)/shard_map/all_gather | solution.py:126
  50.7 2.3 %gather_fusion = bf16[4,1540,128]{2,1,0:T(8,128)(2,1)S(1)} fusion(bf16[4,1540,128]{2,1,0:T(8,128)(2,1)} %all-gather.4.cloned.1.call-done, s32[1024]{0:T(1024)S(1)} %pad_clamp_fusion), kind=kCustom, calls=%fused_computation | custom fusion | bytes 3153936 | tf_op jit(solution)/shard_map/jit(_take)/gather | solution.py:128
  53.0 0.0 copy-start.4
  53.0 1.3 slice.28
  54.2 0.1 reshape_reshape.3
  54.4 0.0 copy-done.4
  54.4 0.2 convolution_bitcast_fusion.1
  54.6 0.1 copy.44
  54.6 0.0 copy-start.1
  54.6 3.4 %convert.9.part_ref = f32[4,64,3,8,128]{4,3,2,1,0:T(8,128)} convert(bf16[4,64,3,8,128]{4,3,2,1,0:T(8,128)(2,1)} %bitcast.39) | non-fusion elementwise | flops 786432 | bytes 4718592 | tf_op jit(solution)/shard_map/reshape | solution.py:131
  58.0 0.0 copy-done.1
  58.0 3.5 %broadcast_in_dim.5.own_ref = f32[64,3,8,8,128]{4,3,2,1,0:T(8,128)} broadcast(f32[64,3,8,128]{3,2,1,0:T(8,128)S(1)} %copy-done.1), dimensions={0,1,2,4} | broadcast | bytes 7077888 | tf_op jit(solution)/shard_map/broadcast_in_dim | solution.py:78
  61.6 51.5 %shard_map.37 = f32[8,3,4,3,8,128]{5,4,3,2,1,0:T(8,128)} custom-call(f32[64,3,8,8,128]{4,3,2,1,0:T(8,128)} %broadcast_in_dim.5.own_ref, f32[4,64,3,8,128]{4,3,2,1,0:T(8,128)} %convert.9.part_ref), custom_call_target="tpu_custom_call" | custom-call | flops 75497472 | bytes 10616832 | tf_op jit(solution)/shard_map/pallas_call | solution.py:80
  113.1 1.4 select_maximum_fusion
  114.5 0.9 constant_dynamic-slice_fusion.2
  115.4 1.5 %collective-permute-start = (f32[2,289,128]{2,1,0:T(8,128)}, f32[2,289,128]{2,1,0:T(8,128)S(1)}, u32[]{:S(2)}, u32[]{:S(2)}) collective-permute-start(f32[2,289,128]{2,1,0:T(8,128)} %get-tuple-element.7), channel_id=1, source_target_pairs={{0,2},{1,3},{2,0},{3,1},{4,6},{5,7},{6,4},{7,5},{8,10},{9,11},{10,... | collective-permute-start | bytes 887816 | tf_op jit(solution)/shard_map/ppermute | solution.py:153
  116.9 0.0 collective-permute-start.2
  116.9 0.7 collective-permute-start.1
  117.5 0.6 cosine_multiply_fusion
  118.2 0.7 copy.37
  118.9 6.8 %collective-permute-done = f32[2,289,128]{2,1,0:T(8,128)S(1)} collective-permute-done((f32[2,289,128]{2,1,0:T(8,128)}, f32[2,289,128]{2,1,0:T(8,128)S(1)}, u32[]{:S(2)}, u32[]{:S(2)}) %collective-permute-start) | collective-permute-done | bytes 295968 | tf_op jit(solution)/shard_map/ppermute | solution.py:153
  125.7 0.0 copy-start.2
  125.7 3.6 %collective-permute-done.2 = f32[2,289,128]{2,1,0:T(8,128)S(1)} collective-permute-done((f32[2,289,128]{2,1,0:T(8,128)}, f32[2,289,128]{2,1,0:T(8,128)S(1)}, u32[]{:S(2)}, u32[]{:S(2)}) %collective-permute-start.2) | collective-permute-done | bytes 295968 | tf_op jit(solution)/shard_map/ppermute | solution.py:153
  129.2 0.0 copy-done.2
  129.2 0.0 collective-permute-done.1
  129.2 1.8 %select_bitcast_fusion.1 = (f32[1,2,289,128]{3,2,1,0:T(8,128)}, f32[2,289,128]{2,1,0:T(8,128)S(1)}) fusion(pred[]{:T(512)S(6)} %eq.8, f32[2,289,128]{2,1,0:T(8,128)} %collective-permute-done.1, f32[2,289,128]{2,1,0:T(8,128)S(1)} %collective-permute-done.2, f32[2,289,128]{2,1,0:T(8,128)} %copy-done.2, f32[8,289,128]{2,1,0:T(8,128)S(1)} %select_maximum_fusion, ...), kind=kLoop, calls=%fused_computation.18 | loop fusion | flops 221952 | bytes 1775621 | tf_op jit(solution)/shard_map/stack | solution.py:159
  131.1 0.1 max.24
  131.2 0.1 div.37
  131.3 1.0 select_bitcast_fusion
  132.3 0.0 copy-start.3
  132.4 1.2 fusion.8
  133.5 0.5 copy.45
  134.0 0.5 div.41
  134.5 0.0 copy-done.3
  134.5 0.7 convolution_bitcast_fusion
  135.1 0.9 copy.46
  (10 shorter events, 0.1 us)
Async XLA Ops:
  6.5 1.7 %copy-start = (bf16[64,3,8,512]{3,2,1,0:T(8,128)(2,1)S(1)}, bf16[64,3,8,512]{3,2,1,0:T(8,128)(2,1)}, u32[]{:S(2)}) copy-start(bf16[64,3,8,512]{3,2,1,0:T(8,128)(2,1)} %param.3) | copy-start | bytes 4718596
  6.5 44.2 %all-gather.4.cloned.1.call-start = ((), (), s32[]{:S(2)}) async-start(), calls=%async_computation | async-start | bytes 1976320 | tf_op jit(solution)/shard_map/all_gather | solution.py:126
  9.6 2.2 %copy-start.5 = (s32[4]{0:T(128)S(1)}, s32[4]{0:T(128)}, u32[]{:S(2)}) copy-start(s32[4]{0:T(128)} %param.5) | copy-start | bytes 52
  53.0 1.4 copy-start.4
  54.6 3.4 %copy-start.1 = (f32[64,3,8,128]{3,2,1,0:T(8,128)S(1)}, f32[64,3,8,128]{3,2,1,0:T(8,128)}, u32[]{:S(2)}) copy-start(f32[64,3,8,128]{3,2,1,0:T(8,128)} %copy.40) | copy-start | bytes 2359300
  115.4 10.3 %collective-permute-start = (f32[2,289,128]{2,1,0:T(8,128)}, f32[2,289,128]{2,1,0:T(8,128)S(1)}, u32[]{:S(2)}, u32[]{:S(2)}) collective-permute-start(f32[2,289,128]{2,1,0:T(8,128)} %get-tuple-element.7), channel_id=1, source_target_pairs={{0,2},{1,3},{2,0},{3,1},{4,6},{5,7},{6,4},{7,5},{8,10},{9,11},{10,... | collective-permute-start | bytes 887816 | tf_op jit(solution)/shard_map/ppermute | solution.py:153
  116.9 12.4 %collective-permute-start.2 = (f32[2,289,128]{2,1,0:T(8,128)}, f32[2,289,128]{2,1,0:T(8,128)S(1)}, u32[]{:S(2)}, u32[]{:S(2)}) collective-permute-start(f32[2,289,128]{2,1,0:T(8,128)} %get-tuple-element.8), channel_id=1, source_target_pairs={{0,3},{1,2},{2,1},{3,0},{4,7},{5,6},{6,5},{7,4},{8,11},{9,10},{10,... | collective-permute-start | bytes 887816 | tf_op jit(solution)/shard_map/ppermute | solution.py:153
  116.9 12.4 %collective-permute-start.1 = (f32[2,289,128]{2,1,0:T(8,128)}, f32[2,289,128]{2,1,0:T(8,128)}, u32[]{:S(2)}, u32[]{:S(2)}) collective-permute-start(f32[2,289,128]{2,1,0:T(8,128)} %get-tuple-element.9), channel_id=1, source_target_pairs={{0,1},{1,0},{2,3},{3,2},{4,5},{5,4},{6,7},{7,6},{8,9},{9,8},{10,11... | collective-permute-start | bytes 887816 | tf_op jit(solution)/shard_map/ppermute | solution.py:153
  125.7 3.6 %copy-start.2 = (f32[2,289,128]{2,1,0:T(8,128)}, f32[2,289,128]{2,1,0:T(8,128)S(1)}, u32[]{:S(2)}) copy-start(f32[2,289,128]{2,1,0:T(8,128)S(1)} %collective-permute-done) | copy-start | bytes 887812
  132.3 2.1 %copy-start.3 = (f32[2,2,64,256]{3,2,1,0:T(8,128)S(1)}, f32[2,2,64,256]{3,2,1,0:T(8,128)}, u32[]{:S(2)}) copy-start(f32[2,2,64,256]{3,2,1,0:T(8,128)} %copy.37) | copy-start | bytes 786436
Sparse Core Ops, SparseCore 0:
  10.8 39.8 all-gather.3

commit v7 on v5

--- a/solution.py
+++ b/solution.py
@@ -10,6 +10,7 @@
 FREQ = 128
 NLAG = 256
 ROUNDS = 4
+WSTEP = 4
 
 
 def dft_table(sample_points, bin_count, first_bin):
@@ -47,47 +48,55 @@
 
 
 def cross_kernel(own_ref, part_ref, out_ref):
-    window_count = own_ref.shape[0]
-    station_count = own_ref.shape[2]
-    lanes = own_ref.shape[4]
+    window_count, comp_count, station_count, lanes = own_ref.shape
     nb = lanes // 2
-    lower = lax.broadcasted_iota(jnp.int32, (station_count, station_count, lanes), 2) < nb
-    for b in range(part_ref.shape[2]):
+    rows = lax.broadcasted_iota(jnp.int32, (station_count, lanes), 0)
+    lower = lax.broadcasted_iota(jnp.int32, (station_count, lanes), 1) < nb
+    moved = [pltpu.roll(rows, k, 0) if k else rows for k in range(station_count)]
+    zero = tuple(jnp.zeros((station_count, lanes), jnp.float32) for _ in range(station_count))
+    for a in range(comp_count):
+        for b in range(part_ref.shape[2]):
 
-        def step(w, carry):
-            direct, turned = carry
-            a_rows = own_ref[w, 0]
-            b_rows = part_ref[0, w, b]
-            b_turn = pltpu.roll(b_rows, nb, 1)
-            direct = direct + a_rows * b_rows[None, :, :]
-            turned = turned + a_rows * b_turn[None, :, :]
-            return direct, turned
+            def step(k, carry):
+                direct, turned = list(carry[0]), list(carry[1])
+                for u in range(WSTEP):
+                    w = k * WSTEP + u
+                    a_tile = own_ref[w, a]
+                    b_tile = part_ref[0, w, b]
+                    b_turn = pltpu.roll(b_tile, nb, 1)
+                    for d in range(station_count):
+                        a_rot = pltpu.roll(a_tile, d, 0) if d else a_tile
+                        direct[d] = direct[d] + a_rot * b_tile
+                        turned[d] = turned[d] + a_rot * b_turn
+                return tuple(direct), tuple(turned)
 
-        zero = jnp.zeros((station_count, station_count, lanes), jnp.float32)
-        direct, turned = lax.fori_loop(0, window_count, step, (zero, zero), unroll=4)
-        real = direct + pltpu.roll(direct, nb, 2)
-        imag = turned - pltpu.roll(turned, nb, 2)
-        out_ref[:, 0, 0, b] = jnp.where(lower, real, imag)
+            direct, turned = lax.fori_loop(0, window_count // WSTEP, step, (zero, zero))
+            for i in range(station_count):
+                dsum = jnp.where(moved[0] == i, direct[0], 0.0)
+                tsum = jnp.where(moved[0] == i, turned[0], 0.0)
+                for d in range(1, station_count):
+                    dsum = jnp.where(moved[d] == i, direct[d], dsum)
+                    tsum = jnp.where(moved[d] == i, turned[d], tsum)
+                real = dsum + pltpu.roll(dsum, nb, 1)
+                imag = tsum - pltpu.roll(tsum, nb, 1)
+                out_ref[i, a, 0, b] = jnp.where(lower, real, imag)
 
 
 def cross_products(own, partners):
     rounds, window_count, comp_count, station_count, lanes = partners.shape
-    own = jnp.broadcast_to(own[:, :, :, None, :], (window_count, comp_count, station_count, station_count, lanes))
     flops = 4 * rounds * window_count * comp_count * comp_count * station_count * station_count * lanes
     return pl.pallas_call(
         cross_kernel,
-        grid=(comp_count, rounds),
+        grid=(rounds,),
         in_specs=[
+            pl.BlockSpec((window_count, comp_count, station_count, lanes), lambda r: (0, 0, 0, 0)),
             pl.BlockSpec(
-                (window_count, 1, station_count, station_count, lanes), lambda a, r: (0, a, 0, 0, 0)
-            ),
-            pl.BlockSpec(
-                (1, window_count, comp_count, station_count, lanes), lambda a, r: (r, 0, 0, 0, 0)
+                (1, window_count, comp_count, station_count, lanes), lambda r: (r, 0, 0, 0, 0)
             ),
         ],
         out_specs=pl.BlockSpec(
-            (station_count, 1, 1, comp_count, station_count, lanes),
-            lambda a, r: (0, a, r, 0, 0, 0),
+            (station_count, comp_count, 1, comp_count, station_count, lanes),
+            lambda r: (0, 0, r, 0, 0, 0),
         ),
         out_shape=jax.ShapeDtypeStruct(
             (station_count, comp_count, rounds, comp_count, station_count, lanes), jnp.float32

time: 143 us -> 144 us (level)
  local copies, waits for them, and re-layouts: 12.5 us -> 8.37 us
  waiting for transfers between devices: 49.2 us -> 52.1 us
    broadcast_in_dim x1 -> x0, local copies, waits for them, and re-layouts: 3.54 us -> none  [cross_products(): jnp.broadcast_to(own[:, :, :, None, :], (window_count, comp_count, statio...]
    ppermute x3, waiting for transfers between devices: 10.4 us -> 12.1 us  [body(): chunk = lax.ppermute(chunk, ('win', 'band'), perm)]
  transfers between devices with their start and end apart: 4 -> 4, of which waited for: 3 -> 3; matrix products, arithmetic and copies ran while one was open for 2% -> 1% of each run, Pallas kernels for 0% -> 0%
where the time goes in v7:
time: 144 us; the launch traced here: 143 us
  Pallas kernels  52.7 us (37%)
  waiting for transfers between devices  52.1 us (36%)
  between operations  13.6 us (9%)
  other arithmetic  13.1 us (9%)
  local copies, waits for them, and re-layouts  8.37 us (6%)
  starting transfers between devices  2.14 us (1%)
    pallas_call x1, Pallas kernels, cross_products(): pl.pallas_call(cross_kernel, grid=(rounds,), in_specs=[pl.BlockSpec((wind...  52.7 us
    all_gather x1, waiting for transfers between devices, body(): gathered = lax.all_gather(payload, 'pair', axis=0, tiled=False)  40 us
    ppermute x3, waiting for transfers between devices, body(): chunk = lax.ppermute(chunk, ('win', 'band'), perm)  12.1 us
    reshape x1, other arithmetic, body(): partners[:, :rows].astype(jnp.float32)  3.25 us
  transfers between devices with their start and end apart: 4, of which 3 were waited for; matrix products, arithmetic and copies ran while one was open for 1% of the time, Pallas kernels for 0%

profile of v7, /device:TPU:0, one launch (start us, length us, event | category | flops | bytes accessed | tf_op | source)
XLA Modules:
  0.0 143.4 jit_solution(2888140372055818260)
XLA Ops:
  6.5 0.0 copy-start
  6.5 0.0 all-gather.4.cloned.1.call-start
  6.6 0.8 fusion.20
  7.4 0.1 copy.43
  7.5 0.1 reshape.66
  7.6 0.6 multiply_convert_fusion.1
  8.2 0.0 copy-done
  8.2 0.6 convolution_bitcast_fusion
  8.8 0.3 fusion.1
  9.1 0.1 copy.42
  9.2 0.1 rsqrt_multiply_fusion
  9.3 0.1 pad_maximum_fusion.2
  9.4 0.0 copy-start.4
  9.5 1.0 fusion.19
  10.5 0.8 maximum_bitcast_fusion
  11.2 0.0 all-gather.4.cloned.1.call-update
  11.3 0.0 copy-done.4
  11.4 40.0 %all-gather.4.cloned.1.call-done = bf16[4,1540,128]{2,1,0:T(8,128)(2,1)} async-done(((bf16[1,1540,128]{2,1,0:T(8,128)(2,1)}), bf16[4,1540,128]{2,1,0:T(8,128)(2,1)}) %all-gather.4.cloned.1.call-update) | async-done | bytes 1576976 | tf_op jit(solution)/shard_map/all_gather | solution.py:132
  51.3 2.3 %gather_fusion = bf16[4,1540,128]{2,1,0:T(8,128)(2,1)S(1)} fusion(bf16[4,1540,128]{2,1,0:T(8,128)(2,1)} %all-gather.4.cloned.1.call-done, s32[1024]{0:T(1024)S(1)} %pad_clamp_fusion), kind=kCustom, calls=%fused_computation | custom fusion | bytes 3153936 | tf_op jit(solution)/shard_map/jit(_take)/gather | solution.py:134
  53.6 0.0 copy-start.3
  53.6 1.3 slice.28
  54.9 0.1 reshape_reshape.3
  55.0 0.0 copy-done.3
  55.0 0.2 convolution_bitcast_fusion.2
  55.2 0.1 copy.45
  55.2 3.2 %convert.9.part_ref = f32[4,64,3,8,128]{4,3,2,1,0:T(8,128)} convert(bf16[4,64,3,8,128]{4,3,2,1,0:T(8,128)(2,1)} %bitcast.40) | non-fusion elementwise | flops 786432 | bytes 4718592 | tf_op jit(solution)/shard_map/reshape | solution.py:137
  58.5 52.7 %shard_map.37 = f32[8,3,4,3,8,128]{5,4,3,2,1,0:T(8,128)} custom-call(f32[64,3,8,128]{3,2,1,0:T(8,128)} %get-tuple-element.7.own_ref, f32[4,64,3,8,128]{4,3,2,1,0:T(8,128)} %convert.9.part_ref), custom_call_target="tpu_custom_call" | custom-call | flops 75497472 | bytes 5111808 | tf_op jit(solution)/shard_map/pallas_call | solution.py:88
  111.2 1.4 select_maximum_fusion
  112.5 0.9 constant_dynamic-slice_fusion.2
  113.5 0.0 collective-permute-start.1
  113.5 1.6 %collective-permute-start.2 = (f32[2,289,128]{2,1,0:T(8,128)}, f32[2,289,128]{2,1,0:T(8,128)S(1)}, u32[]{:S(2)}, u32[]{:S(2)}) collective-permute-start(f32[2,289,128]{2,1,0:T(8,128)} %get-tuple-element.10), channel_id=1, source_target_pairs={{0,3},{1,2},{2,1},{3,0},{4,7},{5,6},{6,5},{7,4},{8,11},{9,10},{10,... | collective-permute-start | bytes 887816 | tf_op jit(solution)/shard_map/ppermute | solution.py:159
  115.1 0.6 collective-permute-start
  115.6 0.6 cosine_multiply_fusion
  116.2 0.7 copy.38
  117.0 0.0 collective-permute-done.1
  117.0 6.0 %collective-permute-done.2 = f32[2,289,128]{2,1,0:T(8,128)S(1)} collective-permute-done((f32[2,289,128]{2,1,0:T(8,128)}, f32[2,289,128]{2,1,0:T(8,128)S(1)}, u32[]{:S(2)}, u32[]{:S(2)}) %collective-permute-start.2) | collective-permute-done | bytes 295968 | tf_op jit(solution)/shard_map/ppermute | solution.py:159
  122.9 0.0 copy-start.1
  122.9 0.7 copy-done.1
  123.7 6.1 %collective-permute-done = f32[2,289,128]{2,1,0:T(8,128)} collective-permute-done((f32[2,289,128]{2,1,0:T(8,128)}, f32[2,289,128]{2,1,0:T(8,128)}, u32[]{:S(2)}, u32[]{:S(2)}) %collective-permute-start) | collective-permute-done | bytes 295968 | tf_op jit(solution)/shard_map/ppermute | solution.py:159
  129.8 1.8 %select_bitcast_fusion.1 = (f32[1,2,289,128]{3,2,1,0:T(8,128)}, f32[2,289,128]{2,1,0:T(8,128)S(1)}) fusion(pred[]{:T(512)S(6)} %eq.8, f32[2,289,128]{2,1,0:T(8,128)S(1)} %collective-permute-done.1, f32[2,289,128]{2,1,0:T(8,128)} %copy-done.1, f32[2,289,128]{2,1,0:T(8,128)} %collective-permute-done, f32[8,289,128]{2,1,0:T(8,128)S(1)} %select_maximum_fusion, ...), kind=kLoop, calls=%fused_computation.16 | loop fusion | flops 221952 | bytes 1775621 | tf_op jit(solution)/shard_map/stack | solution.py:165
  131.6 0.1 max.24
  131.7 0.1 div.37
  131.8 1.0 select_bitcast_fusion
  132.9 0.0 copy-start.2
  132.9 1.2 fusion.3
  134.0 0.5 copy.46
  134.5 0.5 div.41
  135.0 0.0 copy-done.2
  135.0 0.7 convolution_bitcast_fusion.1
  135.7 0.9 copy.47
  (10 shorter events, 0.1 us)
Async XLA Ops:
  6.5 1.7 %copy-start = (bf16[64,3,8,512]{3,2,1,0:T(8,128)(2,1)S(1)}, bf16[64,3,8,512]{3,2,1,0:T(8,128)(2,1)}, u32[]{:S(2)}) copy-start(bf16[64,3,8,512]{3,2,1,0:T(8,128)(2,1)} %param.3) | copy-start | bytes 4718596
  6.5 44.8 %all-gather.4.cloned.1.call-start = ((), (), s32[]{:S(2)}) async-start(), calls=%async_computation | async-start | bytes 1976320 | tf_op jit(solution)/shard_map/all_gather | solution.py:132
  9.4 1.9 %copy-start.4 = (s32[4]{0:T(128)S(1)}, s32[4]{0:T(128)}, u32[]{:S(2)}) copy-start(s32[4]{0:T(128)} %param.5) | copy-start | bytes 52
  53.6 1.4 copy-start.3
  113.5 3.5 %collective-permute-start.1 = (f32[2,289,128]{2,1,0:T(8,128)}, f32[2,289,128]{2,1,0:T(8,128)S(1)}, u32[]{:S(2)}, u32[]{:S(2)}) collective-permute-start(f32[2,289,128]{2,1,0:T(8,128)} %get-tuple-element.11), channel_id=1, source_target_pairs={{0,1},{1,0},{2,3},{3,2},{4,5},{5,4},{6,7},{7,6},{8,9},{9,8},{10,11... | collective-permute-start | bytes 887816 | tf_op jit(solution)/shard_map/ppermute | solution.py:159
  113.5 9.5 %collective-permute-start.2 = (f32[2,289,128]{2,1,0:T(8,128)}, f32[2,289,128]{2,1,0:T(8,128)S(1)}, u32[]{:S(2)}, u32[]{:S(2)}) collective-permute-start(f32[2,289,128]{2,1,0:T(8,128)} %get-tuple-element.10), channel_id=1, source_target_pairs={{0,3},{1,2},{2,1},{3,0},{4,7},{5,6},{6,5},{7,4},{8,11},{9,10},{10,... | collective-permute-start | bytes 887816 | tf_op jit(solution)/shard_map/ppermute | solution.py:159
  115.1 14.7 %collective-permute-start = (f32[2,289,128]{2,1,0:T(8,128)}, f32[2,289,128]{2,1,0:T(8,128)}, u32[]{:S(2)}, u32[]{:S(2)}) collective-permute-start(f32[2,289,128]{2,1,0:T(8,128)} %get-tuple-element.9), channel_id=1, source_target_pairs={{0,2},{1,3},{2,0},{3,1},{4,6},{5,7},{6,4},{7,5},{8,10},{9,11},{10,... | collective-permute-start | bytes 887816 | tf_op jit(solution)/shard_map/ppermute | solution.py:159
  122.9 0.7 copy-start.1
  132.9 2.1 %copy-start.2 = (f32[2,2,64,256]{3,2,1,0:T(8,128)S(1)}, f32[2,2,64,256]{3,2,1,0:T(8,128)}, u32[]{:S(2)}) copy-start(f32[2,2,64,256]{3,2,1,0:T(8,128)} %copy.38) | copy-start | bytes 786436
Sparse Core Ops, SparseCore 0:
  11.4 39.8 all-gather.3

commit v8 on v1

v8 whole, which is shorter than its diff:
```python
import math

import jax
import jax.numpy as jnp
from jax import lax
from jax.experimental import pallas as pl
from jax.experimental.pallas import tpu as pltpu
from jax.sharding import PartitionSpec as P

FREQ = 128
NLAG = 256
ROUNDS = 4
WSTEP = 4


def dft_table(sample_points, bin_count, first_bin):
    sample_moments = jnp.arange(sample_points, dtype=jnp.int32)
    spectral_bin_index = first_bin + 1 + jnp.arange(bin_count, dtype=jnp.int32)
    phase_turns = jnp.mod(sample_moments[:, None] * spectral_bin_index[None, :], sample_points)
    phases = phase_turns.astype(jnp.float32) * (2.0 * math.pi / sample_points)
    hanning_taper = 0.5 - 0.5 * jnp.cos(
        sample_moments.astype(jnp.float32) * (2.0 * math.pi / sample_points)
    )
    weight = (hanning_taper * math.sqrt(8.0 / (3.0 * sample_points)))[:, None]
    return jnp.concatenate([weight * jnp.cos(phases), -(weight * jnp.sin(phases))], axis=1).astype(
        jnp.bfloat16
    )


def lag_table(sample_points, bin_count, first_bin, lag_count, all_bins):
    spectral_bin_index = first_bin + 1 + jnp.arange(bin_count, dtype=jnp.int32)
    shifts = jnp.arange(lag_count, dtype=jnp.int32) - lag_count // 2
    phase_turns = jnp.mod(spectral_bin_index[:, None] * shifts[None, :], sample_points)
    phases = phase_turns.astype(jnp.float32) * (2.0 * math.pi / sample_points)
    lag_scale = 1.0 / math.sqrt(all_bins)
    return jnp.concatenate([jnp.cos(phases) * lag_scale, -(jnp.sin(phases) * lag_scale)], axis=0)


def whiten(spectra, validity):
    bin_count = spectra.shape[-1] // 2
    real_part = spectra[..., :bin_count]
    imag_part = spectra[..., bin_count:]
    band_power = jnp.mean(real_part * real_part + imag_part * imag_part, axis=1)
    amplitude = jnp.sqrt(jnp.maximum(band_power, 0.25))
    factor = validity[:, :, None] / amplitude
    factor = jnp.concatenate([factor, factor], axis=-1)
    return (spectra * factor[:, None]).astype(jnp.bfloat16)


def dft_kernel(rec_ref, table_ref, valid_ref, out_ref):
    station_count, window_count = valid_ref.shape
    comp_count = rec_ref.shape[0] // station_count
    nb = table_ref.shape[0] // 2
    table = table_ref[...]
    for s in range(station_count):
        parts = []
        for c in range(comp_count):
            z = lax.dot_general(
                table,
                rec_ref[c * station_count + s],
                (((1,), (1,)), ((), ())),
                preferred_element_type=jnp.float32,
            )
            parts.append((z[:nb], z[nb:]))
        total = parts[0][0] * parts[0][0] + parts[0][1] * parts[0][1]
        for c in range(1, comp_count):
            total = total + (parts[c][0] * parts[c][0] + parts[c][1] * parts[c][1])
        band_power = total / float(comp_count)
        amplitude = jnp.sqrt(jnp.maximum(band_power, 0.25))
        factor = valid_ref[pl.ds(s, 1), :] / amplitude
        for c in range(comp_count):
            out_ref[c * station_count + s, :, pl.ds(0, window_count)] = parts[c][0] * factor
            out_ref[c * station_count + s, :, pl.ds(window_count, window_count)] = parts[c][1] * factor


def dft_whiten(rec_t, table_t, valid_t):
    rows, window_count, sample_points = rec_t.shape
    nb = table_t.shape[0] // 2
    return pl.pallas_call(
        dft_kernel,
        out_shape=jax.ShapeDtypeStruct((rows, nb, 2 * window_count), jnp.float32),
        cost_estimate=pl.CostEstimate(
            flops=2 * rows * window_count * sample_points * 2 * nb,
            transcendentals=rows * nb * window_count,
            bytes_accessed=2 * rec_t.size + 2 * table_t.size + 4 * rows * nb * 2 * window_count,
        ),
    )(rec_t, table_t, valid_t)


def body(records, valid_mask, round_keys):
    window_count, comp_count, station_count, sample_points = records.shape
    bands = lax.axis_size("band")
    wins = lax.axis_size("win")
    band_index = lax.axis_index("band")
    pair_index = lax.axis_index("pair")
    nb = FREQ // bands
    lanes = 2 * window_count
    rounds = round_keys.shape[0]
    xs = comp_count * station_count

    dft_rows = dft_table(sample_points, nb, band_index * nb)
    rec_t = records.reshape(window_count, xs, sample_points).transpose(1, 0, 2)
    validity = valid_mask.astype(jnp.float32)
    spec = dft_whiten(rec_t, dft_rows.T, validity.T).astype(jnp.bfloat16)

    vrows = -(-window_count * station_count // lanes)
    vflat = validity.astype(jnp.bfloat16).reshape(-1)
    vflat = jnp.pad(vflat, (0, vrows * lanes - vflat.shape[0])).reshape(vrows, lanes)
    payload = jnp.concatenate([spec.reshape(xs * nb, lanes), vflat], axis=0)

    gathered = lax.all_gather(payload, "pair", axis=0, tiled=False)
    partner_list = jnp.bitwise_xor(pair_index, round_keys)
    partners = jnp.take(gathered, partner_list, axis=0, mode="clip")
    partner_valid = partners[:, xs * nb :].reshape(rounds, -1)[:, : window_count * station_count]
    partner_valid = partner_valid.reshape(rounds, window_count, station_count).astype(jnp.float32)
    other = partners[:, : xs * nb].reshape(rounds, xs, nb, lanes)

    half = lax.broadcasted_iota(jnp.int32, (lanes,), 0) < window_count
    turned = jnp.roll(other, window_count, axis=-1) * jnp.where(half, -1.0, 1.0).astype(jnp.bfloat16)
    rhs = jnp.stack([other, turned], axis=0)
    rhs = rhs.transpose(3, 0, 1, 2, 4).reshape(nb, 2 * rounds * xs, lanes)
    lhs = spec.transpose(1, 0, 2)
    prod = jnp.einsum("fxk,fyk->fxy", lhs, rhs, preferred_element_type=jnp.float32)
    prod = prod.reshape(nb, comp_count, station_count, 2 * rounds * xs)

    counts = jnp.einsum("wi,rwj->irj", validity, partner_valid).reshape(station_count, rounds * station_count)
    slab = jnp.zeros((1, comp_count, station_count, 2 * rounds * xs), jnp.float32)
    slab = slab.at[0, 0, :, : rounds * station_count].set(counts)
    ext = jnp.concatenate([prod, slab], axis=0)

    group = wins * bands
    per_dev = station_count // group
    me = lax.axis_index("win") * bands + band_index
    by_offset = [None] * bands
    for shift in range(group):
        dest = (me + shift) % group
        chunk = lax.dynamic_slice_in_dim(ext, dest * per_dev, per_dev, 2)
        if shift:
            perm = [(k, (k + shift) % group) for k in range(group)]
            chunk = lax.ppermute(chunk, ("win", "band"), perm)
        q = shift % bands
        by_offset[q] = chunk if by_offset[q] is None else by_offset[q] + chunk
    totals = by_offset[0][nb, 0, :, : rounds * station_count].reshape(per_dev, rounds, station_count)
    ordered = []
    for bb in range(bands):
        pick = by_offset[0]
        for q in range(1, bands):
            pick = jnp.where((band_index - q) % bands == bb, by_offset[q], pick)
        ordered.append(pick[:nb])
    stacked = jnp.stack(ordered, axis=0)
    stacked = stacked.reshape(bands, nb, comp_count, per_dev, 2, rounds, comp_count, station_count)
    divisor = jnp.maximum(totals, 1.0)[None, None, None, :, None, :, None, :]
    stacked = stacked / divisor

    full_lag = lag_table(sample_points, FREQ, 0, NLAG, FREQ)
    full_lag = full_lag.reshape(2, bands, nb, NLAG).transpose(1, 0, 2, 3)
    lagged = jnp.einsum(
        "gfaiurbj,gufl->riabjl",
        stacked,
        full_lag,
        precision=lax.Precision.HIGHEST,
        preferred_element_type=jnp.float32,
    )
    return lagged.reshape(rounds, per_dev, comp_count, comp_count * station_count, NLAG)


def solution(mesh):
    placed = (P(("hours", "win"), None, "pair", None), P(("hours", "win"), "pair"), P())
    return jax.shard_map(
        body,
        mesh=mesh,
        in_specs=placed,
        out_specs=P(None, ("hours", "pair", "win", "band"), None, None, None),
        check_vma=False,
    )
```

time: 174 us -> 105 us (0.60)
  blocking collectives: 35.1 us -> 0 us
  local copies, waits for them, and re-layouts: 40.3 us -> 22.9 us
  other arithmetic: 27.9 us -> 11.4 us
  matrix products: 18 us -> 3.2 us
  waiting for transfers between devices: 38.7 us -> 46.9 us
  Pallas kernels: 0 us -> 3.44 us
  starting transfers between devices: 0.04 us -> 3.22 us
    all_gather x1 -> x0, blocking collectives: 30.9 us -> none  [body(): mask_all = lax.all_gather(valid_mask, ('pair', 'win'), axis=0, tiled=False)]
    add x1 -> x2, other arithmetic: 21 us -> 0.13 us  [body(): by_offset[q] = chunk if by_offset[q] is None else by_offset[q] + chunk]
    reshape x7 -> x3, local copies, waits for them, and re-layouts: 20.4 us -> 2.96 us  [the longest x1 1.99 us: body(): prod = prod.reshape(nb, comp_count, station_count, 2 * rounds * xs)]
    dot_general x4 -> x3, matrix products: 18 us -> 3.2 us  [the longest x1 1.83 us: body(): jnp.einsum('fxk,fyk->fxy', lhs, rhs, preferred_element_type=jnp.float32)]
    ppermute x0 -> x3, waiting for transfers between devices: none -> 8.76 us  [body(): chunk = lax.ppermute(chunk, ('win', 'band'), perm)]
    sub x1 -> x0, local copies, waits for them, and re-layouts: 5.61 us -> none  [body(): imag = prod[..., 1, 0, :] - prod[..., 0, 1, :]]
    add x1 -> x0, local copies, waits for them, and re-layouts: 5.6 us -> none  [body(): real = prod[..., 0, 0, :] + prod[..., 1, 1, :]]
    dynamic_slice x0 -> x4, local copies, waits for them, and re-layouts: none -> 5.14 us  [body(): chunk = lax.dynamic_slice_in_dim(ext, dest * per_dev, per_dev, 2)]
  transfers between devices with their start and end apart: 2 -> 4, of which waited for: 2 -> 3; matrix products, arithmetic and copies ran while one was open for 3% -> 8% of each run, Pallas kernels for 0% -> 0%
where the time goes in v8:
time: 105 us
  waiting for transfers between devices  46.9 us (45%)
  local copies, waits for them, and re-layouts  22.9 us (22%)
  between operations  13.7 us (13%)
  other arithmetic  11.4 us (11%)
  Pallas kernels  3.44 us (3%)
  starting transfers between devices  3.22 us (3%)
  matrix products  3.2 us (3%)
    all_gather x1, waiting for transfers between devices, body(): gathered = lax.all_gather(payload, 'pair', axis=0, tiled=False)  38.1 us
    ppermute x3, waiting for transfers between devices, body(): chunk = lax.ppermute(chunk, ('win', 'band'), perm)  8.76 us
    dynamic_slice x4, local copies, waits for them, and re-layouts, body(): chunk = lax.dynamic_slice_in_dim(ext, dest * per_dev, per_dev, 2)  5.14 us
    unnamed x15, local copies, waits for them, and re-layouts  4.41 us
    ppermute x3, local copies, waits for them, and re-layouts, body(): chunk = lax.ppermute(chunk, ('win', 'band'), perm)  3.71 us
    pallas_call x1, Pallas kernels, dft_whiten(): pl.pallas_call(dft_kernel, out_shape=jax.ShapeDtypeStruct((rows, nb, 2 *...  3.44 us
    ppermute x3, starting transfers between devices, body(): chunk = lax.ppermute(chunk, ('win', 'band'), perm)  3.21 us
    gather x1, local copies, waits for them, and re-layouts, body(): partners = jnp.take(gathered, partner_list, axis=0, mode='clip')  2.26 us
  transfers between devices with their start and end apart: 4, of which 3 were waited for; matrix products, arithmetic and copies ran while one was open for 8% of the time, Pallas kernels for 0%

profile of v8, /device:TPU:0, one launch (start us, length us, event | category | flops | bytes accessed | tf_op | source)
XLA Modules:
  0.0 104.7 jit_solution(933817613009530108)
XLA Ops:
  6.5 0.0 all-gather.4.cloned.1.call-start
  6.6 1.3 %convert_bitcast_fusion = (f32[8,64]{1,0:T(8,128)}, bf16[64,8]{0,1:T(8,128)(2,1)S(1)}) fusion(s32[64,8]{0,1:T(8,128)} %param.6), kind=kLoop, calls=%fused_computation.50 | loop fusion | flops 1024 | bytes 5120 | tf_op jit(solution)/shard_map/transpose | solution.py:104
  7.9 0.1 copy.39
  8.0 0.1 reshape.142
  8.1 3.1 %copy.38 = bf16[64,3,8,512]{3,0,2,1:T(8,128)(2,1)} copy(bf16[64,3,8,512]{3,2,1,0:T(8,128)(2,1)} %param.5) | data formatting | bytes 3145728 | tf_op args[0]
  11.2 0.6 multiply_convert_fusion
  11.8 0.7 maximum_bitcast_fusion.1.table_ref
  12.5 3.4 %shard_map.37 = f32[24,64,128]{2,1,0:T(8,128)} custom-call(bf16[24,64,512]{2,1,0:T(8,128)(2,1)} %bitcast.57, bf16[128,512]{1,0:T(8,128)(2,1)} %maximum_bitcast_fusion.1.table_ref, f32[8,64]{1,0:T(8,128)} %get-tuple-element.24.valid_ref), custom_call_target="tpu_custom_call" | custom-call | flops 201326592 | bytes 2490368 | tf_op jit(solution)/shard_map/pallas_call | solution.py:79
  15.9 0.0 copy-start.6
  15.9 1.3 %convert_element_type.39 = bf16[24,64,128]{2,1,0:T(8,128)(2,1)S(1)} convert(f32[24,64,128]{2,1,0:T(8,128)} %shard_map.37) | non-fusion elementwise | flops 196608 | bytes 1179648 | tf_op jit(solution)/shard_map/convert_element_type | solution.py:104
  17.2 0.8 maximum_bitcast_fusion
  18.0 0.0 all-gather.4.cloned.1.call-update
  18.1 0.6 iota_add_fusion.2
  18.7 0.6 fusion.18
  19.3 0.6 iota_add_fusion
  19.8 0.0 copy-done.6
  19.8 0.0 copy-done
  19.9 0.1 convert_bitcast_fusion.1
  19.9 38.1 %all-gather.4.cloned.1.call-done = bf16[4,1540,128]{2,1,0:T(8,128)(2,1)} async-done(((bf16[1,1540,128]{2,1,0:T(8,128)(2,1)}), bf16[4,1540,128]{2,1,0:T(8,128)(2,1)}) %all-gather.4.cloned.1.call-update) | async-done | bytes 1576976 | tf_op jit(solution)/shard_map/all_gather | solution.py:111
  58.0 2.3 %gather_fusion = bf16[4,1540,128]{2,1,0:T(8,128)(2,1)S(1)} fusion(bf16[4,1540,128]{2,1,0:T(8,128)(2,1)} %all-gather.4.cloned.1.call-done, s32[1024]{0:T(1024)S(1)} %pad_clamp_fusion), kind=kCustom, calls=%fused_computation | custom fusion | bytes 3153936 | tf_op jit(solution)/shard_map/jit(_take)/gather | solution.py:113
  60.3 0.0 copy-start.2
  60.3 0.1 slice.60
  60.4 0.1 reshape_reshape.3
  60.5 0.5 copy-done.2
  61.0 0.2 convolution_bitcast_fusion.2
  61.2 0.3 copy.45
  61.5 1.0 copy.42
  62.5 0.7 fusion.20
  63.2 0.0 copy-start.5
  63.2 2.0 %copy_bitcast_fusion = (bf16[1,4,24,64,64]{4,2,1,0,3:T(8,128)(2,1)S(1)}, bf16[1,4,24,64,64]{4,2,1,0,3:T(8,128)(2,1)S(1)}) fusion(bf16[4,24,64,64]{3,2,1,0:T(8,128)(2,1)S(1)} %get-tuple-element.21, bf16[4,24,64,64]{3,2,1,0:T(8,128)(2,1)S(1)} %get-tuple-element.20), kind=kLoop, calls=%fused_computation.5 | loop fusion | bytes 3145728 | tf_op jit(solution)/shard_map/jit(_roll_static)/concatenate | solution.py:119
  65.2 0.0 copy-done.5
  65.3 1.0 maximum_multiply_fusion
  66.2 0.3 pad_maximum_fusion
  66.5 1.8 %convolution_bitcast_fusion = f32[64,3,8,192]{3,2,1,0:T(8,128)S(1)} fusion(bf16[64,192,128]{2,1,0:T(8,128)(2,1)S(1)} %bitcast.56, bf16[64,24,128]{2,0,1:T(8,128)(2,1)S(1)} %convert_bitcast_fusion.1), kind=kOutput, calls=%fused_computation.7 | convolution fusion | flops 75497472 | bytes 4718592 | tf_op jit(solution)/shard_map/fxk,fyk->fxy/dot_general | solution.py:123
  68.3 2.0 %copy.46 = f32[64,3,8,192]{0,3,2,1:T(8,128)} copy(f32[64,3,8,192]{3,2,1,0:T(8,128)S(1)} %convolution_bitcast_fusion) | data formatting | bytes 2359296 | tf_op jit(solution)/shard_map/reshape | solution.py:124
  70.3 1.9 %select_maximum_fusion = f32[65,3,8,192]{0,3,2,1:T(8,128)S(1)} fusion(f32[1,1,8,32]{0,3,2,1:T(8,128)S(1)} %copy.45, f32[64,3,8,192]{0,3,2,1:T(8,128)} %copy.46), kind=kLoop, calls=%fused_computation.2 | loop fusion | flops 898560 | bytes 2378752 | tf_op jit(solution)/shard_map/concatenate | solution.py:129
  72.3 0.0 copy-start.3
  72.3 0.0 copy-start.4
  72.3 1.0 constant_dynamic-slice_fusion.1
  73.3 2.1 %copy.51 = f32[65,3,2,192]{3,2,1,0:T(2,128)} copy(f32[65,3,2,192]{0,3,2,1:T(8,128)} %get-tuple-element.18) | data formatting | bytes 599040 | tf_op jit(solution)/shard_map/dynamic_slice | solution.py:137
  75.4 1.5 %collective-permute-start.2 = (f32[65,3,2,192]{3,2,1,0:T(2,128)}, f32[65,3,2,192]{3,2,1,0:T(2,128)}, u32[]{:S(2)}, u32[]{:S(2)}) collective-permute-start(f32[65,3,2,192]{3,2,1,0:T(2,128)} %copy.51), channel_id=1, source_target_pairs={{0,2},{1,3},{2,0},{3,1},{4,6},{5,7},{6,4},{7,5},{8,10},{9,11},{10,... | collective-permute-start | bytes 898568 | tf_op jit(solution)/shard_map/ppermute | solution.py:140
  76.8 0.0 copy-done.3
  76.8 0.0 copy-done.4
  76.8 0.6 cosine_multiply_fusion
  77.4 0.7 pad_maximum_fusion.1
  78.2 1.0 copy.48
  79.2 1.0 copy.47
  80.2 0.0 collective-permute-start
  80.2 1.7 %collective-permute-start.1 = (f32[65,3,2,192]{3,2,1,0:T(2,128)}, f32[65,3,2,192]{3,2,1,0:T(2,128)}, u32[]{:S(2)}, u32[]{:S(2)}) collective-permute-start(f32[65,3,2,192]{3,2,1,0:T(2,128)} %copy.48), channel_id=1, source_target_pairs={{0,3},{1,0},{2,1},{3,2},{4,7},{5,4},{6,5},{7,6},{8,11},{9,8},{10,9... | collective-permute-start | bytes 898568 | tf_op jit(solution)/shard_map/ppermute | solution.py:140
  82.0 5.8 %collective-permute-done.2 = f32[65,3,2,192]{3,2,1,0:T(2,128)} collective-permute-done((f32[65,3,2,192]{3,2,1,0:T(2,128)}, f32[65,3,2,192]{3,2,1,0:T(2,128)}, u32[]{:S(2)}, u32[]{:S(2)}) %collective-permute-start.2) | collective-permute-done | bytes 299552 | tf_op jit(solution)/shard_map/ppermute | solution.py:140
  87.8 1.2 %copy.52 = f32[65,3,2,192]{0,3,2,1:T(8,128)S(1)} copy(f32[65,3,2,192]{3,2,1,0:T(2,128)} %collective-permute-done.2) | data formatting | bytes 599040 | tf_op jit(solution)/shard_map/ppermute | solution.py:140
  89.0 0.1 dynamic-slice_add_fusion
  89.1 0.2 fusion.15
  89.3 0.1 max.15
  89.4 2.9 %collective-permute-done = f32[65,3,2,192]{3,2,1,0:T(2,128)} collective-permute-done((f32[65,3,2,192]{3,2,1,0:T(2,128)}, f32[65,3,2,192]{3,2,1,0:T(2,128)}, u32[]{:S(2)}, u32[]{:S(2)}) %collective-permute-start) | collective-permute-done | bytes 299552 | tf_op jit(solution)/shard_map/ppermute | solution.py:140
  92.3 1.2 %copy.49 = f32[65,3,2,192]{0,3,2,1:T(8,128)S(1)} copy(f32[65,3,2,192]{3,2,1,0:T(2,128)} %collective-permute-done) | data formatting | bytes 599040 | tf_op jit(solution)/shard_map/ppermute | solution.py:140
  93.6 0.0 collective-permute-done.1
  93.6 1.2 %copy.50 = f32[65,3,2,192]{0,3,2,1:T(8,128)S(1)} copy(f32[65,3,2,192]{3,2,1,0:T(2,128)} %collective-permute-done.1) | data formatting | bytes 599040 | tf_op jit(solution)/shard_map/ppermute | solution.py:140
  94.8 0.1 add.111
  94.9 0.0 copy-start.1
  94.9 0.1 slice_select_fusion.1
  95.0 0.8 copy-done.1
  95.8 1.2 %convolution_bitcast_fusion.1 = f32[4,2,3,24,256]{4,3,0,1,2:T(8,128)S(1)} fusion(f32[1,64,3,2,2,4,3,8]{1,7,6,5,4,3,2,0:T(8,128)S(1)} %bitcast.60, f32[1,64,3,2,2,4,3,8]{1,7,6,5,4,3,2,0:T(8,128)S(1)} %bitcast.59, f32[2,4,8]{2,1,0:T(4,128)S(1)} %max.15, f32[2,2,64,256]{3,2,1,0:T(8,128)S(1)} %bitcast.61), kind=kOutput, calls=%fused_computation.8 | convolution fusion | flops 453279744 | bytes 1442048 | tf_op jit(solution)/shard_map/gfaiurbj,gufl->riabjl/dot_general | solution.py:157
  97.0 0.9 copy.54
  (6 shorter events, 0.1 us)
Async XLA Ops:
  6.5 51.5 %all-gather.4.cloned.1.call-start = ((), (), s32[]{:S(2)}) async-start(), calls=%async_computation | async-start | bytes 1976320 | tf_op jit(solution)/shard_map/all_gather | solution.py:111
  15.9 3.9 %copy-start.6 = (s32[4]{0:T(128)S(1)}, s32[4]{0:T(128)}, u32[]{:S(2)}) copy-start(s32[4]{0:T(128)} %param.7) | copy-start | bytes 52
  15.9 3.9 %copy-start = (f32[24,64,128]{2,1,0:T(8,128)S(1)}, f32[24,64,128]{2,1,0:T(8,128)}, u32[]{:S(2)}) copy-start(f32[24,64,128]{2,1,0:T(8,128)} %shard_map.37) | copy-start | bytes 2359300
  60.3 0.7 copy-start.2
  63.2 2.0 %copy-start.5 = (bf16[128]{0:T(256)(128)(2,1)S(1)}, bf16[128]{0:T(256)(128)(2,1)}, u32[]{:S(2)}) copy-start(bf16[128]{0:T(256)(128)(2,1)} %fusion.18) | copy-start | bytes 772
  72.3 4.6 %copy-start.3 = (s32[256]{0:T(256)S(1)}, s32[256]{0:T(256)}, u32[]{:S(2)}) copy-start(s32[256]{0:T(256)} %iota_add_fusion) | copy-start | bytes 3076
  72.3 4.6 %copy-start.4 = (s32[128]{0:T(128)S(1)}, s32[128]{0:T(128)}, u32[]{:S(2)}) copy-start(s32[128]{0:T(128)} %iota_add_fusion.2) | copy-start | bytes 1540
  75.4 12.4 %collective-permute-start.2 = (f32[65,3,2,192]{3,2,1,0:T(2,128)}, f32[65,3,2,192]{3,2,1,0:T(2,128)}, u32[]{:S(2)}, u32[]{:S(2)}) collective-permute-start(f32[65,3,2,192]{3,2,1,0:T(2,128)} %copy.51), channel_id=1, source_target_pairs={{0,2},{1,3},{2,0},{3,1},{4,6},{5,7},{6,4},{7,5},{8,10},{9,11},{10,... | collective-permute-start | bytes 898568 | tf_op jit(solution)/shard_map/ppermute | solution.py:140
  80.2 12.1 %collective-permute-start = (f32[65,3,2,192]{3,2,1,0:T(2,128)}, f32[65,3,2,192]{3,2,1,0:T(2,128)}, u32[]{:S(2)}, u32[]{:S(2)}) collective-permute-start(f32[65,3,2,192]{3,2,1,0:T(2,128)} %copy.47), channel_id=1, source_target_pairs={{0,1},{1,2},{2,3},{3,0},{4,5},{5,6},{6,7},{7,4},{8,9},{9,10},{10,1... | collective-permute-start | bytes 898568 | tf_op jit(solution)/shard_map/ppermute | solution.py:140
  80.2 13.3 %collective-permute-start.1 = (f32[65,3,2,192]{3,2,1,0:T(2,128)}, f32[65,3,2,192]{3,2,1,0:T(2,128)}, u32[]{:S(2)}, u32[]{:S(2)}) collective-permute-start(f32[65,3,2,192]{3,2,1,0:T(2,128)} %copy.48), channel_id=1, source_target_pairs={{0,3},{1,0},{2,1},{3,2},{4,7},{5,4},{6,5},{7,6},{8,11},{9,8},{10,9... | collective-permute-start | bytes 898568 | tf_op jit(solution)/shard_map/ppermute | solution.py:140
  94.9 1.0 copy-start.1
Sparse Core Ops, SparseCore 0:
  18.1 39.8 all-gather.3

commit v9 on v8

v9 whole, which is shorter than its diff:
```python
import math

import jax
import jax.numpy as jnp
from jax import lax
from jax.experimental import pallas as pl
from jax.experimental.pallas import tpu as pltpu
from jax.sharding import PartitionSpec as P

FREQ = 128
NLAG = 256
ROUNDS = 4
WSTEP = 4


def dft_table(sample_points, bin_count, first_bin):
    sample_moments = jnp.arange(sample_points, dtype=jnp.int32)
    spectral_bin_index = first_bin + 1 + jnp.arange(bin_count, dtype=jnp.int32)
    phase_turns = jnp.mod(sample_moments[:, None] * spectral_bin_index[None, :], sample_points)
    phases = phase_turns.astype(jnp.float32) * (2.0 * math.pi / sample_points)
    hanning_taper = 0.5 - 0.5 * jnp.cos(
        sample_moments.astype(jnp.float32) * (2.0 * math.pi / sample_points)
    )
    weight = (hanning_taper * math.sqrt(8.0 / (3.0 * sample_points)))[:, None]
    return jnp.concatenate([weight * jnp.cos(phases), -(weight * jnp.sin(phases))], axis=1).astype(
        jnp.bfloat16
    )


def lag_table(sample_points, bin_count, first_bin, lag_count, all_bins):
    spectral_bin_index = first_bin + 1 + jnp.arange(bin_count, dtype=jnp.int32)
    shifts = jnp.arange(lag_count, dtype=jnp.int32) - lag_count // 2
    phase_turns = jnp.mod(spectral_bin_index[:, None] * shifts[None, :], sample_points)
    phases = phase_turns.astype(jnp.float32) * (2.0 * math.pi / sample_points)
    lag_scale = 1.0 / math.sqrt(all_bins)
    return jnp.concatenate([jnp.cos(phases) * lag_scale, -(jnp.sin(phases) * lag_scale)], axis=0)


def whiten(spectra, validity):
    bin_count = spectra.shape[-1] // 2
    real_part = spectra[..., :bin_count]
    imag_part = spectra[..., bin_count:]
    band_power = jnp.mean(real_part * real_part + imag_part * imag_part, axis=1)
    amplitude = jnp.sqrt(jnp.maximum(band_power, 0.25))
    factor = validity[:, :, None] / amplitude
    factor = jnp.concatenate([factor, factor], axis=-1)
    return (spectra * factor[:, None]).astype(jnp.bfloat16)


def dft_kernel(rec_ref, table_ref, valid_ref, out_ref):
    station_count, window_count = valid_ref.shape
    comp_count = rec_ref.shape[0] // station_count
    nb = table_ref.shape[0] // 2
    table = table_ref[...]
    zero_row = jnp.zeros((1, window_count), jnp.float32)
    for s in range(station_count):
        parts = []
        for c in range(comp_count):
            z = lax.dot_general(
                table,
                rec_ref[c * station_count + s],
                (((1,), (1,)), ((), ())),
                preferred_element_type=jnp.float32,
            )
            parts.append((z[:nb], z[nb:]))
        total = parts[0][0] * parts[0][0] + parts[0][1] * parts[0][1]
        for c in range(1, comp_count):
            total = total + (parts[c][0] * parts[c][0] + parts[c][1] * parts[c][1])
        band_power = total / float(comp_count)
        amplitude = jnp.sqrt(jnp.maximum(band_power, 0.25))
        valid_row = valid_ref[pl.ds(s, 1), :]
        factor = valid_row / amplitude
        for c in range(comp_count):
            x = c * station_count + s
            out_ref[x, pl.ds(0, 1), pl.ds(0, window_count)] = valid_row if c == 0 else zero_row
            out_ref[x, pl.ds(0, 1), pl.ds(window_count, window_count)] = zero_row
            out_ref[x, pl.ds(1, nb), pl.ds(0, window_count)] = parts[c][0] * factor
            out_ref[x, pl.ds(1, nb), pl.ds(window_count, window_count)] = parts[c][1] * factor


def dft_whiten(rec_t, table_t, valid_t):
    rows, window_count, sample_points = rec_t.shape
    nb = table_t.shape[0] // 2
    return pl.pallas_call(
        dft_kernel,
        out_shape=jax.ShapeDtypeStruct((rows, 1 + nb, 2 * window_count), jnp.float32),
        cost_estimate=pl.CostEstimate(
            flops=2 * rows * window_count * sample_points * 2 * nb,
            transcendentals=rows * nb * window_count,
            bytes_accessed=2 * rec_t.size + 2 * table_t.size + 4 * rows * (nb + 1) * 2 * window_count,
        ),
    )(rec_t, table_t, valid_t)


def exchange(prod, station_count, bands, band_index):
    group = lax.axis_size("win") * bands
    per_dev = station_count // group
    me = lax.axis_index("win") * bands + band_index
    by_offset = [None] * bands
    for shift in range(group):
        dest = (me + shift) % group
        chunk = lax.dynamic_slice_in_dim(prod, dest * per_dev, per_dev, 2)
        if shift:
            perm = [(k, (k + shift) % group) for k in range(group)]
            chunk = lax.ppermute(chunk, ("win", "band"), perm)
        q = shift % bands
        by_offset[q] = chunk if by_offset[q] is None else by_offset[q] + chunk
    ordered = []
    for bb in range(bands):
        pick = by_offset[0]
        for q in range(1, bands):
            pick = jnp.where((band_index - q) % bands == bb, by_offset[q], pick)
        ordered.append(pick)
    return jnp.stack(ordered, axis=0), by_offset[0]


def body(records, valid_mask, round_keys):
    window_count, comp_count, station_count, sample_points = records.shape
    bands = lax.axis_size("band")
    band_index = lax.axis_index("band")
    pair_index = lax.axis_index("pair")
    nb = FREQ // bands
    rounds = round_keys.shape[0]
    xs = comp_count * station_count
    lanes = 2 * window_count
    slots = nb + 1

    dft_rows = dft_table(sample_points, nb, band_index * nb)
    rec_t = records.reshape(window_count, xs, sample_points).transpose(1, 0, 2)
    validity = valid_mask.astype(jnp.float32)
    spec = dft_whiten(rec_t, dft_rows.T, validity.T).astype(jnp.bfloat16)

    gathered = lax.all_gather(spec.reshape(xs * slots, lanes), "pair", axis=0, tiled=False)
    partner_list = jnp.bitwise_xor(pair_index, round_keys)
    other = jnp.take(gathered, partner_list, axis=0, mode="clip").reshape(rounds, xs, slots, lanes)
    rhs = other.transpose(2, 0, 1, 3).reshape(slots, rounds * xs, lanes)

    half = lax.broadcasted_iota(jnp.int32, (lanes,), 0) < window_count
    turned = jnp.roll(spec, window_count, axis=-1) * jnp.where(half, 1.0, -1.0).astype(jnp.bfloat16)
    lhs = jnp.stack([spec, turned], axis=0).transpose(2, 0, 1, 3).reshape(slots, 2 * xs, lanes)
    prod = jnp.einsum("fxk,fyk->fxy", lhs, rhs, preferred_element_type=jnp.float32)
    prod = prod.reshape(slots, 2 * comp_count, station_count, rounds * xs)

    stacked, same = exchange(prod, station_count, bands, band_index)
    per_dev = stacked.shape[3]
    totals = same[0, 0].reshape(per_dev, rounds, comp_count, station_count)[:, :, 0, :]
    stacked = stacked[:, 1:].reshape(
        bands, nb, 2, comp_count, per_dev, rounds, comp_count, station_count
    )

    full_lag = lag_table(sample_points, FREQ, 0, NLAG, FREQ)
    full_lag = full_lag.reshape(2, bands, nb, NLAG).transpose(1, 0, 2, 3)
    lagged = jnp.einsum(
        "gfuairbj,gufl->riabjl",
        stacked,
        full_lag,
        precision=lax.Precision.HIGHEST,
        preferred_element_type=jnp.float32,
    )
    divisor = jnp.maximum(totals, 1.0).transpose(1, 0, 2)[:, :, None, None, :, None]
    lagged = lagged / divisor
    return lagged.reshape(rounds, per_dev, comp_count, comp_count * station_count, NLAG)


def solution(mesh):
    placed = (P(("hours", "win"), None, "pair", None), P(("hours", "win"), "pair"), P())
    return jax.shard_map(
        body,
        mesh=mesh,
        in_specs=placed,
        out_specs=P(None, ("hours", "pair", "win", "band"), None, None, None),
        check_vma=False,
    )
```

time: 105 us -> 99.7 us (0.950)
  waiting for transfers between devices: 46.9 us -> 52.9 us
  other arithmetic: 11.4 us -> 5.55 us
  local copies, waits for them, and re-layouts: 22.9 us -> 18.1 us
    gather x1 -> x2, local copies, waits for them, and re-layouts: 2.26 us -> 8.07 us  [body(): jnp.take(gathered, partner_list, axis=0, mode='clip')]
    ppermute x3, waiting for transfers between devices: 8.76 us -> 13.9 us  [exchange(): chunk = lax.ppermute(chunk, ('win', 'band'), perm)]
    dynamic_slice x4 -> x1, local copies, waits for them, and re-layouts: 5.14 us -> 0.55 us  [exchange(): chunk = lax.dynamic_slice_in_dim(prod, dest * per_dev, per_dev, 2)]
    reshape x2 -> x0, local copies, waits for them, and re-layouts: 2.09 us -> none  [the longest x1 1.99 us: body(): prod = prod.reshape(nb, comp_count, station_count, 2 * rounds * xs)]
    concatenate x1 -> x0, other arithmetic: 1.93 us -> none  [body(): ext = jnp.concatenate([prod, slab], axis=0)]
    concatenate x1, local copies, waits for them, and re-layouts: 2.03 us -> 0.19 us  [body(): jnp.roll(spec, window_count, axis=-1)]
    unnamed x15 -> x10, local copies, waits for them, and re-layouts: 4.41 us -> 4.39 us
  transfers between devices with their start and end apart: 4 -> 4, of which waited for: 3 -> 4; matrix products, arithmetic and copies ran while one was open for 8% -> 4% of each run, Pallas kernels for 0% -> 0%
where the time goes in v9:
time: 99.7 us; the launch traced here: 99.3 us
  waiting for transfers between devices  52.9 us (53%)
  local copies, waits for them, and re-layouts  18.1 us (18%)
  between operations  13.7 us (14%)
  other arithmetic  5.55 us (6%)
  Pallas kernels  3.47 us (3%)
  starting transfers between devices  3.27 us (3%)
  matrix products  2.31 us (2%)
    all_gather x1, waiting for transfers between devices, body(): lax.all_gather(spec.reshape(xs * slots, lanes), 'pair', axis=0, tiled=False)  39 us
    ppermute x3, waiting for transfers between devices, exchange(): chunk = lax.ppermute(chunk, ('win', 'band'), perm)  13.9 us
    gather x2, local copies, waits for them, and re-layouts, body(): jnp.take(gathered, partner_list, axis=0, mode='clip')  8.07 us
    unnamed x10, local copies, waits for them, and re-layouts  4.39 us
    pallas_call x1, Pallas kernels, dft_whiten(): pl.pallas_call(dft_kernel, out_shape=jax.ShapeDtypeStruct((rows, 1 + nb,...  3.47 us
    ppermute x3, starting transfers between devices, exchange(): chunk = lax.ppermute(chunk, ('win', 'band'), perm)  3.27 us
    ppermute x3, local copies, waits for them, and re-layouts, exchange(): chunk = lax.ppermute(chunk, ('win', 'band'), perm)  2.69 us
  transfers between devices with their start and end apart: 4, of which 4 were waited for; matrix products, arithmetic and copies ran while one was open for 4% of the time, Pallas kernels for 0%

profile of v9, /device:TPU:0, one launch (start us, length us, event | category | flops | bytes accessed | tf_op | source)
XLA Modules:
  0.0 99.3 jit_solution(4578969399962825046)
XLA Ops:
  6.5 0.0 copy-start.2
  6.5 0.0 all-gather.2.cloned.1.call-start
  6.6 3.1 %copy.30 = bf16[64,3,8,512]{3,0,2,1:T(8,128)(2,1)} copy(bf16[64,3,8,512]{3,2,1,0:T(8,128)(2,1)} %param.3) | data formatting | bytes 3145728 | tf_op args[0]
  9.7 0.0 copy-done.2
  9.7 0.6 convert_bitcast_fusion.valid_ref
  10.3 0.6 multiply_convert_fusion
  10.9 0.7 maximum_bitcast_fusion.table_ref
  11.6 3.5 %shard_map.37 = f32[24,65,128]{2,1,0:T(8,128)} custom-call(bf16[24,64,512]{2,1,0:T(8,128)(2,1)} %bitcast.59, bf16[128,512]{1,0:T(8,128)(2,1)} %maximum_bitcast_fusion.table_ref, f32[8,64]{1,0:T(8,128)} %convert_bitcast_fusion.valid_ref), custom_call_target="tpu_custom_call" | custom-call | flops 201326592 | bytes 2502656 | tf_op jit(solution)/shard_map/pallas_call | solution.py:84
  15.1 0.0 copy-start.3
  15.1 1.2 %convert_element_type.35 = bf16[24,65,128]{2,1,0:T(8,128)(2,1)S(1)} convert(f32[24,65,128]{2,1,0:T(8,128)} %shard_map.37) | non-fusion elementwise | flops 199680 | bytes 1198080 | tf_op jit(solution)/shard_map/convert_element_type | solution.py:131
  16.3 0.9 all_gather_reshape.3
  17.2 0.0 all-gather.2.cloned.1.call-update
  17.2 0.0 copy-start
  17.3 0.0 copy-done.3
  17.4 0.2 slice_bitcast_fusion.1
  17.6 0.3 maximum_multiply_fusion
  17.8 0.6 copy-done
  18.4 0.1 convert_bitcast_fusion.1
  18.5 0.1 pad_maximum_fusion.1
  18.6 39.0 %all-gather.2.cloned.1.call-done = bf16[4,1560,128]{2,1,0:T(8,128)(2,1)} async-done(((bf16[1,1560,128]{2,1,0:T(8,128)(2,1)}), bf16[4,1560,128]{2,1,0:T(8,128)(2,1)}) %all-gather.2.cloned.1.call-update) | async-done | bytes 1597456 | tf_op jit(solution)/shard_map/all_gather | solution.py:133
  57.5 2.3 %gather_fusion = bf16[4,1560,128]{2,1,0:T(8,128)(2,1)S(1)} fusion(bf16[4,1560,128]{2,1,0:T(8,128)(2,1)} %all-gather.2.cloned.1.call-done, s32[1024]{0:T(1024)S(1)} %pad_clamp_fusion), kind=kCustom, calls=%fused_computation | custom fusion | bytes 3194896 | tf_op jit(solution)/shard_map/jit(_take)/gather | solution.py:135
  59.8 5.8 %copy.31 = bf16[4,1560,128]{2,0,1:T(4,128)(2,1)S(1)} copy(bf16[4,1560,128]{2,1,0:T(8,128)(2,1)S(1)} %gather_fusion) | data formatting | bytes 3194880 | tf_op jit(solution)/shard_map/jit(_take)/gather | solution.py:135
  65.6 0.3 copy.32
  65.9 1.2 %convolution_bitcast_fusion = f32[65,6,8,96]{3,2,1,0:T(8,128)S(1)} fusion(bf16[65,96,128]{2,1,0:T(8,128)(2,1)S(1)} %bitcast.57, bf16[65,48,128]{2,0,1:T(8,128)(2,1)S(1)} %bitcast.60), kind=kOutput, calls=%fused_computation.1 | convolution fusion | flops 76677120 | bytes 3594240 | tf_op jit(solution)/shard_map/fxk,fyk->fxy/dot_general | solution.py:141
  67.1 0.6 constant_dynamic-slice_fusion
  67.6 0.1 collective-permute-start
  67.7 1.7 %collective-permute-start.1 = (f32[65,6,2,96]{3,2,1,0:T(2,128)S(1)}, f32[65,6,2,96]{3,2,1,0:T(2,128)S(1)}, u32[]{:S(2)}, u32[]{:S(2)}) collective-permute-start(f32[65,6,2,96]{3,2,1,0:T(2,128)S(1)} %get-tuple-element.9), channel_id=1, source_target_pairs={{0,3},{1,0},{2,1},{3,2},{4,7},{5,4},{6,5},{7,6},{8,11},{9,8},{10,9... | collective-permute-start | bytes 898568 | tf_op jit(solution)/shard_map/ppermute | solution.py:105
  69.4 1.5 %collective-permute-start.2 = (f32[65,6,2,96]{3,2,1,0:T(2,128)S(1)}, f32[65,6,2,96]{3,2,1,0:T(2,128)}, u32[]{:S(2)}, u32[]{:S(2)}) collective-permute-start(f32[65,6,2,96]{3,2,1,0:T(2,128)S(1)} %get-tuple-element.7), channel_id=1, source_target_pairs={{0,2},{1,3},{2,0},{3,1},{4,6},{5,7},{6,4},{7,5},{8,10},{9,11},{10,... | collective-permute-start | bytes 898568 | tf_op jit(solution)/shard_map/ppermute | solution.py:105
  70.9 0.6 cosine_multiply_fusion
  71.5 0.7 pad_maximum_fusion.2
  72.2 0.2 copy.42
  72.5 5.1 %collective-permute-done = f32[65,6,2,96]{3,2,1,0:T(2,128)} collective-permute-done((f32[65,6,2,96]{3,2,1,0:T(2,128)S(1)}, f32[65,6,2,96]{3,2,1,0:T(2,128)}, u32[]{:S(2)}, u32[]{:S(2)}) %collective-permute-start) | collective-permute-done | bytes 299552 | tf_op jit(solution)/shard_map/ppermute | solution.py:105
  77.6 1.2 %copy.34 = f32[65,6,2,96]{0,3,2,1:T(8,128)S(1)} copy(f32[65,6,2,96]{3,2,1,0:T(2,128)} %collective-permute-done) | data formatting | bytes 599040 | tf_op jit(solution)/shard_map/ppermute | solution.py:105
  78.8 0.3 collective-permute-done.1
  79.1 0.2 copy.35
  79.3 8.6 %collective-permute-done.2 = f32[65,6,2,96]{3,2,1,0:T(2,128)} collective-permute-done((f32[65,6,2,96]{3,2,1,0:T(2,128)S(1)}, f32[65,6,2,96]{3,2,1,0:T(2,128)}, u32[]{:S(2)}, u32[]{:S(2)}) %collective-permute-start.2) | collective-permute-done | bytes 299552 | tf_op jit(solution)/shard_map/ppermute | solution.py:105
  87.9 1.2 %copy.37 = f32[65,6,2,96]{0,3,2,1:T(8,128)S(1)} copy(f32[65,6,2,96]{3,2,1,0:T(2,128)} %collective-permute-done.2) | data formatting | bytes 599040 | tf_op jit(solution)/shard_map/ppermute | solution.py:105
  89.1 0.1 select_bitcast_fusion.1
  89.3 0.1 slice_reduce_fusion
  89.4 0.1 select_bitcast_fusion
  89.5 0.0 copy-start.1
  89.5 0.1 reshape_squeeze.3
  89.6 0.4 pad_maximum_fusion
  90.0 0.5 copy-done.1
  90.5 1.1 %fusion.1 = f32[4,2,3,24,256]{4,3,0,1,2:T(8,128)S(1)} fusion(f32[2,64,2,3,2,4,3,8]{1,7,6,5,4,3,2,0:T(8,128)S(1)} %bitcast.61, f32[4,2,8]{2,0,1:T(4,128)S(1)} %bitcast.63, f32[2,2,64,256]{3,2,1,0:T(8,128)S(1)} %bitcast.62), kind=kOutput, calls=%fused_computation.4 | convolution fusion | flops 453132288 | bytes 1442048 | tf_op jit(solution)/shard_map/gfuairbj,gufl->riabjl/dot_general | solution.py:153
  91.6 0.9 copy.39
  (8 shorter events, 0.1 us)
Async XLA Ops:
  6.5 3.2 %copy-start.2 = (s32[64,8]{0,1:T(8,128)S(1)}, s32[64,8]{0,1:T(8,128)}, u32[]{:S(2)}) copy-start(s32[64,8]{0,1:T(8,128)} %param.4) | copy-start | bytes 6148
  6.5 51.0 %all-gather.2.cloned.1.call-start = ((), (), s32[]{:S(2)}) async-start(), calls=%async_computation | async-start | bytes 1996800 | tf_op jit(solution)/shard_map/all_gather | solution.py:133
  15.1 2.3 %copy-start.3 = (s32[4]{0:T(128)S(1)}, s32[4]{0:T(128)}, u32[]{:S(2)}) copy-start(s32[4]{0:T(128)} %param.5) | copy-start | bytes 52
  17.2 1.2 %copy-start = (f32[24,65,128]{2,1,0:T(8,128)S(1)}, f32[24,65,128]{2,1,0:T(8,128)}, u32[]{:S(2)}) copy-start(f32[24,65,128]{2,1,0:T(8,128)} %shard_map.37) | copy-start | bytes 2396164
  67.6 9.9 %collective-permute-start = (f32[65,6,2,96]{3,2,1,0:T(2,128)S(1)}, f32[65,6,2,96]{3,2,1,0:T(2,128)}, u32[]{:S(2)}, u32[]{:S(2)}) collective-permute-start(f32[65,6,2,96]{3,2,1,0:T(2,128)S(1)} %get-tuple-element.10), channel_id=1, source_target_pairs={{0,1},{1,2},{2,3},{3,0},{4,5},{5,6},{6,7},{7,4},{8,9},{9,10},{10,1... | collective-permute-start | bytes 898568 | tf_op jit(solution)/shard_map/ppermute | solution.py:105
  67.7 11.4 %collective-permute-start.1 = (f32[65,6,2,96]{3,2,1,0:T(2,128)S(1)}, f32[65,6,2,96]{3,2,1,0:T(2,128)S(1)}, u32[]{:S(2)}, u32[]{:S(2)}) collective-permute-start(f32[65,6,2,96]{3,2,1,0:T(2,128)S(1)} %get-tuple-element.9), channel_id=1, source_target_pairs={{0,3},{1,0},{2,1},{3,2},{4,7},{5,4},{6,5},{7,6},{8,11},{9,8},{10,9... | collective-permute-start | bytes 898568 | tf_op jit(solution)/shard_map/ppermute | solution.py:105
  69.4 18.5 %collective-permute-start.2 = (f32[65,6,2,96]{3,2,1,0:T(2,128)S(1)}, f32[65,6,2,96]{3,2,1,0:T(2,128)}, u32[]{:S(2)}, u32[]{:S(2)}) collective-permute-start(f32[65,6,2,96]{3,2,1,0:T(2,128)S(1)} %get-tuple-element.7), channel_id=1, source_target_pairs={{0,2},{1,3},{2,0},{3,1},{4,6},{5,7},{6,4},{7,5},{8,10},{9,11},{10,... | collective-permute-start | bytes 898568 | tf_op jit(solution)/shard_map/ppermute | solution.py:105
  89.5 1.0 copy-start.1
Sparse Core Ops, SparseCore 0:
  17.3 40.1 all-gather.1

commit v10 on v9

--- a/solution.py
+++ b/solution.py
@@ -102,7 +102,8 @@
         chunk = lax.dynamic_slice_in_dim(prod, dest * per_dev, per_dev, 2)
         if shift:
             perm = [(k, (k + shift) % group) for k in range(group)]
-            chunk = lax.ppermute(chunk, ("win", "band"), perm)
+            chunk = lax.ppermute(chunk.astype(jnp.bfloat16), ("win", "band"), perm)
+            chunk = chunk.astype(jnp.float32)
         q = shift % bands
         by_offset[q] = chunk if by_offset[q] is None else by_offset[q] + chunk
     ordered = []

time: 99.7 us -> 95.1 us (0.954)
  waiting for transfers between devices: 52.9 us -> 47.9 us
    ppermute x3, waiting for transfers between devices: 13.9 us -> 9.54 us  [exchange(): chunk = lax.ppermute(chunk.astype(jnp.bfloat16), ('win', 'band'), perm)]
    ppermute x3 -> x0, local copies, waits for them, and re-layouts: 2.69 us -> none  [exchange(): chunk = lax.ppermute(chunk, ('win', 'band'), perm)]
    unnamed x10 -> x13, local copies, waits for them, and re-layouts: 4.39 us -> 6.58 us
where the time goes in v10:
time: 95.1 us; the launch traced here: 94.8 us
  waiting for transfers between devices  47.9 us (50%)
  local copies, waits for them, and re-layouts  17.7 us (19%)
  between operations  13.7 us (14%)
  other arithmetic  6.52 us (7%)
  Pallas kernels  3.47 us (4%)
  starting transfers between devices  3.27 us (3%)
  matrix products  2.31 us (2%)
    all_gather x1, waiting for transfers between devices, body(): lax.all_gather(spec.reshape(xs * slots, lanes), 'pair', axis=0, tiled=False)  38.4 us
    ppermute x3, waiting for transfers between devices, exchange(): chunk = lax.ppermute(chunk.astype(jnp.bfloat16), ('win', 'band'), perm)  9.54 us
    gather x2, local copies, waits for them, and re-layouts, body(): jnp.take(gathered, partner_list, axis=0, mode='clip')  8.07 us
    unnamed x13, local copies, waits for them, and re-layouts  6.58 us
    pallas_call x1, Pallas kernels, dft_whiten(): pl.pallas_call(dft_kernel, out_shape=jax.ShapeDtypeStruct((rows, 1 + nb,...  3.47 us
    ppermute x3, starting transfers between devices, exchange(): chunk = lax.ppermute(chunk.astype(jnp.bfloat16), ('win', 'band'), perm)  3.27 us
  transfers between devices with their start and end apart: 4, of which 4 were waited for; matrix products, arithmetic and copies ran while one was open for 4% of the time, Pallas kernels for 0%

profile of v10, /device:TPU:0, one launch (start us, length us, event | category | flops | bytes accessed | tf_op | source)
XLA Modules:
  0.0 94.8 jit_solution(13325561948701083177)
XLA Ops:
  6.5 0.0 copy-start.2
  6.5 0.0 all-gather.2.cloned.1.call-start
  6.6 3.1 %copy.30 = bf16[64,3,8,512]{3,0,2,1:T(8,128)(2,1)} copy(bf16[64,3,8,512]{3,2,1,0:T(8,128)(2,1)} %param.3) | data formatting | bytes 3145728 | tf_op args[0]
  9.7 0.0 copy-done.2
  9.7 0.6 convert_bitcast_fusion.valid_ref
  10.3 0.6 multiply_convert_fusion
  10.9 0.7 maximum_bitcast_fusion.table_ref
  11.6 3.5 %shard_map.37 = f32[24,65,128]{2,1,0:T(8,128)} custom-call(bf16[24,64,512]{2,1,0:T(8,128)(2,1)} %bitcast.59, bf16[128,512]{1,0:T(8,128)(2,1)} %maximum_bitcast_fusion.table_ref, f32[8,64]{1,0:T(8,128)} %convert_bitcast_fusion.valid_ref), custom_call_target="tpu_custom_call" | custom-call | flops 201326592 | bytes 2502656 | tf_op jit(solution)/shard_map/pallas_call | solution.py:84
  15.1 0.0 copy-start.3
  15.1 1.2 %convert_element_type.53 = bf16[24,65,128]{2,1,0:T(8,128)(2,1)S(1)} convert(f32[24,65,128]{2,1,0:T(8,128)} %shard_map.37) | non-fusion elementwise | flops 199680 | bytes 1198080 | tf_op jit(solution)/shard_map/convert_element_type | solution.py:132
  16.3 0.9 all_gather_reshape.3
  17.2 0.0 all-gather.2.cloned.1.call-update
  17.2 0.0 copy-start
  17.3 0.0 copy-done.3
  17.3 0.2 slice_bitcast_fusion.1
  17.5 0.3 maximum_multiply_fusion
  17.8 0.6 copy-done
  18.4 0.1 convert_bitcast_fusion.1
  18.4 0.1 pad_maximum_fusion.1
  18.5 0.6 cosine_multiply_fusion
  19.1 38.4 %all-gather.2.cloned.1.call-done = bf16[4,1560,128]{2,1,0:T(8,128)(2,1)} async-done(((bf16[1,1560,128]{2,1,0:T(8,128)(2,1)}), bf16[4,1560,128]{2,1,0:T(8,128)(2,1)}) %all-gather.2.cloned.1.call-update) | async-done | bytes 1597456 | tf_op jit(solution)/shard_map/all_gather | solution.py:134
  57.5 2.3 %gather_fusion = bf16[4,1560,128]{2,1,0:T(8,128)(2,1)S(1)} fusion(bf16[4,1560,128]{2,1,0:T(8,128)(2,1)} %all-gather.2.cloned.1.call-done, s32[1024]{0:T(1024)S(1)} %pad_clamp_fusion), kind=kCustom, calls=%fused_computation | custom fusion | bytes 3194896 | tf_op jit(solution)/shard_map/jit(_take)/gather | solution.py:136
  59.8 5.8 %copy.31 = bf16[4,1560,128]{2,0,1:T(4,128)(2,1)S(1)} copy(bf16[4,1560,128]{2,1,0:T(8,128)(2,1)S(1)} %gather_fusion) | data formatting | bytes 3194880 | tf_op jit(solution)/shard_map/jit(_take)/gather | solution.py:136
  65.6 0.3 copy.32
  65.9 1.2 %convolution_bitcast_fusion = f32[65,6,8,96]{3,2,1,0:T(8,128)S(1)} fusion(bf16[65,96,128]{2,1,0:T(8,128)(2,1)S(1)} %bitcast.57, bf16[65,48,128]{2,0,1:T(8,128)(2,1)S(1)} %bitcast.60), kind=kOutput, calls=%fused_computation.1 | convolution fusion | flops 76677120 | bytes 3594240 | tf_op jit(solution)/shard_map/fxk,fyk->fxy/dot_general | solution.py:142
  67.1 0.5 constant_dynamic-slice_fusion
  67.6 0.2 copy.42
  67.8 0.1 collective-permute-start
  67.9 0.9 copy.43
  68.8 1.7 %collective-permute-start.1 = (bf16[65,6,2,96]{0,3,2,1:T(8,128)(2,1)}, bf16[65,6,2,96]{0,3,2,1:T(8,128)(2,1)S(1)}, u32[]{:S(2)}, u32[]{:S(2)}) collective-permute-start(bf16[65,6,2,96]{0,3,2,1:T(8,128)(2,1)} %copy.43), channel_id=1, source_target_pairs={{0,3},{1,0},{2,1},{3,2},{4,7},{5,4},{6,5},{7,6},{8,11},{9,8},{10,9... | collective-permute-start | bytes 449288 | tf_op jit(solution)/shard_map/ppermute | solution.py:105
  70.5 0.9 copy.45
  71.4 1.5 %collective-permute-start.2 = (bf16[65,6,2,96]{0,3,2,1:T(8,128)(2,1)}, bf16[65,6,2,96]{0,3,2,1:T(8,128)(2,1)}, u32[]{:S(2)}, u32[]{:S(2)}) collective-permute-start(bf16[65,6,2,96]{0,3,2,1:T(8,128)(2,1)} %copy.45), channel_id=1, source_target_pairs={{0,2},{1,3},{2,0},{3,1},{4,6},{5,7},{6,4},{7,5},{8,10},{9,11},{10,... | collective-permute-start | bytes 449288 | tf_op jit(solution)/shard_map/ppermute | solution.py:105
  72.9 0.7 pad_maximum_fusion.2
  73.6 0.1 constant_dynamic-slice_fusion.1
  73.8 0.2 copy.44
  74.0 0.2 collective-permute-done
  74.2 4.0 %collective-permute-done.1 = bf16[65,6,2,96]{0,3,2,1:T(8,128)(2,1)S(1)} collective-permute-done((bf16[65,6,2,96]{0,3,2,1:T(8,128)(2,1)}, bf16[65,6,2,96]{0,3,2,1:T(8,128)(2,1)S(1)}, u32[]{:S(2)}, u32[]{:S(2)}) %collective-permute-start.1) | collective-permute-done | bytes 149792 | tf_op jit(solution)/shard_map/ppermute | solution.py:105
  78.2 5.4 %collective-permute-done.2 = bf16[65,6,2,96]{0,3,2,1:T(8,128)(2,1)} collective-permute-done((bf16[65,6,2,96]{0,3,2,1:T(8,128)(2,1)}, bf16[65,6,2,96]{0,3,2,1:T(8,128)(2,1)}, u32[]{:S(2)}, u32[]{:S(2)}) %collective-permute-start.2) | collective-permute-done | bytes 149792 | tf_op jit(solution)/shard_map/ppermute | solution.py:105
  83.6 1.1 %select_bitcast_fusion.1 = (f32[1,65,6,2,96]{1,4,3,2,0:T(8,128)S(1)}, f32[65,6,2,96]{0,3,2,1:T(8,128)S(1)}) fusion(bf16[65,6,2,96]{0,3,2,1:T(8,128)(2,1)S(1)} %collective-permute-done.1, bf16[65,6,2,96]{0,3,2,1:T(8,128)(2,1)S(1)} %collective-permute-done, pred[]{:T(512)S(6)} %eq.17, f32[65,6,2,96]{0,3,2,1:T(8,128)S(1)} %copy.44, ...), kind=kLoop, calls=%fused_computation.9 | loop fusion | flops 449280 | bytes 1347841 | tf_op jit(solution)/shard_map/stack | solution.py:115
  84.7 0.1 slice_reduce_fusion
  84.8 0.1 reshape_squeeze.3
  84.9 0.1 select_bitcast_fusion
  85.0 0.0 copy-start.1
  85.0 0.4 pad_maximum_fusion
  85.4 0.6 copy-done.1
  86.0 1.1 %fusion.1 = f32[4,2,3,24,256]{4,3,0,1,2:T(8,128)S(1)} fusion(f32[2,64,2,3,2,4,3,8]{1,7,6,5,4,3,2,0:T(8,128)S(1)} %bitcast.61, f32[4,2,8]{2,0,1:T(4,128)S(1)} %bitcast.63, f32[2,2,64,256]{3,2,1,0:T(8,128)S(1)} %bitcast.62), kind=kOutput, calls=%fused_computation.4 | convolution fusion | flops 453132288 | bytes 1442048 | tf_op jit(solution)/shard_map/gfuairbj,gufl->riabjl/dot_general | solution.py:154
  87.1 0.9 copy.39
  (8 shorter events, 0.1 us)
Async XLA Ops:
  6.5 3.2 %copy-start.2 = (s32[64,8]{0,1:T(8,128)S(1)}, s32[64,8]{0,1:T(8,128)}, u32[]{:S(2)}) copy-start(s32[64,8]{0,1:T(8,128)} %param.4) | copy-start | bytes 6148
  6.5 51.0 %all-gather.2.cloned.1.call-start = ((), (), s32[]{:S(2)}) async-start(), calls=%async_computation | async-start | bytes 1996800 | tf_op jit(solution)/shard_map/all_gather | solution.py:134
  15.1 2.2 %copy-start.3 = (s32[4]{0:T(128)S(1)}, s32[4]{0:T(128)}, u32[]{:S(2)}) copy-start(s32[4]{0:T(128)} %param.5) | copy-start | bytes 52
  17.2 1.2 %copy-start = (f32[24,65,128]{2,1,0:T(8,128)S(1)}, f32[24,65,128]{2,1,0:T(8,128)}, u32[]{:S(2)}) copy-start(f32[24,65,128]{2,1,0:T(8,128)} %shard_map.37) | copy-start | bytes 2396164
  67.8 6.5 %collective-permute-start = (bf16[65,6,2,96]{0,3,2,1:T(8,128)(2,1)S(1)}, bf16[65,6,2,96]{0,3,2,1:T(8,128)(2,1)S(1)}, u32[]{:S(2)}, u32[]{:S(2)}) collective-permute-start(bf16[65,6,2,96]{0,3,2,1:T(8,128)(2,1)S(1)} %copy.42), channel_id=1, source_target_pairs={{0,1},{1,2},{2,3},{3,0},{4,5},{5,6},{6,7},{7,4},{8,9},{9,10},{10,1... | collective-permute-start | bytes 449288 | tf_op jit(solution)/shard_map/ppermute | solution.py:105
  68.8 9.4 %collective-permute-start.1 = (bf16[65,6,2,96]{0,3,2,1:T(8,128)(2,1)}, bf16[65,6,2,96]{0,3,2,1:T(8,128)(2,1)S(1)}, u32[]{:S(2)}, u32[]{:S(2)}) collective-permute-start(bf16[65,6,2,96]{0,3,2,1:T(8,128)(2,1)} %copy.43), channel_id=1, source_target_pairs={{0,3},{1,0},{2,1},{3,2},{4,7},{5,4},{6,5},{7,6},{8,11},{9,8},{10,9... | collective-permute-start | bytes 449288 | tf_op jit(solution)/shard_map/ppermute | solution.py:105
  71.4 12.1 %collective-permute-start.2 = (bf16[65,6,2,96]{0,3,2,1:T(8,128)(2,1)}, bf16[65,6,2,96]{0,3,2,1:T(8,128)(2,1)}, u32[]{:S(2)}, u32[]{:S(2)}) collective-permute-start(bf16[65,6,2,96]{0,3,2,1:T(8,128)(2,1)} %copy.45), channel_id=1, source_target_pairs={{0,2},{1,3},{2,0},{3,1},{4,6},{5,7},{6,4},{7,5},{8,10},{9,11},{10,... | collective-permute-start | bytes 449288 | tf_op jit(solution)/shard_map/ppermute | solution.py:105
  85.0 1.0 %copy-start.1 = (f32[256,256]{1,0:T(8,128)S(1)}, f32[256,256]{1,0:T(8,128)}, u32[]{:S(2)}) copy-start(f32[256,256]{1,0:T(8,128)} %pad_maximum_fusion.2) | copy-start | bytes 786436
Sparse Core Ops, SparseCore 0:
  17.3 40.1 all-gather.1

commit v11 on v10

--- a/solution.py
+++ b/solution.py
@@ -131,9 +131,18 @@
     validity = valid_mask.astype(jnp.float32)
     spec = dft_whiten(rec_t, dft_rows.T, validity.T).astype(jnp.bfloat16)
 
-    gathered = lax.all_gather(spec.reshape(xs * slots, lanes), "pair", axis=0, tiled=False)
-    partner_list = jnp.bitwise_xor(pair_index, round_keys)
-    other = jnp.take(gathered, partner_list, axis=0, mode="clip").reshape(rounds, xs, slots, lanes)
+    flat = spec.reshape(xs * slots, lanes)
+    blocks = lax.axis_size("pair")
+    if blocks <= 8 and blocks & (blocks - 1) == 0:
+        held = [flat]
+        for k in range(1, blocks):
+            held.append(lax.ppermute(flat, "pair", [(p, p ^ k) for p in range(blocks)]))
+        other = jnp.take(jnp.stack(held), round_keys, axis=0, mode="clip")
+    else:
+        gathered = lax.all_gather(flat, "pair", axis=0, tiled=False)
+        partner_list = jnp.bitwise_xor(pair_index, round_keys)
+        other = jnp.take(gathered, partner_list, axis=0, mode="clip")
+    other = other.reshape(rounds, xs, slots, lanes)
     rhs = other.transpose(2, 0, 1, 3).reshape(slots, rounds * xs, lanes)
 
     half = lax.broadcasted_iota(jnp.int32, (lanes,), 0) < window_count

time: 95.1 us -> 83.6 us (0.88)
  between operations: 13.7 us -> 0.28 us
  starting transfers between devices: 3.27 us -> 8.87 us
  waiting for transfers between devices: 47.9 us -> 42.9 us
  other arithmetic: 6.52 us -> 9.35 us
  local copies, waits for them, and re-layouts: 17.7 us -> 16 us
    all_gather x1 -> x0, waiting for transfers between devices: 38.4 us -> none  [body(): lax.all_gather(spec.reshape(xs * slots, lanes), 'pair', axis=0, tiled=False)]
    ppermute x0 -> x3, waiting for transfers between devices: none -> 31.3 us  [body(): held.append(lax.ppermute(flat, 'pair', [(p, p ^ k) for p in range(blocks)]))]
    ppermute x0 -> x3, starting transfers between devices: none -> 5.64 us  [body(): held.append(lax.ppermute(flat, 'pair', [(p, p ^ k) for p in range(blocks)]))]
    ppermute x3, waiting for transfers between devices: 9.54 us -> 11.6 us  [exchange(): chunk = lax.ppermute(chunk.astype(jnp.bfloat16), ('win', 'band'), perm)]
    gather x2, local copies, waits for them, and re-layouts: 8.07 us -> 6.66 us  [body(): other = jnp.take(jnp.stack(held), round_keys, axis=0, mode='clip')]
    another operation x1 -> x2, other arithmetic: 0.6 us -> 1.8 us  [the longest x1 1.2 us: body(): other = jnp.take(jnp.stack(held), round_keys, axis=0, mode='clip')]
  transfers between devices with their start and end apart: 4 -> 6, of which waited for: 4 -> 5; matrix products, arithmetic and copies ran while one was open for 4% -> 4% of each run, Pallas kernels for 0% -> 0%
where the time goes in v11:
time: 83.6 us; the launch traced here: 83.2 us
  waiting for transfers between devices  42.9 us (51%)
  local copies, waits for them, and re-layouts  16 us (19%)
  other arithmetic  9.35 us (11%)
  starting transfers between devices  8.87 us (11%)
  Pallas kernels  3.46 us (4%)
  matrix products  2.32 us (3%)
    ppermute x3, waiting for transfers between devices, body(): held.append(lax.ppermute(flat, 'pair', [(p, p ^ k) for p in range(blocks)]))  31.3 us
    ppermute x3, waiting for transfers between devices, exchange(): chunk = lax.ppermute(chunk.astype(jnp.bfloat16), ('win', 'band'), perm)  11.6 us
    gather x2, local copies, waits for them, and re-layouts, body(): other = jnp.take(jnp.stack(held), round_keys, axis=0, mode='clip')  6.66 us
    unnamed x13, local copies, waits for them, and re-layouts  6.2 us
    ppermute x3, starting transfers between devices, body(): held.append(lax.ppermute(flat, 'pair', [(p, p ^ k) for p in range(blocks)]))  5.64 us
    pallas_call x1, Pallas kernels, dft_whiten(): pl.pallas_call(dft_kernel, out_shape=jax.ShapeDtypeStruct((rows, 1 + nb,...  3.46 us
    ppermute x3, starting transfers between devices, exchange(): chunk = lax.ppermute(chunk.astype(jnp.bfloat16), ('win', 'band'), perm)  3.22 us
    transpose x2, other arithmetic, body(): spec = dft_whiten(rec_t, dft_rows.T, validity.T).astype(jnp.bfloat16)  1.94 us
  transfers between devices with their start and end apart: 6, of which 5 were waited for; matrix products, arithmetic and copies ran while one was open for 4% of the time, Pallas kernels for 0%

profile of v11, /device:TPU:0, one launch (start us, length us, event | category | flops | bytes accessed | tf_op | source)
XLA Modules:
  0.0 83.2 jit_solution(16376662140846783112)
XLA Ops:
  0.1 1.3 %convert_bitcast_fusion.valid_ref = f32[8,64]{1,0:T(8,128)} fusion(s32[64,8]{0,1:T(8,128)} %param.4), kind=kLoop, calls=%fused_computation.44 | loop fusion | flops 512 | bytes 4096 | tf_op jit(solution)/shard_map/transpose | solution.py:132
  1.3 3.1 %copy.19 = bf16[64,3,8,512]{3,0,2,1:T(8,128)(2,1)} copy(bf16[64,3,8,512]{3,2,1,0:T(8,128)(2,1)} %param.3) | data formatting | bytes 3145728 | tf_op args[0]
  4.4 0.6 multiply_convert_fusion
  5.0 0.7 maximum_bitcast_fusion.table_ref
  5.7 3.5 %shard_map.37 = f32[24,65,128]{2,1,0:T(8,128)} custom-call(bf16[24,64,512]{2,1,0:T(8,128)(2,1)} %bitcast.62, bf16[128,512]{1,0:T(8,128)(2,1)} %maximum_bitcast_fusion.table_ref, f32[8,64]{1,0:T(8,128)} %convert_bitcast_fusion.valid_ref), custom_call_target="tpu_custom_call" | custom-call | flops 201326592 | bytes 2502656 | tf_op jit(solution)/shard_map/pallas_call | solution.py:84
  9.2 0.0 copy-start
  9.2 1.3 %convert_element_type.53 = bf16[24,65,128]{2,1,0:T(8,128)(2,1)S(1)} convert(f32[24,65,128]{2,1,0:T(8,128)} %shard_map.37) | non-fusion elementwise | flops 199680 | bytes 1198080 | tf_op jit(solution)/shard_map/convert_element_type | solution.py:132
  10.5 0.9 %reshape.89 = bf16[1560,128]{1,0:T(8,128)(2,1)} reshape(bf16[24,65,128]{2,1,0:T(8,128)(2,1)S(1)} %convert_element_type.53) | data formatting | bytes 798720 | tf_op jit(solution)/shard_map/reshape | solution.py:134
  11.4 0.0 copy-start.3
  11.4 5.1 %collective-permute-start.2 = (bf16[1560,128]{1,0:T(8,128)(2,1)}, bf16[1560,128]{1,0:T(8,128)(2,1)S(1)}, u32[]{:S(2)}, u32[]{:S(2)}) collective-permute-start(bf16[1560,128]{1,0:T(8,128)(2,1)} %reshape.89), channel_id=1, source_target_pairs={{0,12},{4,8},{8,4},{12,0},{1,13},{5,9},{9,5},{13,1},{2,14},{6,10},... | collective-permute-start | bytes 1198088 | tf_op jit(solution)/shard_map/ppermute | solution.py:139
  16.4 0.0 collective-permute-start.1
  16.5 0.6 collective-permute-start
  17.0 0.0 copy-done
  17.0 0.1 convert_bitcast_fusion.1
  17.1 0.2 slice_bitcast_fusion.1
  17.3 0.0 copy-done.3
  17.3 0.3 maximum_multiply_fusion
  17.7 0.1 stack_reshape.3
  17.8 1.0 %pad_maximum_fusion.2 = bf16[2,24,65,128]{3,2,1,0:T(8,128)(2,1)} fusion(bf16[1,24,65,128]{3,2,1,0:T(8,128)(2,1)S(1)} %maximum_multiply_fusion, bf16[1,24,65,128]{3,2,1,0:T(8,128)(2,1)S(1)} %convert_bitcast_fusion.1), kind=kLoop, calls=%fused_computation.7 | loop fusion | flops 399360 | bytes 1597440 | tf_op jit(solution)/shard_map/stack | solution.py:150
  18.8 0.6 cosine_multiply_fusion
  19.4 7.5 %collective-permute-done.2 = bf16[1560,128]{1,0:T(8,128)(2,1)S(1)} collective-permute-done((bf16[1560,128]{1,0:T(8,128)(2,1)}, bf16[1560,128]{1,0:T(8,128)(2,1)S(1)}, u32[]{:S(2)}, u32[]{:S(2)}) %collective-permute-start.2) | collective-permute-done | bytes 399392 | tf_op jit(solution)/shard_map/ppermute | solution.py:139
  26.9 23.8 %collective-permute-done.1 = bf16[1560,128]{1,0:T(8,128)(2,1)S(1)} collective-permute-done((bf16[1560,128]{1,0:T(8,128)(2,1)}, bf16[1560,128]{1,0:T(8,128)(2,1)S(1)}, u32[]{:S(2)}, u32[]{:S(2)}) %collective-permute-start.1) | collective-permute-done | bytes 399392 | tf_op jit(solution)/shard_map/ppermute | solution.py:139
  50.7 0.0 collective-permute-done
  50.7 1.2 %pad_maximum_fusion = bf16[4,1560,128]{2,1,0:T(8,128)(2,1)S(1)} fusion(bf16[1,1560,128]{2,1,0:T(8,128)(2,1)S(1)} %bitcast.65, bf16[1,1560,128]{2,1,0:T(8,128)(2,1)S(1)} %bitcast.66, bf16[1,1560,128]{2,1,0:T(8,128)(2,1)} %bitcast.9, bf16[1,1560,128]{2,1,0:T(8,128)(2,1)S(1)} %stack_reshape.3), kind=kLoop, calls=%fused_computation.1 | loop fusion | flops 2396160 | bytes 3194880 | tf_op jit(solution)/shard_map/stack | solution.py:140
  51.9 0.9 %gather_fusion = bf16[4,1560,128]{2,1,0:T(8,128)(2,1)S(1)} fusion(bf16[4,1560,128]{2,1,0:T(8,128)(2,1)S(1)} %pad_maximum_fusion, s32[1024]{0:T(1024)S(1)} %pad_clamp_fusion), kind=kCustom, calls=%fused_computation | custom fusion | bytes 3194896 | tf_op jit(solution)/shard_map/jit(_take)/gather | solution.py:140
  52.8 5.8 %copy.20 = bf16[4,1560,128]{2,0,1:T(4,128)(2,1)S(1)} copy(bf16[4,1560,128]{2,1,0:T(8,128)(2,1)S(1)} %gather_fusion) | data formatting | bytes 3194880 | tf_op jit(solution)/shard_map/jit(_take)/gather | solution.py:140
  58.6 0.0 copy-start.1
  58.6 0.3 copy.21
  58.9 0.9 %copy-done.1 = bf16[2,24,65,128]{3,2,1,0:T(8,128)(2,1)S(1)} copy-done((bf16[2,24,65,128]{3,2,1,0:T(8,128)(2,1)S(1)}, bf16[2,24,65,128]{3,2,1,0:T(8,128)(2,1)}, u32[]{:S(2)}) %copy-start.1) | copy-done | bytes 798744
  59.8 1.2 %convolution_bitcast_fusion = f32[65,6,8,96]{3,2,1,0:T(8,128)S(1)} fusion(bf16[65,96,128]{2,1,0:T(8,128)(2,1)S(1)} %bitcast.60, bf16[65,48,128]{2,0,1:T(8,128)(2,1)S(1)} %bitcast.63), kind=kOutput, calls=%fused_computation.2 | convolution fusion | flops 76677120 | bytes 3594240 | tf_op jit(solution)/shard_map/fxk,fyk->fxy/dot_general | solution.py:151
  61.0 0.5 constant_dynamic-slice_fusion
  61.5 0.2 copy.34
  61.7 0.2 copy.32
  62.0 0.9 %copy.31 = bf16[65,6,2,96]{0,3,2,1:T(8,128)(2,1)} copy(bf16[65,6,2,96]{3,2,1,0:T(2,128)(2,1)S(1)} %get-tuple-element.9) | data formatting | bytes 299520
  62.9 0.0 collective-permute-start.3
  62.9 1.7 %collective-permute-start.4 = (bf16[65,6,2,96]{0,3,2,1:T(8,128)(2,1)S(1)}, bf16[65,6,2,96]{0,3,2,1:T(8,128)(2,1)S(1)}, u32[]{:S(2)}, u32[]{:S(2)}) collective-permute-start(bf16[65,6,2,96]{0,3,2,1:T(8,128)(2,1)S(1)} %copy.32), channel_id=1, source_target_pairs={{0,3},{1,0},{2,1},{3,2},{4,7},{5,4},{6,5},{7,6},{8,11},{9,8},{10,9... | collective-permute-start | bytes 449288 | tf_op jit(solution)/shard_map/ppermute | solution.py:105
  64.6 1.5 %collective-permute-start.5 = (bf16[65,6,2,96]{0,3,2,1:T(8,128)(2,1)S(1)}, bf16[65,6,2,96]{0,3,2,1:T(8,128)(2,1)}, u32[]{:S(2)}, u32[]{:S(2)}) collective-permute-start(bf16[65,6,2,96]{0,3,2,1:T(8,128)(2,1)S(1)} %copy.34), channel_id=1, source_target_pairs={{0,2},{1,3},{2,0},{3,1},{4,6},{5,7},{6,4},{7,5},{8,10},{9,11},{10,... | collective-permute-start | bytes 449288 | tf_op jit(solution)/shard_map/ppermute | solution.py:105
  66.1 0.7 pad_maximum_fusion.3
  66.8 0.1 constant_dynamic-slice_fusion.1
  67.0 0.2 copy.33
  67.2 3.6 %collective-permute-done.3 = bf16[65,6,2,96]{0,3,2,1:T(8,128)(2,1)S(1)} collective-permute-done((bf16[65,6,2,96]{0,3,2,1:T(8,128)(2,1)}, bf16[65,6,2,96]{0,3,2,1:T(8,128)(2,1)S(1)}, u32[]{:S(2)}, u32[]{:S(2)}) %collective-permute-start.3) | collective-permute-done | bytes 149792 | tf_op jit(solution)/shard_map/ppermute | solution.py:105
  70.8 1.2 %collective-permute-done.4 = bf16[65,6,2,96]{0,3,2,1:T(8,128)(2,1)S(1)} collective-permute-done((bf16[65,6,2,96]{0,3,2,1:T(8,128)(2,1)S(1)}, bf16[65,6,2,96]{0,3,2,1:T(8,128)(2,1)S(1)}, u32[]{:S(2)}, u32[]{:S(2)}) %collective-permute-start.4) | collective-permute-done | bytes 149792 | tf_op jit(solution)/shard_map/ppermute | solution.py:105
  72.0 6.8 %collective-permute-done.5 = bf16[65,6,2,96]{0,3,2,1:T(8,128)(2,1)} collective-permute-done((bf16[65,6,2,96]{0,3,2,1:T(8,128)(2,1)S(1)}, bf16[65,6,2,96]{0,3,2,1:T(8,128)(2,1)}, u32[]{:S(2)}, u32[]{:S(2)}) %collective-permute-start.5) | collective-permute-done | bytes 149792 | tf_op jit(solution)/shard_map/ppermute | solution.py:105
  78.8 1.1 %select_bitcast_fusion.1 = (f32[1,65,6,2,96]{1,4,3,2,0:T(8,128)S(1)}, f32[65,6,2,96]{0,3,2,1:T(8,128)S(1)}) fusion(bf16[65,6,2,96]{0,3,2,1:T(8,128)(2,1)S(1)} %collective-permute-done.4, bf16[65,6,2,96]{0,3,2,1:T(8,128)(2,1)S(1)} %collective-permute-done.3, pred[]{:T(512)S(6)} %eq.17, f32[65,6,2,96]{0,3,2,1:T(8,128)S(1)} %copy.33, ...), kind=kLoop, calls=%fused_computation.10 | loop fusion | flops 449280 | bytes 1347841 | tf_op jit(solution)/shard_map/stack | solution.py:115
  79.9 0.1 slice_reduce_fusion
  80.0 0.1 reshape_squeeze.3
  80.2 0.1 select_bitcast_fusion
  80.3 0.0 copy-start.2
  80.3 0.4 pad_maximum_fusion.1
  80.6 0.6 copy-done.2
  81.2 1.1 %fusion.1 = f32[4,2,3,24,256]{4,3,0,1,2:T(8,128)S(1)} fusion(f32[2,64,2,3,2,4,3,8]{1,7,6,5,4,3,2,0:T(8,128)S(1)} %bitcast.64, f32[4,2,8]{2,0,1:T(4,128)S(1)} %bitcast.68, f32[2,2,64,256]{3,2,1,0:T(8,128)S(1)} %bitcast.67), kind=kOutput, calls=%fused_computation.5 | convolution fusion | flops 453132288 | bytes 1442048 | tf_op jit(solution)/shard_map/gfuairbj,gufl->riabjl/dot_general | solution.py:163
  82.3 0.9 %copy.28 = f32[4,2,3,24,256]{4,3,2,1,0:T(8,128)} copy(f32[4,2,3,24,256]{4,3,0,1,2:T(8,128)S(1)} %fusion.1) | data formatting | bytes 1179648 | tf_op jit(solution)/shard_map/reshape | solution.py:172
  (7 shorter events, 0.1 us)
Async XLA Ops:
  9.2 7.8 %copy-start = (f32[24,65,128]{2,1,0:T(8,128)S(1)}, f32[24,65,128]{2,1,0:T(8,128)}, u32[]{:S(2)}) copy-start(f32[24,65,128]{2,1,0:T(8,128)} %shard_map.37) | copy-start | bytes 2396164
  11.4 5.9 %copy-start.3 = (s32[4]{0:T(128)S(1)}, s32[4]{0:T(128)}, u32[]{:S(2)}) copy-start(s32[4]{0:T(128)} %param.5) | copy-start | bytes 52
  11.4 15.5 %collective-permute-start.2 = (bf16[1560,128]{1,0:T(8,128)(2,1)}, bf16[1560,128]{1,0:T(8,128)(2,1)S(1)}, u32[]{:S(2)}, u32[]{:S(2)}) collective-permute-start(bf16[1560,128]{1,0:T(8,128)(2,1)} %reshape.89), channel_id=1, source_target_pairs={{0,12},{4,8},{8,4},{12,0},{1,13},{5,9},{9,5},{13,1},{2,14},{6,10},... | collective-permute-start | bytes 1198088 | tf_op jit(solution)/shard_map/ppermute | solution.py:139
  16.4 34.3 %collective-permute-start.1 = (bf16[1560,128]{1,0:T(8,128)(2,1)}, bf16[1560,128]{1,0:T(8,128)(2,1)S(1)}, u32[]{:S(2)}, u32[]{:S(2)}) collective-permute-start(bf16[1560,128]{1,0:T(8,128)(2,1)} %reshape.89), channel_id=1, source_target_pairs={{0,8},{4,12},{8,0},{12,4},{1,9},{5,13},{9,1},{13,5},{2,10},{6,14},... | collective-permute-start | bytes 1198088 | tf_op jit(solution)/shard_map/ppermute | solution.py:139
  16.5 34.3 %collective-permute-start = (bf16[1560,128]{1,0:T(8,128)(2,1)}, bf16[1560,128]{1,0:T(8,128)(2,1)}, u32[]{:S(2)}, u32[]{:S(2)}) collective-permute-start(bf16[1560,128]{1,0:T(8,128)(2,1)} %reshape.89), channel_id=1, source_target_pairs={{0,4},{4,0},{8,12},{12,8},{1,5},{5,1},{9,13},{13,9},{2,6},{6,2},{1... | collective-permute-start | bytes 1198088 | tf_op jit(solution)/shard_map/ppermute | solution.py:139
  58.6 1.2 %copy-start.1 = (bf16[2,24,65,128]{3,2,1,0:T(8,128)(2,1)S(1)}, bf16[2,24,65,128]{3,2,1,0:T(8,128)(2,1)}, u32[]{:S(2)}) copy-start(bf16[2,24,65,128]{3,2,1,0:T(8,128)(2,1)} %pad_maximum_fusion.2) | copy-start | bytes 2396164
  62.9 8.0 %collective-permute-start.3 = (bf16[65,6,2,96]{0,3,2,1:T(8,128)(2,1)}, bf16[65,6,2,96]{0,3,2,1:T(8,128)(2,1)S(1)}, u32[]{:S(2)}, u32[]{:S(2)}) collective-permute-start(bf16[65,6,2,96]{0,3,2,1:T(8,128)(2,1)} %copy.31), channel_id=1, source_target_pairs={{0,1},{1,2},{2,3},{3,0},{4,5},{5,6},{6,7},{7,4},{8,9},{9,10},{10,1... | collective-permute-start | bytes 449288 | tf_op jit(solution)/shard_map/ppermute | solution.py:105
  62.9 9.1 %collective-permute-start.4 = (bf16[65,6,2,96]{0,3,2,1:T(8,128)(2,1)S(1)}, bf16[65,6,2,96]{0,3,2,1:T(8,128)(2,1)S(1)}, u32[]{:S(2)}, u32[]{:S(2)}) collective-permute-start(bf16[65,6,2,96]{0,3,2,1:T(8,128)(2,1)S(1)} %copy.32), channel_id=1, source_target_pairs={{0,3},{1,0},{2,1},{3,2},{4,7},{5,4},{6,5},{7,6},{8,11},{9,8},{10,9... | collective-permute-start | bytes 449288 | tf_op jit(solution)/shard_map/ppermute | solution.py:105
  64.6 14.2 %collective-permute-start.5 = (bf16[65,6,2,96]{0,3,2,1:T(8,128)(2,1)S(1)}, bf16[65,6,2,96]{0,3,2,1:T(8,128)(2,1)}, u32[]{:S(2)}, u32[]{:S(2)}) collective-permute-start(bf16[65,6,2,96]{0,3,2,1:T(8,128)(2,1)S(1)} %copy.34), channel_id=1, source_target_pairs={{0,2},{1,3},{2,0},{3,1},{4,6},{5,7},{6,4},{7,5},{8,10},{9,11},{10,... | collective-permute-start | bytes 449288 | tf_op jit(solution)/shard_map/ppermute | solution.py:105
  80.3 1.0 %copy-start.2 = (f32[256,256]{1,0:T(8,128)S(1)}, f32[256,256]{1,0:T(8,128)}, u32[]{:S(2)}) copy-start(f32[256,256]{1,0:T(8,128)} %pad_maximum_fusion.3) | copy-start | bytes 786436

commit v12 on v10

--- a/solution.py
+++ b/solution.py
@@ -131,21 +131,44 @@
     validity = valid_mask.astype(jnp.float32)
     spec = dft_whiten(rec_t, dft_rows.T, validity.T).astype(jnp.bfloat16)
 
-    gathered = lax.all_gather(spec.reshape(xs * slots, lanes), "pair", axis=0, tiled=False)
-    partner_list = jnp.bitwise_xor(pair_index, round_keys)
-    other = jnp.take(gathered, partner_list, axis=0, mode="clip").reshape(rounds, xs, slots, lanes)
-    rhs = other.transpose(2, 0, 1, 3).reshape(slots, rounds * xs, lanes)
+    flat = spec.reshape(xs * slots, lanes)
+    blocks = lax.axis_size("pair")
 
     half = lax.broadcasted_iota(jnp.int32, (lanes,), 0) < window_count
     turned = jnp.roll(spec, window_count, axis=-1) * jnp.where(half, 1.0, -1.0).astype(jnp.bfloat16)
     lhs = jnp.stack([spec, turned], axis=0).transpose(2, 0, 1, 3).reshape(slots, 2 * xs, lanes)
-    prod = jnp.einsum("fxk,fyk->fxy", lhs, rhs, preferred_element_type=jnp.float32)
-    prod = prod.reshape(slots, 2 * comp_count, station_count, rounds * xs)
 
-    stacked, same = exchange(prod, station_count, bands, band_index)
-    per_dev = stacked.shape[3]
-    totals = same[0, 0].reshape(per_dev, rounds, comp_count, station_count)[:, :, 0, :]
-    stacked = stacked[:, 1:].reshape(
+    def cross_with(other):
+        count = other.shape[0]
+        rhs = other.transpose(2, 0, 1, 3).reshape(slots, count * xs, lanes)
+        prod = jnp.einsum("fxk,fyk->fxy", lhs, rhs, preferred_element_type=jnp.float32)
+        prod = prod.reshape(slots, 2 * comp_count, station_count, count * xs)
+        stacked, same = exchange(prod, station_count, bands, band_index)
+        per_dev = stacked.shape[3]
+        totals = same[0, 0].reshape(per_dev, count, comp_count, station_count)[:, :, 0, :]
+        stacked = stacked.reshape(bands, slots, 2 * comp_count, per_dev, count, xs)
+        return stacked, totals
+
+    if blocks <= 8 and blocks & (blocks - 1) == 0:
+        outs, tots = [], []
+        for k in range(blocks):
+            held = flat
+            if k:
+                held = lax.ppermute(flat, "pair", [(p, p ^ k) for p in range(blocks)])
+            st, to = cross_with(held.reshape(1, xs, slots, lanes))
+            outs.append(st[..., 0, :])
+            tots.append(to[:, 0])
+        chosen = jnp.take(jnp.stack(outs), round_keys, axis=0, mode="clip")
+        totals = jnp.take(jnp.stack(tots), round_keys, axis=0, mode="clip")
+        chosen = jnp.moveaxis(chosen, 0, -2)
+    else:
+        gathered = lax.all_gather(flat, "pair", axis=0, tiled=False)
+        partner_list = jnp.bitwise_xor(pair_index, round_keys)
+        other = jnp.take(gathered, partner_list, axis=0, mode="clip").reshape(rounds, xs, slots, lanes)
+        chosen, totals = cross_with(other)
+        totals = totals.transpose(1, 0, 2)
+    per_dev = chosen.shape[3]
+    stacked = chosen[:, 1:].reshape(
         bands, nb, 2, comp_count, per_dev, rounds, comp_count, station_count
     )
 
@@ -158,7 +181,7 @@
         precision=lax.Precision.HIGHEST,
         preferred_element_type=jnp.float32,
     )
-    divisor = jnp.maximum(totals, 1.0).transpose(1, 0, 2)[:, :, None, None, :, None]
+    divisor = jnp.maximum(totals, 1.0)[:, :, None, None, :, None]
     lagged = lagged / divisor
     return lagged.reshape(rounds, per_dev, comp_count, comp_count * station_count, NLAG)
 

time: 95.1 us -> 68.4 us (0.72)
  the two profiles are of different devices: /device:TPU:0 before, /device:TPU:16 now
where the time goes in v12:
time: 68.4 us; the launch traced here: 67.9 us
  waiting for transfers between devices  26.3 us (38%)
  local copies, waits for them, and re-layouts  14.3 us (21%)
  starting transfers between devices  13 us (19%)
  other arithmetic  7.31 us (11%)
  Pallas kernels  3.47 us (5%)
  matrix products  3.19 us (5%)
    ppermute x3, waiting for transfers between devices, body(): held = lax.ppermute(flat, 'pair', [(p, p ^ k) for p in range(blocks)])  22.6 us
    ppermute x12, starting transfers between devices, exchange(): chunk = lax.ppermute(chunk.astype(jnp.bfloat16), ('win', 'band'), perm)  9.45 us
    unnamed x13, local copies, waits for them, and re-layouts  3.7 us
    ppermute x12, waiting for transfers between devices, exchange(): chunk = lax.ppermute(chunk.astype(jnp.bfloat16), ('win', 'band'), perm)  3.68 us
    ppermute x3, starting transfers between devices, body(): held = lax.ppermute(flat, 'pair', [(p, p ^ k) for p in range(blocks)])  3.55 us
    pallas_call x1, Pallas kernels, dft_whiten(): pl.pallas_call(dft_kernel, out_shape=jax.ShapeDtypeStruct((rows, 1 + nb,...  3.47 us
    reshape x3, local copies, waits for them, and re-layouts, body(): st, to = cross_with(held.reshape(1, xs, slots, lanes))  3.39 us
    convert_element_type x4, local copies, waits for them, and re-layouts, exchange(): chunk = lax.ppermute(chunk.astype(jnp.bfloat16), ('win', 'band'), perm)  2.18 us
  transfers between devices with their start and end apart: 15, of which 6 were waited for; matrix products, arithmetic and copies ran while one was open for 19% of the time, Pallas kernels for 0%

profile of v12, /device:TPU:16, one launch (start us, length us, event | category | flops | bytes accessed | tf_op | source)
XLA Modules:
  0.0 67.9 jit_solution(16938011435348482592)
XLA Ops:
  0.1 0.0 copy-start.4
  0.1 3.1 %copy.64 = bf16[64,3,8,512]{3,0,2,1:T(8,128)(2,1)} copy(bf16[64,3,8,512]{3,2,1,0:T(8,128)(2,1)} %param.3) | data formatting | bytes 3145728 | tf_op args[0]
  3.2 0.6 convert_bitcast_fusion.valid_ref
  3.8 0.6 multiply_convert_fusion
  4.4 0.7 maximum_bitcast_fusion.4.table_ref
  5.1 3.5 %shard_map.37 = f32[24,65,128]{2,1,0:T(8,128)} custom-call(bf16[24,64,512]{2,1,0:T(8,128)(2,1)} %bitcast.96, bf16[128,512]{1,0:T(8,128)(2,1)} %maximum_bitcast_fusion.4.table_ref, f32[8,64]{1,0:T(8,128)} %convert_bitcast_fusion.valid_ref), custom_call_target="tpu_custom_call" | custom-call | flops 201326592 | bytes 2502656 | tf_op jit(solution)/shard_map/pallas_call | solution.py:84
  8.5 1.2 %convert_element_type.107 = bf16[24,65,128]{2,1,0:T(8,128)(2,1)S(1)} convert(f32[24,65,128]{2,1,0:T(8,128)} %shard_map.37) | non-fusion elementwise | flops 199680 | bytes 1198080 | tf_op jit(solution)/shard_map/convert_element_type | solution.py:132
  9.8 0.1 reshape.115
  9.9 1.6 %collective-permute-start.3 = (bf16[1560,128]{1,0:T(8,128)(2,1)S(1)}, bf16[1560,128]{1,0:T(8,128)(2,1)}, u32[]{:S(2)}, u32[]{:S(2)}) collective-permute-start(bf16[1560,128]{1,0:T(8,128)(2,1)S(1)} %reshape.115), channel_id=1, source_target_pairs={{0,4},{4,0},{8,12},{12,8},{1,5},{5,1},{9,13},{13,9},{2,6},{6,2},{1... | collective-permute-start | bytes 1198088 | tf_op jit(solution)/shard_map/ppermute | solution.py:157
  11.5 0.3 collective-permute-start.7
  11.9 1.6 %collective-permute-start.11 = (bf16[1560,128]{1,0:T(8,128)(2,1)S(1)}, bf16[1560,128]{1,0:T(8,128)(2,1)}, u32[]{:S(2)}, u32[]{:S(2)}) collective-permute-start(bf16[1560,128]{1,0:T(8,128)(2,1)S(1)} %reshape.115), channel_id=1, source_target_pairs={{0,12},{4,8},{8,4},{12,0},{1,13},{5,9},{9,5},{13,1},{2,14},{6,10},... | collective-permute-start | bytes 1198088 | tf_op jit(solution)/shard_map/ppermute | solution.py:157
  13.5 0.2 slice_bitcast_fusion.1
  13.7 0.1 convert_bitcast_fusion.2
  13.7 0.1 convert_bitcast_fusion.1
  13.8 0.3 maximum_multiply_fusion
  14.1 0.1 pad_maximum_fusion.1
  14.2 0.5 fusion.12
  14.7 0.4 copy.67
  15.1 0.7 %dynamic-slice_convert_fusion.9 = (bf16[65,6,2,24]{0,3,2,1:T(8,128)(2,1)}, bf16[65,6,2,24]{0,3,2,1:T(8,128)(2,1)}, bf16[65,6,2,24]{0,3,2,1:T(8,128)(2,1)}) fusion(f32[65,6,8,24]{0,3,2,1:T(8,128)S(1)} %bitcast.97, s32[]{:T(128)S(6)} %select_n.157, s32[]{:T(128)S(6)} %select_n.153, s32[]{:T(128)S(6)} %select_n.151), kind=kLoop, calls=%fused_computation.65 | loop fusion | bytes 224652 | tf_op jit(solution)/shard_map/convert_element_type | solution.py:105
  15.9 1.7 %collective-permute-start.1 = (bf16[65,6,2,24]{0,3,2,1:T(8,128)(2,1)}, bf16[65,6,2,24]{0,3,2,1:T(8,128)(2,1)S(1)}, u32[]{:S(2)}, u32[]{:S(2)}) collective-permute-start(bf16[65,6,2,24]{0,3,2,1:T(8,128)(2,1)} %get-tuple-element.14), channel_id=1, source_target_pairs={{0,3},{1,0},{2,1},{3,2},{4,7},{5,4},{6,5},{7,6},{8,11},{9,8},{10,9... | collective-permute-start | bytes 112328 | tf_op jit(solution)/shard_map/ppermute | solution.py:105
  17.6 0.6 cosine_multiply_fusion
  18.2 0.7 %pad_maximum_fusion.2 = f32[256,256]{1,0:T(8,128)} fusion(f32[128,256]{1,0:T(8,128)S(1)} %get-tuple-element.30, f32[128,256]{1,0:T(8,128)S(1)} %get-tuple-element.29), kind=kLoop, calls=%fused_computation.30 | loop fusion | flops 65536 | bytes 524288 | tf_op jit(solution)/shard_map/concatenate | solution.py:36
  19.0 8.3 %collective-permute-done.3 = bf16[1560,128]{1,0:T(8,128)(2,1)} collective-permute-done((bf16[1560,128]{1,0:T(8,128)(2,1)S(1)}, bf16[1560,128]{1,0:T(8,128)(2,1)}, u32[]{:S(2)}, u32[]{:S(2)}) %collective-permute-start.3) | collective-permute-done | bytes 399392 | tf_op jit(solution)/shard_map/ppermute | solution.py:157
  27.3 1.5 %collective-permute-start.2 = (bf16[65,6,2,24]{0,3,2,1:T(8,128)(2,1)}, bf16[65,6,2,24]{0,3,2,1:T(8,128)(2,1)}, u32[]{:S(2)}, u32[]{:S(2)}) collective-permute-start(bf16[65,6,2,24]{0,3,2,1:T(8,128)(2,1)} %get-tuple-element.13), channel_id=1, source_target_pairs={{0,2},{1,3},{2,0},{3,1},{4,6},{5,7},{6,4},{7,5},{8,10},{9,11},{10,... | collective-permute-start | bytes 112328 | tf_op jit(solution)/shard_map/ppermute | solution.py:105
  28.8 1.1 %reshape.116 = bf16[1,24,65,128]{3,2,1,0:T(8,128)(2,1)S(1)} reshape(bf16[1560,128]{1,0:T(8,128)(2,1)} %collective-permute-done.3) | data formatting | bytes 798720 | tf_op jit(solution)/shard_map/reshape | solution.py:158
  29.9 0.5 fusion.7
  30.4 0.4 copy.70
  30.9 0.8 %dynamic-slice_convert_fusion.6 = (bf16[65,6,2,24]{0,3,2,1:T(8,128)(2,1)}, bf16[65,6,2,24]{0,3,2,1:T(8,128)(2,1)}, bf16[65,6,2,24]{0,3,2,1:T(8,128)(2,1)}) fusion(f32[65,6,8,24]{0,3,2,1:T(8,128)S(1)} %bitcast.103, s32[]{:T(128)S(6)} %select_n.157, s32[]{:T(128)S(6)} %select_n.153, s32[]{:T(128)S(6)} %select_n.151), kind=kLoop, calls=%fused_computation.58 | loop fusion | bytes 224652 | tf_op jit(solution)/shard_map/convert_element_type | solution.py:105
  31.6 7.0 %collective-permute-done.7 = bf16[1560,128]{1,0:T(8,128)(2,1)} collective-permute-done((bf16[1560,128]{1,0:T(8,128)(2,1)S(1)}, bf16[1560,128]{1,0:T(8,128)(2,1)}, u32[]{:S(2)}, u32[]{:S(2)}) %collective-permute-start.7) | collective-permute-done | bytes 399392 | tf_op jit(solution)/shard_map/ppermute | solution.py:157
  38.6 1.1 %reshape.119 = bf16[1,24,65,128]{3,2,1,0:T(8,128)(2,1)S(1)} reshape(bf16[1560,128]{1,0:T(8,128)(2,1)} %collective-permute-done.7) | data formatting | bytes 798720 | tf_op jit(solution)/shard_map/reshape | solution.py:158
  39.8 0.5 fusion.5
  40.3 0.4 copy.73
  40.7 7.3 %collective-permute-done.11 = bf16[1560,128]{1,0:T(8,128)(2,1)} collective-permute-done((bf16[1560,128]{1,0:T(8,128)(2,1)S(1)}, bf16[1560,128]{1,0:T(8,128)(2,1)}, u32[]{:S(2)}, u32[]{:S(2)}) %collective-permute-start.11) | collective-permute-done | bytes 399392 | tf_op jit(solution)/shard_map/ppermute | solution.py:157
  48.0 1.1 %reshape.122 = bf16[1,24,65,128]{3,2,1,0:T(8,128)(2,1)S(1)} reshape(bf16[1560,128]{1,0:T(8,128)(2,1)} %collective-permute-done.11) | data formatting | bytes 798720 | tf_op jit(solution)/shard_map/reshape | solution.py:158
  49.1 0.5 fusion.3
  49.6 0.7 dynamic-slice_convert_fusion.3
  50.3 0.4 copy.76
  50.7 1.6 %collective-permute-start.6 = (bf16[65,6,2,24]{0,3,2,1:T(8,128)(2,1)S(1)}, bf16[65,6,2,24]{0,3,2,1:T(8,128)(2,1)S(1)}, u32[]{:S(2)}, u32[]{:S(2)}) collective-permute-start(bf16[65,6,2,24]{0,3,2,1:T(8,128)(2,1)S(1)} %copy-done.3), channel_id=1, source_target_pairs={{0,2},{1,3},{2,0},{3,1},{4,6},{5,7},{6,4},{7,5},{8,10},{9,11},{10,... | collective-permute-start | bytes 112328 | tf_op jit(solution)/shard_map/ppermute | solution.py:105
  52.3 0.6 collective-permute-start.10
  52.9 1.7 %collective-permute-start.9 = (bf16[65,6,2,24]{0,3,2,1:T(8,128)(2,1)S(1)}, bf16[65,6,2,24]{0,3,2,1:T(8,128)(2,1)S(1)}, u32[]{:S(2)}, u32[]{:S(2)}) collective-permute-start(bf16[65,6,2,24]{0,3,2,1:T(8,128)(2,1)S(1)} %get-tuple-element.20), channel_id=1, source_target_pairs={{0,3},{1,0},{2,1},{3,2},{4,7},{5,4},{6,5},{7,6},{8,11},{9,8},{10,9... | collective-permute-start | bytes 112328 | tf_op jit(solution)/shard_map/ppermute | solution.py:105
  54.7 0.8 %collective-permute-done.6 = bf16[65,6,2,24]{0,3,2,1:T(8,128)(2,1)S(1)} collective-permute-done((bf16[65,6,2,24]{0,3,2,1:T(8,128)(2,1)S(1)}, bf16[65,6,2,24]{0,3,2,1:T(8,128)(2,1)S(1)}, u32[]{:S(2)}, u32[]{:S(2)}) %collective-permute-start.6) | collective-permute-done | bytes 37472 | tf_op jit(solution)/shard_map/ppermute | solution.py:105
  55.5 0.9 %collective-permute-start.13 = (bf16[65,6,2,24]{0,3,2,1:T(8,128)(2,1)S(1)}, bf16[65,6,2,24]{0,3,2,1:T(8,128)(2,1)S(1)}, u32[]{:S(2)}, u32[]{:S(2)}) collective-permute-start(bf16[65,6,2,24]{0,3,2,1:T(8,128)(2,1)S(1)} %get-tuple-element.23), channel_id=1, source_target_pairs={{0,3},{1,0},{2,1},{3,2},{4,7},{5,4},{6,5},{7,6},{8,11},{9,8},{10,9... | collective-permute-start | bytes 112328 | tf_op jit(solution)/shard_map/ppermute | solution.py:105
  56.4 1.1 %select_bitcast_fusion.5 = (f32[1,65,6,2,24]{1,4,3,2,0:T(8,128)S(1)}, f32[65,6,2,24]{0,3,2,1:T(8,128)S(1)}, f32[1,65,6,2,24]{1,4,3,2,0:T(8,128)S(1)}, f32[65,6,2,24]{0,3,2,1:T(8,128)S(1)}) fusion(bf16[65,6,2,24]{0,3,2,1:T(8,128)(2,1)} %collective-permute-done.5, bf16[65,6,2,24]{0,3,2,1:T(8,128)(2,1)S(1)} %collective-permute-done.4, pred[]{:T(512)S(6)} %eq.41, ...), kind=kLoop, calls=%fused_computation.56 | loop fusion | flops 224640 | bytes 673925 | tf_op jit(solution)/shard_map/stack | solution.py:115
  57.5 0.1 slice_reduce_fusion.3
  57.6 0.2 collective-permute-done.10
  57.7 1.4 %collective-permute-start.14 = (bf16[65,6,2,24]{0,3,2,1:T(8,128)(2,1)S(1)}, bf16[65,6,2,24]{0,3,2,1:T(8,128)(2,1)S(1)}, u32[]{:S(2)}, u32[]{:S(2)}) collective-permute-start(bf16[65,6,2,24]{0,3,2,1:T(8,128)(2,1)S(1)} %get-tuple-element.22), channel_id=1, source_target_pairs={{0,2},{1,3},{2,0},{3,1},{4,6},{5,7},{6,4},{7,5},{8,10},{9,11},{10,... | collective-permute-start | bytes 112328 | tf_op jit(solution)/shard_map/ppermute | solution.py:105
  59.1 0.1 slice_reduce_fusion.2
  59.2 0.1 reshape_squeeze.12
  59.3 0.1 reshape_squeeze.13
  59.4 0.0 collective-permute-done.12
  59.4 2.7 %collective-permute-done.14 = bf16[65,6,2,24]{0,3,2,1:T(8,128)(2,1)S(1)} collective-permute-done((bf16[65,6,2,24]{0,3,2,1:T(8,128)(2,1)S(1)}, bf16[65,6,2,24]{0,3,2,1:T(8,128)(2,1)S(1)}, u32[]{:S(2)}, u32[]{:S(2)}) %collective-permute-start.14) | collective-permute-done | bytes 37472 | tf_op jit(solution)/shard_map/ppermute | solution.py:105
  62.1 0.1 select_bitcast_fusion.1
  62.2 0.1 slice_reduce_fusion.1
  62.2 0.1 reshape_squeeze.14
  62.3 0.1 slice_reduce_fusion
  62.4 0.1 reshape_squeeze.15
  62.5 0.6 gather_fusion.1
  63.2 0.9 %select_bitcast_fusion.4 = f32[1,65,6,2,24]{1,4,3,2,0:T(8,128)S(1)} fusion(f32[65,6,2,24]{0,3,2,1:T(8,128)S(1)} %get-tuple-element.8, bf16[65,6,2,24]{0,3,2,1:T(8,128)(2,1)} %collective-permute-done.5, bf16[65,6,2,24]{0,3,2,1:T(8,128)(2,1)S(1)} %collective-permute-done.4, pred[]{:T(512)S(6)} %eq.42), kind=kLoop, calls=%fused_computation.55 | loop fusion | flops 74880 | bytes 224641 | tf_op jit(solution)/shard_map/stack | solution.py:115
  64.2 0.1 pad_maximum_fusion
  64.4 0.6 gather_fusion
  65.0 0.4 slice.52
  65.4 0.6 copy-done.2
  65.9 1.1 %fusion.1 = f32[4,2,3,24,256]{4,3,0,1,2:T(8,128)S(1)} fusion(f32[2,64,2,3,2,4,3,8]{1,7,6,4,3,2,0,5:T(8,128)S(1)} %bitcast.105, f32[4,2,8]{2,0,1:T(4,128)S(1)} %copy_maximum_fusion, f32[2,2,64,256]{3,2,1,0:T(8,128)S(1)} %bitcast.106), kind=kOutput, calls=%fused_computation.4 | convolution fusion | flops 453132288 | bytes 1442048 | tf_op jit(solution)/shard_map/gfuairbj,gufl->riabjl/dot_general | solution.py:177
  67.1 0.9 %copy.80 = f32[4,2,3,24,256]{4,3,2,1,0:T(8,128)} copy(f32[4,2,3,24,256]{4,3,0,1,2:T(8,128)S(1)} %fusion.1) | data formatting | bytes 1179648 | tf_op jit(solution)/shard_map/reshape | solution.py:186
  (43 shorter events, 0.4 us)
Async XLA Ops:
  0.1 3.1 %copy-start.4 = (s32[64,8]{0,1:T(8,128)S(1)}, s32[64,8]{0,1:T(8,128)}, u32[]{:S(2)}) copy-start(s32[64,8]{0,1:T(8,128)} %param.4) | copy-start | bytes 6148
  9.8 3.9 %copy-start = (f32[24,65,128]{2,1,0:T(8,128)S(1)}, f32[24,65,128]{2,1,0:T(8,128)}, u32[]{:S(2)}) copy-start(f32[24,65,128]{2,1,0:T(8,128)} %shard_map.37) | copy-start | bytes 2396164
  9.9 17.4 %collective-permute-start.3 = (bf16[1560,128]{1,0:T(8,128)(2,1)S(1)}, bf16[1560,128]{1,0:T(8,128)(2,1)}, u32[]{:S(2)}, u32[]{:S(2)}) collective-permute-start(bf16[1560,128]{1,0:T(8,128)(2,1)S(1)} %reshape.115), channel_id=1, source_target_pairs={{0,4},{4,0},{8,12},{12,8},{1,5},{5,1},{9,13},{13,9},{2,6},{6,2},{1... | collective-permute-start | bytes 1198088 | tf_op jit(solution)/shard_map/ppermute | solution.py:157
  11.5 27.1 %collective-permute-start.7 = (bf16[1560,128]{1,0:T(8,128)(2,1)S(1)}, bf16[1560,128]{1,0:T(8,128)(2,1)}, u32[]{:S(2)}, u32[]{:S(2)}) collective-permute-start(bf16[1560,128]{1,0:T(8,128)(2,1)S(1)} %reshape.115), channel_id=1, source_target_pairs={{0,8},{4,12},{8,0},{12,4},{1,9},{5,13},{9,1},{13,5},{2,10},{6,14},... | collective-permute-start | bytes 1198088 | tf_op jit(solution)/shard_map/ppermute | solution.py:157
  11.9 36.1 %collective-permute-start.11 = (bf16[1560,128]{1,0:T(8,128)(2,1)S(1)}, bf16[1560,128]{1,0:T(8,128)(2,1)}, u32[]{:S(2)}, u32[]{:S(2)}) collective-permute-start(bf16[1560,128]{1,0:T(8,128)(2,1)S(1)} %reshape.115), channel_id=1, source_target_pairs={{0,12},{4,8},{8,4},{12,0},{1,13},{5,9},{9,5},{13,1},{2,14},{6,10},... | collective-permute-start | bytes 1198088 | tf_op jit(solution)/shard_map/ppermute | solution.py:157
  14.7 4.2 %copy-start.5 = (s32[4]{0:T(128)S(1)}, s32[4]{0:T(128)}, u32[]{:S(2)}) copy-start(s32[4]{0:T(128)} %param.5) | copy-start | bytes 52
  15.9 34.8 %collective-permute-start = (bf16[65,6,2,24]{0,3,2,1:T(8,128)(2,1)}, bf16[65,6,2,24]{0,3,2,1:T(8,128)(2,1)S(1)}, u32[]{:S(2)}, u32[]{:S(2)}) collective-permute-start(bf16[65,6,2,24]{0,3,2,1:T(8,128)(2,1)} %get-tuple-element.15), channel_id=1, source_target_pairs={{0,1},{1,2},{2,3},{3,0},{4,5},{5,6},{6,7},{7,4},{8,9},{9,10},{10,1... | collective-permute-start | bytes 112328 | tf_op jit(solution)/shard_map/ppermute | solution.py:105
  15.9 36.4 %collective-permute-start.1 = (bf16[65,6,2,24]{0,3,2,1:T(8,128)(2,1)}, bf16[65,6,2,24]{0,3,2,1:T(8,128)(2,1)S(1)}, u32[]{:S(2)}, u32[]{:S(2)}) collective-permute-start(bf16[65,6,2,24]{0,3,2,1:T(8,128)(2,1)} %get-tuple-element.14), channel_id=1, source_target_pairs={{0,3},{1,0},{2,1},{3,2},{4,7},{5,4},{6,5},{7,6},{8,11},{9,8},{10,9... | collective-permute-start | bytes 112328 | tf_op jit(solution)/shard_map/ppermute | solution.py:105
  27.3 25.6 %collective-permute-start.2 = (bf16[65,6,2,24]{0,3,2,1:T(8,128)(2,1)}, bf16[65,6,2,24]{0,3,2,1:T(8,128)(2,1)}, u32[]{:S(2)}, u32[]{:S(2)}) collective-permute-start(bf16[65,6,2,24]{0,3,2,1:T(8,128)(2,1)} %get-tuple-element.13), channel_id=1, source_target_pairs={{0,2},{1,3},{2,0},{3,1},{4,6},{5,7},{6,4},{7,5},{8,10},{9,11},{10,... | collective-permute-start | bytes 112328 | tf_op jit(solution)/shard_map/ppermute | solution.py:105
  30.9 7.8 %copy-start.1 = (f32[65,48,24]{0,2,1:T(8,128)}, f32[65,48,24]{0,2,1:T(8,128)S(1)}, u32[]{:S(2)}) copy-start(f32[65,48,24]{0,2,1:T(8,128)S(1)} %copy.70) | copy-start | bytes 898564
  38.6 14.3 %collective-permute-start.4 = (bf16[65,6,2,24]{0,3,2,1:T(8,128)(2,1)}, bf16[65,6,2,24]{0,3,2,1:T(8,128)(2,1)S(1)}, u32[]{:S(2)}, u32[]{:S(2)}) collective-permute-start(bf16[65,6,2,24]{0,3,2,1:T(8,128)(2,1)} %get-tuple-element.18), channel_id=1, source_target_pairs={{0,1},{1,2},{2,3},{3,0},{4,5},{5,6},{6,7},{7,4},{8,9},{9,10},{10,1... | collective-permute-start | bytes 112328 | tf_op jit(solution)/shard_map/ppermute | solution.py:105
  48.0 6.7 %collective-permute-start.5 = (bf16[65,6,2,24]{0,3,2,1:T(8,128)(2,1)}, bf16[65,6,2,24]{0,3,2,1:T(8,128)(2,1)}, u32[]{:S(2)}, u32[]{:S(2)}) collective-permute-start(bf16[65,6,2,24]{0,3,2,1:T(8,128)(2,1)} %get-tuple-element.17), channel_id=1, source_target_pairs={{0,3},{1,0},{2,1},{3,2},{4,7},{5,4},{6,5},{7,6},{8,11},{9,8},{10,9... | collective-permute-start | bytes 112328 | tf_op jit(solution)/shard_map/ppermute | solution.py:105
  49.6 1.1 %copy-start.3 = (bf16[65,6,2,24]{0,3,2,1:T(8,128)(2,1)S(1)}, bf16[65,6,2,24]{0,3,2,1:T(8,128)(2,1)}, u32[]{:S(2)}) copy-start(bf16[65,6,2,24]{0,3,2,1:T(8,128)(2,1)} %get-tuple-element.16) | copy-start | bytes 112324
  50.7 4.8 %collective-permute-start.6 = (bf16[65,6,2,24]{0,3,2,1:T(8,128)(2,1)S(1)}, bf16[65,6,2,24]{0,3,2,1:T(8,128)(2,1)S(1)}, u32[]{:S(2)}, u32[]{:S(2)}) collective-permute-start(bf16[65,6,2,24]{0,3,2,1:T(8,128)(2,1)S(1)} %copy-done.3), channel_id=1, source_target_pairs={{0,2},{1,3},{2,0},{3,1},{4,6},{5,7},{6,4},{7,5},{8,10},{9,11},{10,... | collective-permute-start | bytes 112328 | tf_op jit(solution)/shard_map/ppermute | solution.py:105
  52.3 5.4 %collective-permute-start.10 = (bf16[65,6,2,24]{0,3,2,1:T(8,128)(2,1)}, bf16[65,6,2,24]{0,3,2,1:T(8,128)(2,1)S(1)}, u32[]{:S(2)}, u32[]{:S(2)}) collective-permute-start(bf16[65,6,2,24]{0,3,2,1:T(8,128)(2,1)} %get-tuple-element.19), channel_id=1, source_target_pairs={{0,2},{1,3},{2,0},{3,1},{4,6},{5,7},{6,4},{7,5},{8,10},{9,11},{10,... | collective-permute-start | bytes 112328 | tf_op jit(solution)/shard_map/ppermute | solution.py:105
  52.9 6.5 %collective-permute-start.8 = (bf16[65,6,2,24]{0,3,2,1:T(8,128)(2,1)S(1)}, bf16[65,6,2,24]{0,3,2,1:T(8,128)(2,1)S(1)}, u32[]{:S(2)}, u32[]{:S(2)}) collective-permute-start(bf16[65,6,2,24]{0,3,2,1:T(8,128)(2,1)S(1)} %get-tuple-element.21), channel_id=1, source_target_pairs={{0,1},{1,2},{2,3},{3,0},{4,5},{5,6},{6,7},{7,4},{8,9},{9,10},{10,1... | collective-permute-start | bytes 112328 | tf_op jit(solution)/shard_map/ppermute | solution.py:105
  52.9 6.5 %collective-permute-start.9 = (bf16[65,6,2,24]{0,3,2,1:T(8,128)(2,1)S(1)}, bf16[65,6,2,24]{0,3,2,1:T(8,128)(2,1)S(1)}, u32[]{:S(2)}, u32[]{:S(2)}) collective-permute-start(bf16[65,6,2,24]{0,3,2,1:T(8,128)(2,1)S(1)} %get-tuple-element.20), channel_id=1, source_target_pairs={{0,3},{1,0},{2,1},{3,2},{4,7},{5,4},{6,5},{7,6},{8,11},{9,8},{10,9... | collective-permute-start | bytes 112328 | tf_op jit(solution)/shard_map/ppermute | solution.py:105
  54.7 4.7 %collective-permute-start.12 = (bf16[65,6,2,24]{0,3,2,1:T(8,128)(2,1)S(1)}, bf16[65,6,2,24]{0,3,2,1:T(8,128)(2,1)S(1)}, u32[]{:S(2)}, u32[]{:S(2)}) collective-permute-start(bf16[65,6,2,24]{0,3,2,1:T(8,128)(2,1)S(1)} %get-tuple-element.24), channel_id=1, source_target_pairs={{0,1},{1,2},{2,3},{3,0},{4,5},{5,6},{6,7},{7,4},{8,9},{9,10},{10,1... | collective-permute-start | bytes 112328 | tf_op jit(solution)/shard_map/ppermute | solution.py:105
  55.5 3.9 %collective-permute-start.13 = (bf16[65,6,2,24]{0,3,2,1:T(8,128)(2,1)S(1)}, bf16[65,6,2,24]{0,3,2,1:T(8,128)(2,1)S(1)}, u32[]{:S(2)}, u32[]{:S(2)}) collective-permute-start(bf16[65,6,2,24]{0,3,2,1:T(8,128)(2,1)S(1)} %get-tuple-element.23), channel_id=1, source_target_pairs={{0,3},{1,0},{2,1},{3,2},{4,7},{5,4},{6,5},{7,6},{8,11},{9,8},{10,9... | collective-permute-start | bytes 112328 | tf_op jit(solution)/shard_map/ppermute | solution.py:105
  57.7 4.4 %collective-permute-start.14 = (bf16[65,6,2,24]{0,3,2,1:T(8,128)(2,1)S(1)}, bf16[65,6,2,24]{0,3,2,1:T(8,128)(2,1)S(1)}, u32[]{:S(2)}, u32[]{:S(2)}) collective-permute-start(bf16[65,6,2,24]{0,3,2,1:T(8,128)(2,1)S(1)} %get-tuple-element.22), channel_id=1, source_target_pairs={{0,2},{1,3},{2,0},{3,1},{4,6},{5,7},{6,4},{7,5},{8,10},{9,11},{10,... | collective-permute-start | bytes 112328 | tf_op jit(solution)/shard_map/ppermute | solution.py:105
  65.0 1.0 %copy-start.2 = (f32[256,256]{1,0:T(8,128)S(1)}, f32[256,256]{1,0:T(8,128)}, u32[]{:S(2)}) copy-start(f32[256,256]{1,0:T(8,128)} %pad_maximum_fusion.2) | copy-start | bytes 786436

commit v13 on v12

--- a/solution.py
+++ b/solution.py
@@ -150,14 +150,17 @@
         return stacked, totals
 
     if blocks <= 8 and blocks & (blocks - 1) == 0:
+        held = [flat] + [
+            lax.ppermute(flat, "pair", [(p, p ^ k) for p in range(blocks)]) for k in range(1, blocks)
+        ]
+        groups = [[0], [1], list(range(2, blocks))] if blocks > 2 else [[k] for k in range(blocks)]
         outs, tots = [], []
-        for k in range(blocks):
-            held = flat
-            if k:
-                held = lax.ppermute(flat, "pair", [(p, p ^ k) for p in range(blocks)])
-            st, to = cross_with(held.reshape(1, xs, slots, lanes))
-            outs.append(st[..., 0, :])
-            tots.append(to[:, 0])
+        for members in groups:
+            other = jnp.stack([held[k] for k in members]).reshape(len(members), xs, slots, lanes)
+            st, to = cross_with(other)
+            for n in range(len(members)):
+                outs.append(st[..., n, :])
+                tots.append(to[:, n])
         chosen = jnp.take(jnp.stack(outs), round_keys, axis=0, mode="clip")
         totals = jnp.take(jnp.stack(tots), round_keys, axis=0, mode="clip")
         chosen = jnp.moveaxis(chosen, 0, -2)

time: 68.4 us -> 70.3 us (1.028)
  the two profiles are of different devices: /device:TPU:16 before, /device:TPU:8 now
where the time goes in v13:
time: 70.3 us; the launch traced here: 70 us
  waiting for transfers between devices  31.8 us (45%)
  local copies, waits for them, and re-layouts  15.8 us (22%)
  starting transfers between devices  10.3 us (15%)
  other arithmetic  5.49 us (8%)
  Pallas kernels  3.47 us (5%)
  matrix products  2.7 us (4%)
    ppermute x3, waiting for transfers between devices, body(): lax.ppermute(flat, 'pair', [(p, p ^ k) for p in range(blocks)])  24.6 us
    ppermute x9, waiting for transfers between devices, exchange(): chunk = lax.ppermute(chunk.astype(jnp.bfloat16), ('win', 'band'), perm)  7.18 us
    ppermute x9, starting transfers between devices, exchange(): chunk = lax.ppermute(chunk.astype(jnp.bfloat16), ('win', 'band'), perm)  6.82 us
    unnamed x13, local copies, waits for them, and re-layouts  6.41 us
    ppermute x3, starting transfers between devices, body(): lax.ppermute(flat, 'pair', [(p, p ^ k) for p in range(blocks)])  3.49 us
    pallas_call x1, Pallas kernels, dft_whiten(): pl.pallas_call(dft_kernel, out_shape=jax.ShapeDtypeStruct((rows, 1 + nb,...  3.47 us
    another operation x3, local copies, waits for them, and re-layouts, body(): jnp.stack([held[k] for k in members])  2.39 us
    dot_general x3, matrix products, cross_with(): jnp.einsum('fxk,fyk->fxy', lhs, rhs, preferred_element_type=jnp.float32)  1.6 us
  transfers between devices with their start and end apart: 12, of which 5 were waited for; matrix products, arithmetic and copies ran while one was open for 18% of the time, Pallas kernels for 0%

profile of v13, /device:TPU:8, one launch (start us, length us, event | category | flops | bytes accessed | tf_op | source)
XLA Modules:
  0.0 70.0 jit_solution(2885845759278384924)
XLA Ops:
  0.1 0.0 copy-start.2
  0.1 3.1 %copy.63 = bf16[64,3,8,512]{3,0,2,1:T(8,128)(2,1)} copy(bf16[64,3,8,512]{3,2,1,0:T(8,128)(2,1)} %param.3) | data formatting | bytes 3145728 | tf_op args[0]
  3.2 0.6 convert_bitcast_fusion.valid_ref
  3.8 0.6 multiply_convert_fusion
  4.4 0.7 maximum_bitcast_fusion.3.table_ref
  5.0 3.5 %shard_map.37 = f32[24,65,128]{2,1,0:T(8,128)} custom-call(bf16[24,64,512]{2,1,0:T(8,128)(2,1)} %bitcast.88, bf16[128,512]{1,0:T(8,128)(2,1)} %maximum_bitcast_fusion.3.table_ref, f32[8,64]{1,0:T(8,128)} %convert_bitcast_fusion.valid_ref), custom_call_target="tpu_custom_call" | custom-call | flops 201326592 | bytes 2502656 | tf_op jit(solution)/shard_map/pallas_call | solution.py:84
  8.5 1.2 %convert_element_type.89 = bf16[24,65,128]{2,1,0:T(8,128)(2,1)S(1)} convert(f32[24,65,128]{2,1,0:T(8,128)} %shard_map.37) | non-fusion elementwise | flops 199680 | bytes 1198080 | tf_op jit(solution)/shard_map/convert_element_type | solution.py:132
  9.8 0.9 %reshape.110 = bf16[1560,128]{1,0:T(8,128)(2,1)} reshape(bf16[24,65,128]{2,1,0:T(8,128)(2,1)S(1)} %convert_element_type.89) | data formatting | bytes 798720 | tf_op jit(solution)/shard_map/reshape | solution.py:134
  10.6 0.0 collective-permute-start.3
  10.6 3.0 %collective-permute-start.7 = (bf16[1560,128]{1,0:T(8,128)(2,1)}, bf16[1560,128]{1,0:T(8,128)(2,1)}, u32[]{:S(2)}, u32[]{:S(2)}) collective-permute-start(bf16[1560,128]{1,0:T(8,128)(2,1)} %reshape.110), channel_id=1, source_target_pairs={{0,8},{4,12},{8,0},{12,4},{1,9},{5,13},{9,1},{13,5},{2,10},{6,14},... | collective-permute-start | bytes 1198088 | tf_op jit(solution)/shard_map/ppermute | solution.py:154
  13.7 0.4 collective-permute-start.8
  14.1 0.2 slice_bitcast_fusion.1
  14.3 0.1 convert_bitcast_fusion.2
  14.4 0.1 convert_bitcast_fusion.1
  14.5 0.3 maximum_multiply_fusion
  14.8 0.1 pad_maximum_fusion.1
  14.9 0.5 fusion.6
  15.4 0.0 copy-start.3
  15.4 0.4 copy.66
  15.8 0.7 %dynamic-slice_convert_fusion.3 = (bf16[65,6,2,24]{0,3,2,1:T(8,128)(2,1)}, bf16[65,6,2,24]{0,3,2,1:T(8,128)(2,1)}, bf16[65,6,2,24]{0,3,2,1:T(8,128)(2,1)}) fusion(f32[65,6,8,24]{0,3,2,1:T(8,128)S(1)} %bitcast.90, s32[]{:T(128)S(6)} %select_n.139, s32[]{:T(128)S(6)} %select_n.135, s32[]{:T(128)S(6)} %select_n.133), kind=kLoop, calls=%fused_computation.54 | loop fusion | bytes 224652 | tf_op jit(solution)/shard_map/convert_element_type | solution.py:105
  16.5 0.0 collective-permute-start
  16.5 1.7 %collective-permute-start.1 = (bf16[65,6,2,24]{0,3,2,1:T(8,128)(2,1)}, bf16[65,6,2,24]{0,3,2,1:T(8,128)(2,1)S(1)}, u32[]{:S(2)}, u32[]{:S(2)}) collective-permute-start(bf16[65,6,2,24]{0,3,2,1:T(8,128)(2,1)} %get-tuple-element.15), channel_id=1, source_target_pairs={{0,3},{1,0},{2,1},{3,2},{4,7},{5,4},{6,5},{7,6},{8,11},{9,8},{10,9... | collective-permute-start | bytes 112328 | tf_op jit(solution)/shard_map/ppermute | solution.py:105
  18.3 0.6 cosine_multiply_fusion
  18.9 0.7 %pad_maximum_fusion.3 = f32[256,256]{1,0:T(8,128)} fusion(f32[128,256]{1,0:T(8,128)S(1)} %get-tuple-element.29, f32[128,256]{1,0:T(8,128)S(1)} %get-tuple-element.28), kind=kLoop, calls=%fused_computation.33 | loop fusion | flops 65536 | bytes 524288 | tf_op jit(solution)/shard_map/concatenate | solution.py:36
  19.7 7.9 %collective-permute-done.3 = bf16[1560,128]{1,0:T(8,128)(2,1)S(1)} collective-permute-done((bf16[1560,128]{1,0:T(8,128)(2,1)}, bf16[1560,128]{1,0:T(8,128)(2,1)S(1)}, u32[]{:S(2)}, u32[]{:S(2)}) %collective-permute-start.3) | collective-permute-done | bytes 399392 | tf_op jit(solution)/shard_map/ppermute | solution.py:154
  27.6 1.7 %collective-permute-start.2 = (bf16[65,6,2,24]{0,3,2,1:T(8,128)(2,1)}, bf16[65,6,2,24]{0,3,2,1:T(8,128)(2,1)S(1)}, u32[]{:S(2)}, u32[]{:S(2)}) collective-permute-start(bf16[65,6,2,24]{0,3,2,1:T(8,128)(2,1)} %get-tuple-element.14), channel_id=1, source_target_pairs={{0,2},{1,3},{2,0},{3,1},{4,6},{5,7},{6,4},{7,5},{8,10},{9,11},{10,... | collective-permute-start | bytes 112328 | tf_op jit(solution)/shard_map/ppermute | solution.py:105
  29.2 0.1 reshape_stack.3
  29.3 0.5 fusion.4
  29.9 0.4 copy.69
  30.3 0.7 %dynamic-slice_convert_fusion = (bf16[65,6,2,24]{0,3,2,1:T(8,128)(2,1)}, bf16[65,6,2,24]{0,3,2,1:T(8,128)(2,1)}, bf16[65,6,2,24]{0,3,2,1:T(8,128)(2,1)}) fusion(f32[65,6,8,24]{0,3,2,1:T(8,128)S(1)} %bitcast.92, s32[]{:T(128)S(6)} %select_n.139, s32[]{:T(128)S(6)} %select_n.135, s32[]{:T(128)S(6)} %select_n.133), kind=kLoop, calls=%fused_computation.47 | loop fusion | bytes 224652 | tf_op jit(solution)/shard_map/convert_element_type | solution.py:105
  31.0 9.7 %collective-permute-done.7 = bf16[1560,128]{1,0:T(8,128)(2,1)} collective-permute-done((bf16[1560,128]{1,0:T(8,128)(2,1)}, bf16[1560,128]{1,0:T(8,128)(2,1)}, u32[]{:S(2)}, u32[]{:S(2)}) %collective-permute-start.7) | collective-permute-done | bytes 399392 | tf_op jit(solution)/shard_map/ppermute | solution.py:154
  40.7 0.0 collective-permute-start.4
  40.7 1.1 %stack.57 = bf16[1,24,65,128]{3,2,1,0:T(8,128)(2,1)S(1)} reshape(bf16[1560,128]{1,0:T(8,128)(2,1)} %collective-permute-done.7) | data formatting | bytes 798720 | tf_op jit(solution)/shard_map/stack | solution.py:159
  41.9 7.0 %collective-permute-done.8 = bf16[1560,128]{1,0:T(8,128)(2,1)} collective-permute-done((bf16[1560,128]{1,0:T(8,128)(2,1)}, bf16[1560,128]{1,0:T(8,128)(2,1)}, u32[]{:S(2)}, u32[]{:S(2)}) %collective-permute-start.8) | collective-permute-done | bytes 399392 | tf_op jit(solution)/shard_map/ppermute | solution.py:154
  48.9 1.1 %stack.58 = bf16[1,24,65,128]{3,2,1,0:T(8,128)(2,1)S(1)} reshape(bf16[1560,128]{1,0:T(8,128)(2,1)} %collective-permute-done.8) | data formatting | bytes 798720 | tf_op jit(solution)/shard_map/stack | solution.py:159
  50.0 0.1 maximum_bitcast_fusion
  50.1 0.1 copy.70
  50.2 0.6 convolution_bitcast_fusion
  50.8 0.5 constant_dynamic-slice_fusion
  51.2 1.6 %collective-permute-start.6 = (bf16[65,6,2,24]{0,3,2,1:T(8,128)(2,1)}, bf16[65,6,2,24]{0,3,2,1:T(8,128)(2,1)S(1)}, u32[]{:S(2)}, u32[]{:S(2)}) collective-permute-start(bf16[65,6,2,24]{0,3,2,1:T(8,128)(2,1)} %get-tuple-element.17), channel_id=1, source_target_pairs={{0,2},{1,3},{2,0},{3,1},{4,6},{5,7},{6,4},{7,5},{8,10},{9,11},{10,... | collective-permute-start | bytes 112328 | tf_op jit(solution)/shard_map/ppermute | solution.py:105
  52.8 0.1 constant_dynamic-slice_fusion.1
  52.9 0.2 copy.89
  53.1 0.8 %copy.88 = bf16[65,6,2,48]{0,3,2,1:T(8,128)(2,1)} copy(bf16[65,6,2,48]{3,2,1,0:T(2,128)(2,1)S(1)} %get-tuple-element.12) | data formatting | bytes 149760
  54.0 0.8 %copy.90 = bf16[65,6,2,48]{0,3,2,1:T(8,128)(2,1)} copy(bf16[65,6,2,48]{3,2,1,0:T(2,128)(2,1)S(1)} %get-tuple-element.11) | data formatting | bytes 149760
  54.8 0.8 %copy.87 = bf16[65,6,2,48]{0,3,2,1:T(8,128)(2,1)} copy(bf16[65,6,2,48]{3,2,1,0:T(2,128)(2,1)S(1)} %get-tuple-element.13) | data formatting | bytes 149760
  55.7 0.4 collective-permute-start.10
  56.1 1.5 %collective-permute-start.11 = (bf16[65,6,2,48]{0,3,2,1:T(8,128)(2,1)}, bf16[65,6,2,48]{0,3,2,1:T(8,128)(2,1)S(1)}, u32[]{:S(2)}, u32[]{:S(2)}) collective-permute-start(bf16[65,6,2,48]{0,3,2,1:T(8,128)(2,1)} %copy.90), channel_id=1, source_target_pairs={{0,2},{1,3},{2,0},{3,1},{4,6},{5,7},{6,4},{7,5},{8,10},{9,11},{10,... | collective-permute-start | bytes 224648 | tf_op jit(solution)/shard_map/ppermute | solution.py:105
  57.6 0.1 select_bitcast_fusion.1
  57.7 0.1 slice_reduce_fusion.2
  57.7 0.1 reshape_squeeze.9
  57.8 0.1 slice_reduce_fusion.1
  57.9 0.1 reshape_squeeze.10
  58.1 2.5 %collective-permute-done.10 = bf16[65,6,2,48]{0,3,2,1:T(8,128)(2,1)S(1)} collective-permute-done((bf16[65,6,2,48]{0,3,2,1:T(8,128)(2,1)}, bf16[65,6,2,48]{0,3,2,1:T(8,128)(2,1)S(1)}, u32[]{:S(2)}, u32[]{:S(2)}) %collective-permute-start.10) | collective-permute-done | bytes 74912 | tf_op jit(solution)/shard_map/ppermute | solution.py:105
  60.6 4.7 %collective-permute-done.11 = bf16[65,6,2,48]{0,3,2,1:T(8,128)(2,1)S(1)} collective-permute-done((bf16[65,6,2,48]{0,3,2,1:T(8,128)(2,1)}, bf16[65,6,2,48]{0,3,2,1:T(8,128)(2,1)S(1)}, u32[]{:S(2)}, u32[]{:S(2)}) %collective-permute-start.11) | collective-permute-done | bytes 74912 | tf_op jit(solution)/shard_map/ppermute | solution.py:105
  65.3 0.1 fusion.15
  65.4 0.1 slice_reduce_fusion
  65.5 0.1 reshape_squeeze.11
  65.6 0.6 gather_fusion.1
  66.3 0.1 pad_maximum_fusion
  66.4 0.6 gather_fusion
  67.0 0.4 slice.62
  67.4 0.6 copy-done.1
  68.0 1.1 %fusion.1 = f32[4,2,3,24,256]{4,3,0,1,2:T(8,128)S(1)} fusion(f32[2,64,2,3,2,4,3,8]{1,7,6,4,3,2,0,5:T(8,128)S(1)} %bitcast.94, f32[4,2,8]{2,0,1:T(4,128)S(1)} %copy_maximum_fusion, f32[2,2,64,256]{3,2,1,0:T(8,128)S(1)} %bitcast.97), kind=kOutput, calls=%fused_computation.5 | convolution fusion | flops 453132288 | bytes 1442048 | tf_op jit(solution)/shard_map/gfuairbj,gufl->riabjl/dot_general | solution.py:180
  69.1 0.9 %copy.81 = f32[4,2,3,24,256]{4,3,2,1,0:T(8,128)} copy(f32[4,2,3,24,256]{4,3,0,1,2:T(8,128)S(1)} %fusion.1) | data formatting | bytes 1179648 | tf_op jit(solution)/shard_map/reshape | solution.py:189
  (32 shorter events, 0.3 us)
Async XLA Ops:
  0.1 3.1 %copy-start.2 = (s32[64,8]{0,1:T(8,128)S(1)}, s32[64,8]{0,1:T(8,128)}, u32[]{:S(2)}) copy-start(s32[64,8]{0,1:T(8,128)} %param.4) | copy-start | bytes 6148
  9.7 4.6 %copy-start = (f32[24,65,128]{2,1,0:T(8,128)S(1)}, f32[24,65,128]{2,1,0:T(8,128)}, u32[]{:S(2)}) copy-start(f32[24,65,128]{2,1,0:T(8,128)} %shard_map.37) | copy-start | bytes 2396164
  10.6 16.9 %collective-permute-start.3 = (bf16[1560,128]{1,0:T(8,128)(2,1)}, bf16[1560,128]{1,0:T(8,128)(2,1)S(1)}, u32[]{:S(2)}, u32[]{:S(2)}) collective-permute-start(bf16[1560,128]{1,0:T(8,128)(2,1)} %reshape.110), channel_id=1, source_target_pairs={{0,4},{4,0},{8,12},{12,8},{1,5},{5,1},{9,13},{13,9},{2,6},{6,2},{1... | collective-permute-start | bytes 1198088 | tf_op jit(solution)/shard_map/ppermute | solution.py:154
  10.6 30.1 %collective-permute-start.7 = (bf16[1560,128]{1,0:T(8,128)(2,1)}, bf16[1560,128]{1,0:T(8,128)(2,1)}, u32[]{:S(2)}, u32[]{:S(2)}) collective-permute-start(bf16[1560,128]{1,0:T(8,128)(2,1)} %reshape.110), channel_id=1, source_target_pairs={{0,8},{4,12},{8,0},{12,4},{1,9},{5,13},{9,1},{13,5},{2,10},{6,14},... | collective-permute-start | bytes 1198088 | tf_op jit(solution)/shard_map/ppermute | solution.py:154
  13.7 35.2 %collective-permute-start.8 = (bf16[1560,128]{1,0:T(8,128)(2,1)}, bf16[1560,128]{1,0:T(8,128)(2,1)}, u32[]{:S(2)}, u32[]{:S(2)}) collective-permute-start(bf16[1560,128]{1,0:T(8,128)(2,1)} %reshape.110), channel_id=1, source_target_pairs={{0,12},{4,8},{8,4},{12,0},{1,13},{5,9},{9,5},{13,1},{2,14},{6,10},... | collective-permute-start | bytes 1198088 | tf_op jit(solution)/shard_map/ppermute | solution.py:154
  15.4 4.2 %copy-start.3 = (s32[4]{0:T(128)S(1)}, s32[4]{0:T(128)}, u32[]{:S(2)}) copy-start(s32[4]{0:T(128)} %param.5) | copy-start | bytes 52
  16.5 34.7 %collective-permute-start = (bf16[65,6,2,24]{0,3,2,1:T(8,128)(2,1)}, bf16[65,6,2,24]{0,3,2,1:T(8,128)(2,1)S(1)}, u32[]{:S(2)}, u32[]{:S(2)}) collective-permute-start(bf16[65,6,2,24]{0,3,2,1:T(8,128)(2,1)} %get-tuple-element.16), channel_id=1, source_target_pairs={{0,1},{1,2},{2,3},{3,0},{4,5},{5,6},{6,7},{7,4},{8,9},{9,10},{10,1... | collective-permute-start | bytes 112328 | tf_op jit(solution)/shard_map/ppermute | solution.py:105
  16.5 39.1 %collective-permute-start.1 = (bf16[65,6,2,24]{0,3,2,1:T(8,128)(2,1)}, bf16[65,6,2,24]{0,3,2,1:T(8,128)(2,1)S(1)}, u32[]{:S(2)}, u32[]{:S(2)}) collective-permute-start(bf16[65,6,2,24]{0,3,2,1:T(8,128)(2,1)} %get-tuple-element.15), channel_id=1, source_target_pairs={{0,3},{1,0},{2,1},{3,2},{4,7},{5,4},{6,5},{7,6},{8,11},{9,8},{10,9... | collective-permute-start | bytes 112328 | tf_op jit(solution)/shard_map/ppermute | solution.py:105
  27.6 28.5 %collective-permute-start.2 = (bf16[65,6,2,24]{0,3,2,1:T(8,128)(2,1)}, bf16[65,6,2,24]{0,3,2,1:T(8,128)(2,1)S(1)}, u32[]{:S(2)}, u32[]{:S(2)}) collective-permute-start(bf16[65,6,2,24]{0,3,2,1:T(8,128)(2,1)} %get-tuple-element.14), channel_id=1, source_target_pairs={{0,2},{1,3},{2,0},{3,1},{4,6},{5,7},{6,4},{7,5},{8,10},{9,11},{10,... | collective-permute-start | bytes 112328 | tf_op jit(solution)/shard_map/ppermute | solution.py:105
  40.7 16.8 %collective-permute-start.4 = (bf16[65,6,2,24]{0,3,2,1:T(8,128)(2,1)}, bf16[65,6,2,24]{0,3,2,1:T(8,128)(2,1)S(1)}, u32[]{:S(2)}, u32[]{:S(2)}) collective-permute-start(bf16[65,6,2,24]{0,3,2,1:T(8,128)(2,1)} %get-tuple-element.19), channel_id=1, source_target_pairs={{0,1},{1,2},{2,3},{3,0},{4,5},{5,6},{6,7},{7,4},{8,9},{9,10},{10,1... | collective-permute-start | bytes 112328 | tf_op jit(solution)/shard_map/ppermute | solution.py:105
  48.9 8.7 %collective-permute-start.5 = (bf16[65,6,2,24]{0,3,2,1:T(8,128)(2,1)}, bf16[65,6,2,24]{0,3,2,1:T(8,128)(2,1)S(1)}, u32[]{:S(2)}, u32[]{:S(2)}) collective-permute-start(bf16[65,6,2,24]{0,3,2,1:T(8,128)(2,1)} %get-tuple-element.18), channel_id=1, source_target_pairs={{0,3},{1,0},{2,1},{3,2},{4,7},{5,4},{6,5},{7,6},{8,11},{9,8},{10,9... | collective-permute-start | bytes 112328 | tf_op jit(solution)/shard_map/ppermute | solution.py:105
  51.2 6.3 %collective-permute-start.6 = (bf16[65,6,2,24]{0,3,2,1:T(8,128)(2,1)}, bf16[65,6,2,24]{0,3,2,1:T(8,128)(2,1)S(1)}, u32[]{:S(2)}, u32[]{:S(2)}) collective-permute-start(bf16[65,6,2,24]{0,3,2,1:T(8,128)(2,1)} %get-tuple-element.17), channel_id=1, source_target_pairs={{0,2},{1,3},{2,0},{3,1},{4,6},{5,7},{6,4},{7,5},{8,10},{9,11},{10,... | collective-permute-start | bytes 112328 | tf_op jit(solution)/shard_map/ppermute | solution.py:105
  55.7 4.9 %collective-permute-start.10 = (bf16[65,6,2,48]{0,3,2,1:T(8,128)(2,1)}, bf16[65,6,2,48]{0,3,2,1:T(8,128)(2,1)S(1)}, u32[]{:S(2)}, u32[]{:S(2)}) collective-permute-start(bf16[65,6,2,48]{0,3,2,1:T(8,128)(2,1)} %copy.88), channel_id=1, source_target_pairs={{0,3},{1,0},{2,1},{3,2},{4,7},{5,4},{6,5},{7,6},{8,11},{9,8},{10,9... | collective-permute-start | bytes 224648 | tf_op jit(solution)/shard_map/ppermute | solution.py:105
  56.1 9.3 %collective-permute-start.11 = (bf16[65,6,2,48]{0,3,2,1:T(8,128)(2,1)}, bf16[65,6,2,48]{0,3,2,1:T(8,128)(2,1)S(1)}, u32[]{:S(2)}, u32[]{:S(2)}) collective-permute-start(bf16[65,6,2,48]{0,3,2,1:T(8,128)(2,1)} %copy.90), channel_id=1, source_target_pairs={{0,2},{1,3},{2,0},{3,1},{4,6},{5,7},{6,4},{7,5},{8,10},{9,11},{10,... | collective-permute-start | bytes 224648 | tf_op jit(solution)/shard_map/ppermute | solution.py:105
  57.5 7.8 %collective-permute-start.9 = (bf16[65,6,2,48]{0,3,2,1:T(8,128)(2,1)}, bf16[65,6,2,48]{0,3,2,1:T(8,128)(2,1)S(1)}, u32[]{:S(2)}, u32[]{:S(2)}) collective-permute-start(bf16[65,6,2,48]{0,3,2,1:T(8,128)(2,1)} %copy.87), channel_id=1, source_target_pairs={{0,1},{1,2},{2,3},{3,0},{4,5},{5,6},{6,7},{7,4},{8,9},{9,10},{10,1... | collective-permute-start | bytes 224648 | tf_op jit(solution)/shard_map/ppermute | solution.py:105
  67.0 1.0 %copy-start.1 = (f32[256,256]{1,0:T(8,128)S(1)}, f32[256,256]{1,0:T(8,128)}, u32[]{:S(2)}) copy-start(f32[256,256]{1,0:T(8,128)} %pad_maximum_fusion.3) | copy-start | bytes 786436

commit v14 on v12

--- a/solution.py
+++ b/solution.py
@@ -93,26 +93,15 @@
 
 
 def exchange(prod, station_count, bands, band_index):
-    group = lax.axis_size("win") * bands
+    wins = lax.axis_size("win")
+    group = wins * bands
     per_dev = station_count // group
-    me = lax.axis_index("win") * bands + band_index
-    by_offset = [None] * bands
-    for shift in range(group):
-        dest = (me + shift) % group
-        chunk = lax.dynamic_slice_in_dim(prod, dest * per_dev, per_dev, 2)
-        if shift:
-            perm = [(k, (k + shift) % group) for k in range(group)]
-            chunk = lax.ppermute(chunk.astype(jnp.bfloat16), ("win", "band"), perm)
-            chunk = chunk.astype(jnp.float32)
-        q = shift % bands
-        by_offset[q] = chunk if by_offset[q] is None else by_offset[q] + chunk
-    ordered = []
-    for bb in range(bands):
-        pick = by_offset[0]
-        for q in range(1, bands):
-            pick = jnp.where((band_index - q) % bands == bb, by_offset[q], pick)
-        ordered.append(pick)
-    return jnp.stack(ordered, axis=0), by_offset[0]
+    slots, rows, _, ys = prod.shape
+    parts = prod.reshape(slots, rows, group, per_dev, ys)
+    parts = jnp.moveaxis(parts, 2, 0).astype(jnp.bfloat16)
+    got = lax.all_to_all(parts, ("win", "band"), split_axis=0, concat_axis=0, tiled=True)
+    got = got.astype(jnp.float32).reshape(wins, bands, slots, rows, per_dev, ys).sum(axis=0)
+    return got, got[0]
 
 
 def body(records, valid_mask, round_keys):

time: 68.4 us -> 75.4 us (1.10)
  the two profiles are of different devices: /device:TPU:16 before, /device:TPU:12 now
where the time goes in v14:
time: 75.4 us; the launch traced here: 74.9 us
  waiting for transfers between devices  33.1 us (44%)
  starting transfers between devices  17.4 us (23%)
  local copies, waits for them, and re-layouts  12 us (16%)
  other arithmetic  5.28 us (7%)
  Pallas kernels  3.48 us (5%)
  matrix products  3.24 us (4%)
    all_to_all x4, waiting for transfers between devices, exchange(): lax.all_to_all(parts, ('win', 'band'), split_axis=0, concat_axis=0, tiled...  17.1 us
    ppermute x3, waiting for transfers between devices, body(): held = lax.ppermute(flat, 'pair', [(p, p ^ k) for p in range(blocks)])  16 us
    all_to_all x4, starting transfers between devices, exchange(): lax.all_to_all(parts, ('win', 'band'), split_axis=0, concat_axis=0, tiled...  13.8 us
    convert_element_type x8, local copies, waits for them, and re-layouts, exchange(): parts = jnp.moveaxis(parts, 2, 0).astype(jnp.bfloat16)  4.45 us
    unnamed x11, local copies, waits for them, and re-layouts  3.68 us
    ppermute x3, starting transfers between devices, body(): held = lax.ppermute(flat, 'pair', [(p, p ^ k) for p in range(blocks)])  3.55 us
    pallas_call x1, Pallas kernels, dft_whiten(): pl.pallas_call(dft_kernel, out_shape=jax.ShapeDtypeStruct((rows, 1 + nb,...  3.48 us
    dot_general x4, matrix products, cross_with(): jnp.einsum('fxk,fyk->fxy', lhs, rhs, preferred_element_type=jnp.float32)  2.13 us
  transfers between devices with their start and end apart: 7, of which 6 were waited for; matrix products, arithmetic and copies ran while one was open for 13% of the time, Pallas kernels for 0%

profile of v14, /device:TPU:12, one launch (start us, length us, event | category | flops | bytes accessed | tf_op | source)
XLA Modules:
  0.0 74.9 jit_solution(13256747589284339616)
XLA Ops:
  0.1 0.0 copy-start.3
  0.1 3.1 %copy.107 = bf16[64,3,8,512]{3,0,2,1:T(8,128)(2,1)} copy(bf16[64,3,8,512]{3,2,1,0:T(8,128)(2,1)} %param.3) | data formatting | bytes 3145728 | tf_op args[0]
  3.2 0.6 convert_bitcast_fusion.valid_ref
  3.7 0.6 multiply_convert_fusion
  4.4 0.7 maximum_bitcast_fusion.table_ref
  5.0 3.5 %shard_map.37 = f32[24,65,128]{2,1,0:T(8,128)} custom-call(bf16[24,64,512]{2,1,0:T(8,128)(2,1)} %bitcast.104, bf16[128,512]{1,0:T(8,128)(2,1)} %maximum_bitcast_fusion.table_ref, f32[8,64]{1,0:T(8,128)} %convert_bitcast_fusion.valid_ref), custom_call_target="tpu_custom_call" | custom-call | flops 201326592 | bytes 2502656 | tf_op jit(solution)/shard_map/pallas_call | solution.py:84
  8.5 1.2 %convert_element_type.75 = bf16[24,65,128]{2,1,0:T(8,128)(2,1)S(1)} convert(f32[24,65,128]{2,1,0:T(8,128)} %shard_map.37) | non-fusion elementwise | flops 199680 | bytes 1198080 | tf_op jit(solution)/shard_map/convert_element_type | solution.py:121
  9.7 0.1 reshape.132
  9.9 0.5 collective-permute-start
  10.4 2.6 %collective-permute-start.1 = (bf16[1560,128]{1,0:T(8,128)(2,1)S(1)}, bf16[1560,128]{1,0:T(8,128)(2,1)S(1)}, u32[]{:S(2)}, u32[]{:S(2)}) collective-permute-start(bf16[1560,128]{1,0:T(8,128)(2,1)S(1)} %reshape.132), channel_id=1, source_target_pairs={{0,8},{4,12},{8,0},{12,4},{1,9},{5,13},{9,1},{13,5},{2,10},{6,14},... | collective-permute-start | bytes 1198088 | tf_op jit(solution)/shard_map/ppermute | solution.py:146
  13.0 0.5 collective-permute-start.2
  13.4 0.2 slice_bitcast_fusion.1
  13.6 0.1 convert_bitcast_fusion.2
  13.7 0.1 convert_bitcast_fusion.1
  13.8 0.3 maximum_multiply_fusion
  14.1 0.1 pad_maximum_fusion.1
  14.2 0.5 convolution_convert_fusion.3
  14.7 0.0 copy-start.4
  14.7 0.4 copy.110
  15.1 0.7 copy.111
  15.8 3.5 %all-to-all-start = ((bf16[4,65,6,2,24]{1,4,3,2,0:T(8,128)(2,1)}), bf16[4,65,6,2,24]{1,4,3,2,0:T(8,128)(2,1)S(1)}, u32[]{:S(2)}, u32[]{:S(2)}) async-start(bf16[4,65,6,2,24]{1,4,3,2,0:T(8,128)(2,1)} %copy.111), calls=%async_computation | async-start | bytes 589824 | tf_op jit(solution)/shard_map/all_to_all | solution.py:102
  19.3 0.6 cosine_multiply_fusion
  19.9 0.7 pad_maximum_fusion.2
  20.6 5.0 %all-to-all-done = bf16[4,65,6,2,24]{1,4,3,2,0:T(8,128)(2,1)S(1)} async-done(((bf16[4,65,6,2,24]{1,4,3,2,0:T(8,128)(2,1)}), bf16[4,65,6,2,24]{1,4,3,2,0:T(8,128)(2,1)S(1)}, u32[]{:S(2)}, u32[]{:S(2)}) %all-to-all-start) | async-done | bytes 149792 | tf_op jit(solution)/shard_map/all_to_all | solution.py:102
  25.6 0.1 convert_reduce_fusion.3
  25.7 0.1 slice_reduce_fusion.3
  25.8 0.1 reshape_squeeze.12
  25.9 0.8 %collective-permute-done = bf16[1560,128]{1,0:T(8,128)(2,1)S(1)} collective-permute-done((bf16[1560,128]{1,0:T(8,128)(2,1)S(1)}, bf16[1560,128]{1,0:T(8,128)(2,1)S(1)}, u32[]{:S(2)}, u32[]{:S(2)}) %collective-permute-start) | collective-permute-done | bytes 399392 | tf_op jit(solution)/shard_map/ppermute | solution.py:146
  26.7 0.1 reshape.133
  26.9 0.5 convolution_convert_fusion.2
  27.4 0.4 copy.116
  27.8 0.7 copy.117
  28.5 3.5 %all-to-all-start.1 = ((bf16[4,65,6,2,24]{1,4,3,2,0:T(8,128)(2,1)}), bf16[4,65,6,2,24]{1,4,3,2,0:T(8,128)(2,1)S(1)}, u32[]{:S(2)}, u32[]{:S(2)}) async-start(bf16[4,65,6,2,24]{1,4,3,2,0:T(8,128)(2,1)} %copy.117), calls=%async_computation.1 | async-start | bytes 589824 | tf_op jit(solution)/shard_map/all_to_all | solution.py:102
  32.0 7.8 %collective-permute-done.1 = bf16[1560,128]{1,0:T(8,128)(2,1)S(1)} collective-permute-done((bf16[1560,128]{1,0:T(8,128)(2,1)S(1)}, bf16[1560,128]{1,0:T(8,128)(2,1)S(1)}, u32[]{:S(2)}, u32[]{:S(2)}) %collective-permute-start.1) | collective-permute-done | bytes 399392 | tf_op jit(solution)/shard_map/ppermute | solution.py:146
  39.7 0.1 reshape.137
  39.9 0.5 convolution_convert_fusion.1
  40.4 7.4 %collective-permute-done.2 = bf16[1560,128]{1,0:T(8,128)(2,1)S(1)} collective-permute-done((bf16[1560,128]{1,0:T(8,128)(2,1)S(1)}, bf16[1560,128]{1,0:T(8,128)(2,1)S(1)}, u32[]{:S(2)}, u32[]{:S(2)}) %collective-permute-start.2) | collective-permute-done | bytes 399392 | tf_op jit(solution)/shard_map/ppermute | solution.py:146
  47.8 0.1 reshape.141
  48.0 0.5 convolution_convert_fusion
  48.5 0.4 copy.122
  48.9 0.7 copy.123
  49.6 0.4 copy.128
  50.0 0.7 copy.129
  50.8 0.0 all-to-all-done.1
  50.8 3.5 %all-to-all-start.2 = ((bf16[4,65,6,2,24]{1,4,3,2,0:T(8,128)(2,1)}), bf16[4,65,6,2,24]{1,4,3,2,0:T(8,128)(2,1)S(1)}, u32[]{:S(2)}, u32[]{:S(2)}) async-start(bf16[4,65,6,2,24]{1,4,3,2,0:T(8,128)(2,1)} %copy.123), calls=%async_computation.2 | async-start | bytes 589824 | tf_op jit(solution)/shard_map/all_to_all | solution.py:102
  54.2 0.1 convert_reduce_fusion.2
  54.3 0.1 slice_reduce_fusion.2
  54.4 0.1 reshape_squeeze.13
  54.5 6.1 %all-to-all-done.2 = bf16[4,65,6,2,24]{1,4,3,2,0:T(8,128)(2,1)S(1)} async-done(((bf16[4,65,6,2,24]{1,4,3,2,0:T(8,128)(2,1)}), bf16[4,65,6,2,24]{1,4,3,2,0:T(8,128)(2,1)S(1)}, u32[]{:S(2)}, u32[]{:S(2)}) %all-to-all-start.2) | async-done | bytes 149792 | tf_op jit(solution)/shard_map/all_to_all | solution.py:102
  60.5 3.5 %all-to-all-start.3 = ((bf16[4,65,6,2,24]{1,4,3,2,0:T(8,128)(2,1)}), bf16[4,65,6,2,24]{1,4,3,2,0:T(8,128)(2,1)S(1)}, u32[]{:S(2)}, u32[]{:S(2)}) async-start(bf16[4,65,6,2,24]{1,4,3,2,0:T(8,128)(2,1)} %copy.129), calls=%async_computation.3 | async-start | bytes 589824 | tf_op jit(solution)/shard_map/all_to_all | solution.py:102
  64.0 0.1 convert_reduce_fusion.1
  64.1 0.1 slice_reduce_fusion.1
  64.2 0.1 reshape_squeeze.14
  64.3 6.1 %all-to-all-done.3 = bf16[4,65,6,2,24]{1,4,3,2,0:T(8,128)(2,1)S(1)} async-done(((bf16[4,65,6,2,24]{1,4,3,2,0:T(8,128)(2,1)}), bf16[4,65,6,2,24]{1,4,3,2,0:T(8,128)(2,1)S(1)}, u32[]{:S(2)}, u32[]{:S(2)}) %all-to-all-start.3) | async-done | bytes 149792 | tf_op jit(solution)/shard_map/all_to_all | solution.py:102
  70.3 0.1 convert_reduce_fusion
  70.4 0.1 slice_reduce_fusion
  70.5 0.1 reshape_squeeze.15
  70.6 0.6 gather_fusion.1
  71.2 0.1 pad_maximum_fusion
  71.3 0.6 gather_fusion
  71.9 0.4 slice.68
  72.3 0.6 copy-done.1
  72.9 1.1 %fusion.1 = f32[4,2,3,24,256]{4,3,0,1,2:T(8,128)S(1)} fusion(f32[2,64,2,3,2,4,3,8]{1,7,6,4,3,2,0,5:T(8,128)S(1)} %bitcast.109, f32[4,2,8]{2,0,1:T(4,128)S(1)} %copy_maximum_fusion, f32[2,2,64,256]{3,2,1,0:T(8,128)S(1)} %bitcast.122), kind=kOutput, calls=%fused_computation.8 | convolution fusion | flops 453132288 | bytes 1442048 | tf_op jit(solution)/shard_map/gfuairbj,gufl->riabjl/dot_general | solution.py:166
  74.0 0.9 %copy.135 = f32[4,2,3,24,256]{4,3,2,1,0:T(8,128)} copy(f32[4,2,3,24,256]{4,3,0,1,2:T(8,128)S(1)} %fusion.1) | data formatting | bytes 1179648 | tf_op jit(solution)/shard_map/reshape | solution.py:175
  (24 shorter events, 0.2 us)
Async XLA Ops:
  0.1 3.1 %copy-start.3 = (s32[64,8]{0,1:T(8,128)S(1)}, s32[64,8]{0,1:T(8,128)}, u32[]{:S(2)}) copy-start(s32[64,8]{0,1:T(8,128)} %param.4) | copy-start | bytes 6148
  9.7 3.9 %copy-start = (f32[24,65,128]{2,1,0:T(8,128)S(1)}, f32[24,65,128]{2,1,0:T(8,128)}, u32[]{:S(2)}) copy-start(f32[24,65,128]{2,1,0:T(8,128)} %shard_map.37) | copy-start | bytes 2396164
  9.9 16.8 %collective-permute-start = (bf16[1560,128]{1,0:T(8,128)(2,1)S(1)}, bf16[1560,128]{1,0:T(8,128)(2,1)S(1)}, u32[]{:S(2)}, u32[]{:S(2)}) collective-permute-start(bf16[1560,128]{1,0:T(8,128)(2,1)S(1)} %reshape.132), channel_id=1, source_target_pairs={{0,4},{4,0},{8,12},{12,8},{1,5},{5,1},{9,13},{13,9},{2,6},{6,2},{1... | collective-permute-start | bytes 1198088 | tf_op jit(solution)/shard_map/ppermute | solution.py:146
  10.4 29.3 %collective-permute-start.1 = (bf16[1560,128]{1,0:T(8,128)(2,1)S(1)}, bf16[1560,128]{1,0:T(8,128)(2,1)S(1)}, u32[]{:S(2)}, u32[]{:S(2)}) collective-permute-start(bf16[1560,128]{1,0:T(8,128)(2,1)S(1)} %reshape.132), channel_id=1, source_target_pairs={{0,8},{4,12},{8,0},{12,4},{1,9},{5,13},{9,1},{13,5},{2,10},{6,14},... | collective-permute-start | bytes 1198088 | tf_op jit(solution)/shard_map/ppermute | solution.py:146
  13.0 34.9 %collective-permute-start.2 = (bf16[1560,128]{1,0:T(8,128)(2,1)S(1)}, bf16[1560,128]{1,0:T(8,128)(2,1)S(1)}, u32[]{:S(2)}, u32[]{:S(2)}) collective-permute-start(bf16[1560,128]{1,0:T(8,128)(2,1)S(1)} %reshape.132), channel_id=1, source_target_pairs={{0,12},{4,8},{8,4},{12,0},{1,13},{5,9},{9,5},{13,1},{2,14},{6,10},... | collective-permute-start | bytes 1198088 | tf_op jit(solution)/shard_map/ppermute | solution.py:146
  14.7 5.9 %copy-start.4 = (s32[4]{0:T(128)S(1)}, s32[4]{0:T(128)}, u32[]{:S(2)}) copy-start(s32[4]{0:T(128)} %param.5) | copy-start | bytes 52
  15.8 9.8 %all-to-all-start = ((bf16[4,65,6,2,24]{1,4,3,2,0:T(8,128)(2,1)}), bf16[4,65,6,2,24]{1,4,3,2,0:T(8,128)(2,1)S(1)}, u32[]{:S(2)}, u32[]{:S(2)}) async-start(bf16[4,65,6,2,24]{1,4,3,2,0:T(8,128)(2,1)} %copy.111), calls=%async_computation | async-start | bytes 589824 | tf_op jit(solution)/shard_map/all_to_all | solution.py:102
  25.9 1.5 %copy-start.2 = (f32[2,1,3,8]{3,2,0,1:T(4,128)}, f32[2,1,3,8]{3,2,0,1:T(4,128)S(1)}, u32[]{:S(2)}) copy-start(f32[2,1,3,8]{3,2,0,1:T(4,128)S(1)} %reshape_squeeze.12) | copy-start | bytes 580
  28.5 22.2 %all-to-all-start.1 = ((bf16[4,65,6,2,24]{1,4,3,2,0:T(8,128)(2,1)}), bf16[4,65,6,2,24]{1,4,3,2,0:T(8,128)(2,1)S(1)}, u32[]{:S(2)}, u32[]{:S(2)}) async-start(bf16[4,65,6,2,24]{1,4,3,2,0:T(8,128)(2,1)} %copy.117), calls=%async_computation.1 | async-start | bytes 589824 | tf_op jit(solution)/shard_map/all_to_all | solution.py:102
  50.8 9.8 %all-to-all-start.2 = ((bf16[4,65,6,2,24]{1,4,3,2,0:T(8,128)(2,1)}), bf16[4,65,6,2,24]{1,4,3,2,0:T(8,128)(2,1)S(1)}, u32[]{:S(2)}, u32[]{:S(2)}) async-start(bf16[4,65,6,2,24]{1,4,3,2,0:T(8,128)(2,1)} %copy.123), calls=%async_computation.2 | async-start | bytes 589824 | tf_op jit(solution)/shard_map/all_to_all | solution.py:102
  54.5 16.1 %slice-start = ((f32[2,1,3,8]{3,2,0,1:T(4,128)}), f32[2,1,1,8]{3,2,0,1:T(1,128)S(1)}, s32[]{:S(2)}) async-start(f32[2,1,3,8]{3,2,0,1:T(4,128)} %copy-done.2), calls=%async_computation.4 | async-start | bytes 2048 | tf_op jit(solution)/shard_map/slice | solution.py:137
  60.5 9.8 %all-to-all-start.3 = ((bf16[4,65,6,2,24]{1,4,3,2,0:T(8,128)(2,1)}), bf16[4,65,6,2,24]{1,4,3,2,0:T(8,128)(2,1)S(1)}, u32[]{:S(2)}, u32[]{:S(2)}) async-start(bf16[4,65,6,2,24]{1,4,3,2,0:T(8,128)(2,1)} %copy.129), calls=%async_computation.3 | async-start | bytes 589824 | tf_op jit(solution)/shard_map/all_to_all | solution.py:102
  71.9 1.0 %copy-start.1 = (f32[256,256]{1,0:T(8,128)S(1)}, f32[256,256]{1,0:T(8,128)}, u32[]{:S(2)}) copy-start(f32[256,256]{1,0:T(8,128)} %pad_maximum_fusion.2) | copy-start | bytes 786436

commit v15 on v12

--- a/solution.py
+++ b/solution.py
@@ -4,13 +4,11 @@
 import jax.numpy as jnp
 from jax import lax
 from jax.experimental import pallas as pl
-from jax.experimental.pallas import tpu as pltpu
 from jax.sharding import PartitionSpec as P
+
 
 FREQ = 128
 NLAG = 256
-ROUNDS = 4
-WSTEP = 4
 
 
 def dft_table(sample_points, bin_count, first_bin):
@@ -34,17 +32,6 @@
     phases = phase_turns.astype(jnp.float32) * (2.0 * math.pi / sample_points)
     lag_scale = 1.0 / math.sqrt(all_bins)
     return jnp.concatenate([jnp.cos(phases) * lag_scale, -(jnp.sin(phases) * lag_scale)], axis=0)
-
-
-def whiten(spectra, validity):
-    bin_count = spectra.shape[-1] // 2
-    real_part = spectra[..., :bin_count]
-    imag_part = spectra[..., bin_count:]
-    band_power = jnp.mean(real_part * real_part + imag_part * imag_part, axis=1)
-    amplitude = jnp.sqrt(jnp.maximum(band_power, 0.25))
-    factor = validity[:, :, None] / amplitude
-    factor = jnp.concatenate([factor, factor], axis=-1)
-    return (spectra * factor[:, None]).astype(jnp.bfloat16)
 
 
 def dft_kernel(rec_ref, table_ref, valid_ref, out_ref):

time: 68.4 us -> 68.4 us (level)
  no operation moved by 1% of the time
where the time goes in v15:
time: 68.4 us; the launch traced here: 67.9 us
  waiting for transfers between devices  26.3 us (38%)
  local copies, waits for them, and re-layouts  14.3 us (21%)
  starting transfers between devices  13 us (19%)
  other arithmetic  7.31 us (11%)
  Pallas kernels  3.47 us (5%)
  matrix products  3.19 us (5%)
    ppermute x3, waiting for transfers between devices, body(): held = lax.ppermute(flat, 'pair', [(p, p ^ k) for p in range(blocks)])  22.6 us
    ppermute x12, starting transfers between devices, exchange(): chunk = lax.ppermute(chunk.astype(jnp.bfloat16), ('win', 'band'), perm)  9.45 us
    unnamed x13, local copies, waits for them, and re-layouts  3.7 us
    ppermute x12, waiting for transfers between devices, exchange(): chunk = lax.ppermute(chunk.astype(jnp.bfloat16), ('win', 'band'), perm)  3.68 us
    ppermute x3, starting transfers between devices, body(): held = lax.ppermute(flat, 'pair', [(p, p ^ k) for p in range(blocks)])  3.55 us
    pallas_call x1, Pallas kernels, dft_whiten(): pl.pallas_call(dft_kernel, out_shape=jax.ShapeDtypeStruct((rows, 1 + nb,...  3.47 us
    reshape x3, local copies, waits for them, and re-layouts, body(): st, to = cross_with(held.reshape(1, xs, slots, lanes))  3.39 us
    convert_element_type x4, local copies, waits for them, and re-layouts, exchange(): chunk = lax.ppermute(chunk.astype(jnp.bfloat16), ('win', 'band'), perm)  2.18 us
  transfers between devices with their start and end apart: 15, of which 6 were waited for; matrix products, arithmetic and copies ran while one was open for 19% of the time, Pallas kernels for 0%

profile of v15, /device:TPU:16, one launch (start us, length us, event | category | flops | bytes accessed | tf_op | source)
XLA Modules:
  0.0 67.9 jit_solution(16938011435348482592)
XLA Ops:
  0.1 0.0 copy-start.4
  0.1 3.1 %copy.64 = bf16[64,3,8,512]{3,0,2,1:T(8,128)(2,1)} copy(bf16[64,3,8,512]{3,2,1,0:T(8,128)(2,1)} %param.3) | data formatting | bytes 3145728 | tf_op args[0]
  3.2 0.6 convert_bitcast_fusion.valid_ref
  3.8 0.6 multiply_convert_fusion
  4.4 0.7 maximum_bitcast_fusion.4.table_ref
  5.1 3.5 %shard_map.37 = f32[24,65,128]{2,1,0:T(8,128)} custom-call(bf16[24,64,512]{2,1,0:T(8,128)(2,1)} %bitcast.96, bf16[128,512]{1,0:T(8,128)(2,1)} %maximum_bitcast_fusion.4.table_ref, f32[8,64]{1,0:T(8,128)} %convert_bitcast_fusion.valid_ref), custom_call_target="tpu_custom_call" | custom-call | flops 201326592 | bytes 2502656 | tf_op jit(solution)/shard_map/pallas_call | solution.py:71
  8.5 1.2 %convert_element_type.107 = bf16[24,65,128]{2,1,0:T(8,128)(2,1)S(1)} convert(f32[24,65,128]{2,1,0:T(8,128)} %shard_map.37) | non-fusion elementwise | flops 199680 | bytes 1198080 | tf_op jit(solution)/shard_map/convert_element_type | solution.py:119
  9.8 0.1 reshape.115
  9.9 1.6 %collective-permute-start.3 = (bf16[1560,128]{1,0:T(8,128)(2,1)S(1)}, bf16[1560,128]{1,0:T(8,128)(2,1)}, u32[]{:S(2)}, u32[]{:S(2)}) collective-permute-start(bf16[1560,128]{1,0:T(8,128)(2,1)S(1)} %reshape.115), channel_id=1, source_target_pairs={{0,4},{4,0},{8,12},{12,8},{1,5},{5,1},{9,13},{13,9},{2,6},{6,2},{1... | collective-permute-start | bytes 1198088 | tf_op jit(solution)/shard_map/ppermute | solution.py:144
  11.5 0.3 collective-permute-start.7
  11.9 1.6 %collective-permute-start.11 = (bf16[1560,128]{1,0:T(8,128)(2,1)S(1)}, bf16[1560,128]{1,0:T(8,128)(2,1)}, u32[]{:S(2)}, u32[]{:S(2)}) collective-permute-start(bf16[1560,128]{1,0:T(8,128)(2,1)S(1)} %reshape.115), channel_id=1, source_target_pairs={{0,12},{4,8},{8,4},{12,0},{1,13},{5,9},{9,5},{13,1},{2,14},{6,10},... | collective-permute-start | bytes 1198088 | tf_op jit(solution)/shard_map/ppermute | solution.py:144
  13.5 0.2 slice_bitcast_fusion.1
  13.7 0.1 convert_bitcast_fusion.2
  13.7 0.1 convert_bitcast_fusion.1
  13.8 0.3 maximum_multiply_fusion
  14.1 0.1 pad_maximum_fusion.1
  14.2 0.5 fusion.12
  14.7 0.4 copy.67
  15.1 0.7 %dynamic-slice_convert_fusion.9 = (bf16[65,6,2,24]{0,3,2,1:T(8,128)(2,1)}, bf16[65,6,2,24]{0,3,2,1:T(8,128)(2,1)}, bf16[65,6,2,24]{0,3,2,1:T(8,128)(2,1)}) fusion(f32[65,6,8,24]{0,3,2,1:T(8,128)S(1)} %bitcast.97, s32[]{:T(128)S(6)} %select_n.157, s32[]{:T(128)S(6)} %select_n.153, s32[]{:T(128)S(6)} %select_n.151), kind=kLoop, calls=%fused_computation.65 | loop fusion | bytes 224652 | tf_op jit(solution)/shard_map/convert_element_type | solution.py:92
  15.9 1.7 %collective-permute-start.1 = (bf16[65,6,2,24]{0,3,2,1:T(8,128)(2,1)}, bf16[65,6,2,24]{0,3,2,1:T(8,128)(2,1)S(1)}, u32[]{:S(2)}, u32[]{:S(2)}) collective-permute-start(bf16[65,6,2,24]{0,3,2,1:T(8,128)(2,1)} %get-tuple-element.14), channel_id=1, source_target_pairs={{0,3},{1,0},{2,1},{3,2},{4,7},{5,4},{6,5},{7,6},{8,11},{9,8},{10,9... | collective-permute-start | bytes 112328 | tf_op jit(solution)/shard_map/ppermute | solution.py:92
  17.6 0.6 cosine_multiply_fusion
  18.2 0.7 %pad_maximum_fusion.2 = f32[256,256]{1,0:T(8,128)} fusion(f32[128,256]{1,0:T(8,128)S(1)} %get-tuple-element.30, f32[128,256]{1,0:T(8,128)S(1)} %get-tuple-element.29), kind=kLoop, calls=%fused_computation.30 | loop fusion | flops 65536 | bytes 524288 | tf_op jit(solution)/shard_map/concatenate | solution.py:34
  19.0 8.3 %collective-permute-done.3 = bf16[1560,128]{1,0:T(8,128)(2,1)} collective-permute-done((bf16[1560,128]{1,0:T(8,128)(2,1)S(1)}, bf16[1560,128]{1,0:T(8,128)(2,1)}, u32[]{:S(2)}, u32[]{:S(2)}) %collective-permute-start.3) | collective-permute-done | bytes 399392 | tf_op jit(solution)/shard_map/ppermute | solution.py:144
  27.3 1.5 %collective-permute-start.2 = (bf16[65,6,2,24]{0,3,2,1:T(8,128)(2,1)}, bf16[65,6,2,24]{0,3,2,1:T(8,128)(2,1)}, u32[]{:S(2)}, u32[]{:S(2)}) collective-permute-start(bf16[65,6,2,24]{0,3,2,1:T(8,128)(2,1)} %get-tuple-element.13), channel_id=1, source_target_pairs={{0,2},{1,3},{2,0},{3,1},{4,6},{5,7},{6,4},{7,5},{8,10},{9,11},{10,... | collective-permute-start | bytes 112328 | tf_op jit(solution)/shard_map/ppermute | solution.py:92
  28.8 1.1 %reshape.116 = bf16[1,24,65,128]{3,2,1,0:T(8,128)(2,1)S(1)} reshape(bf16[1560,128]{1,0:T(8,128)(2,1)} %collective-permute-done.3) | data formatting | bytes 798720 | tf_op jit(solution)/shard_map/reshape | solution.py:145
  29.9 0.5 fusion.7
  30.4 0.4 copy.70
  30.9 0.8 %dynamic-slice_convert_fusion.6 = (bf16[65,6,2,24]{0,3,2,1:T(8,128)(2,1)}, bf16[65,6,2,24]{0,3,2,1:T(8,128)(2,1)}, bf16[65,6,2,24]{0,3,2,1:T(8,128)(2,1)}) fusion(f32[65,6,8,24]{0,3,2,1:T(8,128)S(1)} %bitcast.103, s32[]{:T(128)S(6)} %select_n.157, s32[]{:T(128)S(6)} %select_n.153, s32[]{:T(128)S(6)} %select_n.151), kind=kLoop, calls=%fused_computation.58 | loop fusion | bytes 224652 | tf_op jit(solution)/shard_map/convert_element_type | solution.py:92
  31.6 7.0 %collective-permute-done.7 = bf16[1560,128]{1,0:T(8,128)(2,1)} collective-permute-done((bf16[1560,128]{1,0:T(8,128)(2,1)S(1)}, bf16[1560,128]{1,0:T(8,128)(2,1)}, u32[]{:S(2)}, u32[]{:S(2)}) %collective-permute-start.7) | collective-permute-done | bytes 399392 | tf_op jit(solution)/shard_map/ppermute | solution.py:144
  38.6 1.1 %reshape.119 = bf16[1,24,65,128]{3,2,1,0:T(8,128)(2,1)S(1)} reshape(bf16[1560,128]{1,0:T(8,128)(2,1)} %collective-permute-done.7) | data formatting | bytes 798720 | tf_op jit(solution)/shard_map/reshape | solution.py:145
  39.8 0.5 fusion.5
  40.3 0.4 copy.73
  40.7 7.3 %collective-permute-done.11 = bf16[1560,128]{1,0:T(8,128)(2,1)} collective-permute-done((bf16[1560,128]{1,0:T(8,128)(2,1)S(1)}, bf16[1560,128]{1,0:T(8,128)(2,1)}, u32[]{:S(2)}, u32[]{:S(2)}) %collective-permute-start.11) | collective-permute-done | bytes 399392 | tf_op jit(solution)/shard_map/ppermute | solution.py:144
  48.0 1.1 %reshape.122 = bf16[1,24,65,128]{3,2,1,0:T(8,128)(2,1)S(1)} reshape(bf16[1560,128]{1,0:T(8,128)(2,1)} %collective-permute-done.11) | data formatting | bytes 798720 | tf_op jit(solution)/shard_map/reshape | solution.py:145
  49.1 0.5 fusion.3
  49.6 0.7 dynamic-slice_convert_fusion.3
  50.3 0.4 copy.76
  50.7 1.6 %collective-permute-start.6 = (bf16[65,6,2,24]{0,3,2,1:T(8,128)(2,1)S(1)}, bf16[65,6,2,24]{0,3,2,1:T(8,128)(2,1)S(1)}, u32[]{:S(2)}, u32[]{:S(2)}) collective-permute-start(bf16[65,6,2,24]{0,3,2,1:T(8,128)(2,1)S(1)} %copy-done.3), channel_id=1, source_target_pairs={{0,2},{1,3},{2,0},{3,1},{4,6},{5,7},{6,4},{7,5},{8,10},{9,11},{10,... | collective-permute-start | bytes 112328 | tf_op jit(solution)/shard_map/ppermute | solution.py:92
  52.3 0.6 collective-permute-start.10
  52.9 1.7 %collective-permute-start.9 = (bf16[65,6,2,24]{0,3,2,1:T(8,128)(2,1)S(1)}, bf16[65,6,2,24]{0,3,2,1:T(8,128)(2,1)S(1)}, u32[]{:S(2)}, u32[]{:S(2)}) collective-permute-start(bf16[65,6,2,24]{0,3,2,1:T(8,128)(2,1)S(1)} %get-tuple-element.20), channel_id=1, source_target_pairs={{0,3},{1,0},{2,1},{3,2},{4,7},{5,4},{6,5},{7,6},{8,11},{9,8},{10,9... | collective-permute-start | bytes 112328 | tf_op jit(solution)/shard_map/ppermute | solution.py:92
  54.7 0.8 %collective-permute-done.6 = bf16[65,6,2,24]{0,3,2,1:T(8,128)(2,1)S(1)} collective-permute-done((bf16[65,6,2,24]{0,3,2,1:T(8,128)(2,1)S(1)}, bf16[65,6,2,24]{0,3,2,1:T(8,128)(2,1)S(1)}, u32[]{:S(2)}, u32[]{:S(2)}) %collective-permute-start.6) | collective-permute-done | bytes 37472 | tf_op jit(solution)/shard_map/ppermute | solution.py:92
  55.5 0.9 %collective-permute-start.13 = (bf16[65,6,2,24]{0,3,2,1:T(8,128)(2,1)S(1)}, bf16[65,6,2,24]{0,3,2,1:T(8,128)(2,1)S(1)}, u32[]{:S(2)}, u32[]{:S(2)}) collective-permute-start(bf16[65,6,2,24]{0,3,2,1:T(8,128)(2,1)S(1)} %get-tuple-element.23), channel_id=1, source_target_pairs={{0,3},{1,0},{2,1},{3,2},{4,7},{5,4},{6,5},{7,6},{8,11},{9,8},{10,9... | collective-permute-start | bytes 112328 | tf_op jit(solution)/shard_map/ppermute | solution.py:92
  56.4 1.1 %select_bitcast_fusion.5 = (f32[1,65,6,2,24]{1,4,3,2,0:T(8,128)S(1)}, f32[65,6,2,24]{0,3,2,1:T(8,128)S(1)}, f32[1,65,6,2,24]{1,4,3,2,0:T(8,128)S(1)}, f32[65,6,2,24]{0,3,2,1:T(8,128)S(1)}) fusion(bf16[65,6,2,24]{0,3,2,1:T(8,128)(2,1)} %collective-permute-done.5, bf16[65,6,2,24]{0,3,2,1:T(8,128)(2,1)S(1)} %collective-permute-done.4, pred[]{:T(512)S(6)} %eq.41, ...), kind=kLoop, calls=%fused_computation.56 | loop fusion | flops 224640 | bytes 673925 | tf_op jit(solution)/shard_map/stack | solution.py:102
  57.5 0.1 slice_reduce_fusion.3
  57.6 0.2 collective-permute-done.10
  57.7 1.4 %collective-permute-start.14 = (bf16[65,6,2,24]{0,3,2,1:T(8,128)(2,1)S(1)}, bf16[65,6,2,24]{0,3,2,1:T(8,128)(2,1)S(1)}, u32[]{:S(2)}, u32[]{:S(2)}) collective-permute-start(bf16[65,6,2,24]{0,3,2,1:T(8,128)(2,1)S(1)} %get-tuple-element.22), channel_id=1, source_target_pairs={{0,2},{1,3},{2,0},{3,1},{4,6},{5,7},{6,4},{7,5},{8,10},{9,11},{10,... | collective-permute-start | bytes 112328 | tf_op jit(solution)/shard_map/ppermute | solution.py:92
  59.1 0.1 slice_reduce_fusion.2
  59.2 0.1 reshape_squeeze.12
  59.3 0.1 reshape_squeeze.13
  59.4 0.0 collective-permute-done.12
  59.4 2.7 %collective-permute-done.14 = bf16[65,6,2,24]{0,3,2,1:T(8,128)(2,1)S(1)} collective-permute-done((bf16[65,6,2,24]{0,3,2,1:T(8,128)(2,1)S(1)}, bf16[65,6,2,24]{0,3,2,1:T(8,128)(2,1)S(1)}, u32[]{:S(2)}, u32[]{:S(2)}) %collective-permute-start.14) | collective-permute-done | bytes 37472 | tf_op jit(solution)/shard_map/ppermute | solution.py:92
  62.1 0.1 select_bitcast_fusion.1
  62.2 0.1 slice_reduce_fusion.1
  62.2 0.1 reshape_squeeze.14
  62.3 0.1 slice_reduce_fusion
  62.4 0.1 reshape_squeeze.15
  62.5 0.6 gather_fusion.1
  63.2 0.9 %select_bitcast_fusion.4 = f32[1,65,6,2,24]{1,4,3,2,0:T(8,128)S(1)} fusion(f32[65,6,2,24]{0,3,2,1:T(8,128)S(1)} %get-tuple-element.8, bf16[65,6,2,24]{0,3,2,1:T(8,128)(2,1)} %collective-permute-done.5, bf16[65,6,2,24]{0,3,2,1:T(8,128)(2,1)S(1)} %collective-permute-done.4, pred[]{:T(512)S(6)} %eq.42), kind=kLoop, calls=%fused_computation.55 | loop fusion | flops 74880 | bytes 224641 | tf_op jit(solution)/shard_map/stack | solution.py:102
  64.2 0.1 pad_maximum_fusion
  64.4 0.6 gather_fusion
  65.0 0.4 slice.52
  65.4 0.6 copy-done.2
  65.9 1.1 %fusion.1 = f32[4,2,3,24,256]{4,3,0,1,2:T(8,128)S(1)} fusion(f32[2,64,2,3,2,4,3,8]{1,7,6,4,3,2,0,5:T(8,128)S(1)} %bitcast.105, f32[4,2,8]{2,0,1:T(4,128)S(1)} %copy_maximum_fusion, f32[2,2,64,256]{3,2,1,0:T(8,128)S(1)} %bitcast.106), kind=kOutput, calls=%fused_computation.4 | convolution fusion | flops 453132288 | bytes 1442048 | tf_op jit(solution)/shard_map/gfuairbj,gufl->riabjl/dot_general | solution.py:164
  67.1 0.9 %copy.80 = f32[4,2,3,24,256]{4,3,2,1,0:T(8,128)} copy(f32[4,2,3,24,256]{4,3,0,1,2:T(8,128)S(1)} %fusion.1) | data formatting | bytes 1179648 | tf_op jit(solution)/shard_map/reshape | solution.py:173
  (43 shorter events, 0.4 us)
Async XLA Ops:
  0.1 3.1 %copy-start.4 = (s32[64,8]{0,1:T(8,128)S(1)}, s32[64,8]{0,1:T(8,128)}, u32[]{:S(2)}) copy-start(s32[64,8]{0,1:T(8,128)} %param.4) | copy-start | bytes 6148
  9.8 3.9 %copy-start = (f32[24,65,128]{2,1,0:T(8,128)S(1)}, f32[24,65,128]{2,1,0:T(8,128)}, u32[]{:S(2)}) copy-start(f32[24,65,128]{2,1,0:T(8,128)} %shard_map.37) | copy-start | bytes 2396164
  9.9 17.4 %collective-permute-start.3 = (bf16[1560,128]{1,0:T(8,128)(2,1)S(1)}, bf16[1560,128]{1,0:T(8,128)(2,1)}, u32[]{:S(2)}, u32[]{:S(2)}) collective-permute-start(bf16[1560,128]{1,0:T(8,128)(2,1)S(1)} %reshape.115), channel_id=1, source_target_pairs={{0,4},{4,0},{8,12},{12,8},{1,5},{5,1},{9,13},{13,9},{2,6},{6,2},{1... | collective-permute-start | bytes 1198088 | tf_op jit(solution)/shard_map/ppermute | solution.py:144
  11.5 27.1 %collective-permute-start.7 = (bf16[1560,128]{1,0:T(8,128)(2,1)S(1)}, bf16[1560,128]{1,0:T(8,128)(2,1)}, u32[]{:S(2)}, u32[]{:S(2)}) collective-permute-start(bf16[1560,128]{1,0:T(8,128)(2,1)S(1)} %reshape.115), channel_id=1, source_target_pairs={{0,8},{4,12},{8,0},{12,4},{1,9},{5,13},{9,1},{13,5},{2,10},{6,14},... | collective-permute-start | bytes 1198088 | tf_op jit(solution)/shard_map/ppermute | solution.py:144
  11.9 36.1 %collective-permute-start.11 = (bf16[1560,128]{1,0:T(8,128)(2,1)S(1)}, bf16[1560,128]{1,0:T(8,128)(2,1)}, u32[]{:S(2)}, u32[]{:S(2)}) collective-permute-start(bf16[1560,128]{1,0:T(8,128)(2,1)S(1)} %reshape.115), channel_id=1, source_target_pairs={{0,12},{4,8},{8,4},{12,0},{1,13},{5,9},{9,5},{13,1},{2,14},{6,10},... | collective-permute-start | bytes 1198088 | tf_op jit(solution)/shard_map/ppermute | solution.py:144
  14.7 4.2 %copy-start.5 = (s32[4]{0:T(128)S(1)}, s32[4]{0:T(128)}, u32[]{:S(2)}) copy-start(s32[4]{0:T(128)} %param.5) | copy-start | bytes 52
  15.9 34.8 %collective-permute-start = (bf16[65,6,2,24]{0,3,2,1:T(8,128)(2,1)}, bf16[65,6,2,24]{0,3,2,1:T(8,128)(2,1)S(1)}, u32[]{:S(2)}, u32[]{:S(2)}) collective-permute-start(bf16[65,6,2,24]{0,3,2,1:T(8,128)(2,1)} %get-tuple-element.15), channel_id=1, source_target_pairs={{0,1},{1,2},{2,3},{3,0},{4,5},{5,6},{6,7},{7,4},{8,9},{9,10},{10,1... | collective-permute-start | bytes 112328 | tf_op jit(solution)/shard_map/ppermute | solution.py:92
  15.9 36.4 %collective-permute-start.1 = (bf16[65,6,2,24]{0,3,2,1:T(8,128)(2,1)}, bf16[65,6,2,24]{0,3,2,1:T(8,128)(2,1)S(1)}, u32[]{:S(2)}, u32[]{:S(2)}) collective-permute-start(bf16[65,6,2,24]{0,3,2,1:T(8,128)(2,1)} %get-tuple-element.14), channel_id=1, source_target_pairs={{0,3},{1,0},{2,1},{3,2},{4,7},{5,4},{6,5},{7,6},{8,11},{9,8},{10,9... | collective-permute-start | bytes 112328 | tf_op jit(solution)/shard_map/ppermute | solution.py:92
  27.3 25.6 %collective-permute-start.2 = (bf16[65,6,2,24]{0,3,2,1:T(8,128)(2,1)}, bf16[65,6,2,24]{0,3,2,1:T(8,128)(2,1)}, u32[]{:S(2)}, u32[]{:S(2)}) collective-permute-start(bf16[65,6,2,24]{0,3,2,1:T(8,128)(2,1)} %get-tuple-element.13), channel_id=1, source_target_pairs={{0,2},{1,3},{2,0},{3,1},{4,6},{5,7},{6,4},{7,5},{8,10},{9,11},{10,... | collective-permute-start | bytes 112328 | tf_op jit(solution)/shard_map/ppermute | solution.py:92
  30.9 7.8 %copy-start.1 = (f32[65,48,24]{0,2,1:T(8,128)}, f32[65,48,24]{0,2,1:T(8,128)S(1)}, u32[]{:S(2)}) copy-start(f32[65,48,24]{0,2,1:T(8,128)S(1)} %copy.70) | copy-start | bytes 898564
  38.6 14.3 %collective-permute-start.4 = (bf16[65,6,2,24]{0,3,2,1:T(8,128)(2,1)}, bf16[65,6,2,24]{0,3,2,1:T(8,128)(2,1)S(1)}, u32[]{:S(2)}, u32[]{:S(2)}) collective-permute-start(bf16[65,6,2,24]{0,3,2,1:T(8,128)(2,1)} %get-tuple-element.18), channel_id=1, source_target_pairs={{0,1},{1,2},{2,3},{3,0},{4,5},{5,6},{6,7},{7,4},{8,9},{9,10},{10,1... | collective-permute-start | bytes 112328 | tf_op jit(solution)/shard_map/ppermute | solution.py:92
  48.0 6.7 %collective-permute-start.5 = (bf16[65,6,2,24]{0,3,2,1:T(8,128)(2,1)}, bf16[65,6,2,24]{0,3,2,1:T(8,128)(2,1)}, u32[]{:S(2)}, u32[]{:S(2)}) collective-permute-start(bf16[65,6,2,24]{0,3,2,1:T(8,128)(2,1)} %get-tuple-element.17), channel_id=1, source_target_pairs={{0,3},{1,0},{2,1},{3,2},{4,7},{5,4},{6,5},{7,6},{8,11},{9,8},{10,9... | collective-permute-start | bytes 112328 | tf_op jit(solution)/shard_map/ppermute | solution.py:92
  49.6 1.1 %copy-start.3 = (bf16[65,6,2,24]{0,3,2,1:T(8,128)(2,1)S(1)}, bf16[65,6,2,24]{0,3,2,1:T(8,128)(2,1)}, u32[]{:S(2)}) copy-start(bf16[65,6,2,24]{0,3,2,1:T(8,128)(2,1)} %get-tuple-element.16) | copy-start | bytes 112324
  50.7 4.8 %collective-permute-start.6 = (bf16[65,6,2,24]{0,3,2,1:T(8,128)(2,1)S(1)}, bf16[65,6,2,24]{0,3,2,1:T(8,128)(2,1)S(1)}, u32[]{:S(2)}, u32[]{:S(2)}) collective-permute-start(bf16[65,6,2,24]{0,3,2,1:T(8,128)(2,1)S(1)} %copy-done.3), channel_id=1, source_target_pairs={{0,2},{1,3},{2,0},{3,1},{4,6},{5,7},{6,4},{7,5},{8,10},{9,11},{10,... | collective-permute-start | bytes 112328 | tf_op jit(solution)/shard_map/ppermute | solution.py:92
  52.3 5.4 %collective-permute-start.10 = (bf16[65,6,2,24]{0,3,2,1:T(8,128)(2,1)}, bf16[65,6,2,24]{0,3,2,1:T(8,128)(2,1)S(1)}, u32[]{:S(2)}, u32[]{:S(2)}) collective-permute-start(bf16[65,6,2,24]{0,3,2,1:T(8,128)(2,1)} %get-tuple-element.19), channel_id=1, source_target_pairs={{0,2},{1,3},{2,0},{3,1},{4,6},{5,7},{6,4},{7,5},{8,10},{9,11},{10,... | collective-permute-start | bytes 112328 | tf_op jit(solution)/shard_map/ppermute | solution.py:92
  52.9 6.5 %collective-permute-start.8 = (bf16[65,6,2,24]{0,3,2,1:T(8,128)(2,1)S(1)}, bf16[65,6,2,24]{0,3,2,1:T(8,128)(2,1)S(1)}, u32[]{:S(2)}, u32[]{:S(2)}) collective-permute-start(bf16[65,6,2,24]{0,3,2,1:T(8,128)(2,1)S(1)} %get-tuple-element.21), channel_id=1, source_target_pairs={{0,1},{1,2},{2,3},{3,0},{4,5},{5,6},{6,7},{7,4},{8,9},{9,10},{10,1... | collective-permute-start | bytes 112328 | tf_op jit(solution)/shard_map/ppermute | solution.py:92
  52.9 6.5 %collective-permute-start.9 = (bf16[65,6,2,24]{0,3,2,1:T(8,128)(2,1)S(1)}, bf16[65,6,2,24]{0,3,2,1:T(8,128)(2,1)S(1)}, u32[]{:S(2)}, u32[]{:S(2)}) collective-permute-start(bf16[65,6,2,24]{0,3,2,1:T(8,128)(2,1)S(1)} %get-tuple-element.20), channel_id=1, source_target_pairs={{0,3},{1,0},{2,1},{3,2},{4,7},{5,4},{6,5},{7,6},{8,11},{9,8},{10,9... | collective-permute-start | bytes 112328 | tf_op jit(solution)/shard_map/ppermute | solution.py:92
  54.7 4.7 %collective-permute-start.12 = (bf16[65,6,2,24]{0,3,2,1:T(8,128)(2,1)S(1)}, bf16[65,6,2,24]{0,3,2,1:T(8,128)(2,1)S(1)}, u32[]{:S(2)}, u32[]{:S(2)}) collective-permute-start(bf16[65,6,2,24]{0,3,2,1:T(8,128)(2,1)S(1)} %get-tuple-element.24), channel_id=1, source_target_pairs={{0,1},{1,2},{2,3},{3,0},{4,5},{5,6},{6,7},{7,4},{8,9},{9,10},{10,1... | collective-permute-start | bytes 112328 | tf_op jit(solution)/shard_map/ppermute | solution.py:92
  55.5 3.9 %collective-permute-start.13 = (bf16[65,6,2,24]{0,3,2,1:T(8,128)(2,1)S(1)}, bf16[65,6,2,24]{0,3,2,1:T(8,128)(2,1)S(1)}, u32[]{:S(2)}, u32[]{:S(2)}) collective-permute-start(bf16[65,6,2,24]{0,3,2,1:T(8,128)(2,1)S(1)} %get-tuple-element.23), channel_id=1, source_target_pairs={{0,3},{1,0},{2,1},{3,2},{4,7},{5,4},{6,5},{7,6},{8,11},{9,8},{10,9... | collective-permute-start | bytes 112328 | tf_op jit(solution)/shard_map/ppermute | solution.py:92
  57.7 4.4 %collective-permute-start.14 = (bf16[65,6,2,24]{0,3,2,1:T(8,128)(2,1)S(1)}, bf16[65,6,2,24]{0,3,2,1:T(8,128)(2,1)S(1)}, u32[]{:S(2)}, u32[]{:S(2)}) collective-permute-start(bf16[65,6,2,24]{0,3,2,1:T(8,128)(2,1)S(1)} %get-tuple-element.22), channel_id=1, source_target_pairs={{0,2},{1,3},{2,0},{3,1},{4,6},{5,7},{6,4},{7,5},{8,10},{9,11},{10,... | collective-permute-start | bytes 112328 | tf_op jit(solution)/shard_map/ppermute | solution.py:92
  65.0 1.0 %copy-start.2 = (f32[256,256]{1,0:T(8,128)S(1)}, f32[256,256]{1,0:T(8,128)}, u32[]{:S(2)}) copy-start(f32[256,256]{1,0:T(8,128)} %pad_maximum_fusion.2) | copy-start | bytes 786436

commit v16 on v12

--- a/solution.py
+++ b/solution.py
@@ -149,38 +149,40 @@
         stacked = stacked.reshape(bands, slots, 2 * comp_count, per_dev, count, xs)
         return stacked, totals
 
+    full_lag = lag_table(sample_points, FREQ, 0, NLAG, FREQ)
+    full_lag = full_lag.reshape(2, bands, nb, NLAG).transpose(1, 0, 2, 3)
+
+    def to_lags(chosen, subscripts):
+        per_dev = chosen.shape[3]
+        shape = chosen.shape[:3] + (per_dev,) + chosen.shape[4:-1] + (comp_count, station_count)
+        stacked = chosen[:, 1:].reshape((bands, nb, 2, comp_count) + shape[3:])
+        return jnp.einsum(
+            subscripts,
+            stacked,
+            full_lag,
+            precision=lax.Precision.HIGHEST,
+            preferred_element_type=jnp.float32,
+        )
+
     if blocks <= 8 and blocks & (blocks - 1) == 0:
-        outs, tots = [], []
+        lags, tots = [], []
         for k in range(blocks):
             held = flat
             if k:
                 held = lax.ppermute(flat, "pair", [(p, p ^ k) for p in range(blocks)])
             st, to = cross_with(held.reshape(1, xs, slots, lanes))
-            outs.append(st[..., 0, :])
+            lags.append(to_lags(st[..., 0, :], "gfuaibj,gufl->iabjl"))
             tots.append(to[:, 0])
-        chosen = jnp.take(jnp.stack(outs), round_keys, axis=0, mode="clip")
+        lagged = jnp.take(jnp.stack(lags), round_keys, axis=0, mode="clip")
         totals = jnp.take(jnp.stack(tots), round_keys, axis=0, mode="clip")
-        chosen = jnp.moveaxis(chosen, 0, -2)
     else:
         gathered = lax.all_gather(flat, "pair", axis=0, tiled=False)
         partner_list = jnp.bitwise_xor(pair_index, round_keys)
         other = jnp.take(gathered, partner_list, axis=0, mode="clip").reshape(rounds, xs, slots, lanes)
         chosen, totals = cross_with(other)
         totals = totals.transpose(1, 0, 2)
-    per_dev = chosen.shape[3]
-    stacked = chosen[:, 1:].reshape(
-        bands, nb, 2, comp_count, per_dev, rounds, comp_count, station_count
-    )
-
-    full_lag = lag_table(sample_points, FREQ, 0, NLAG, FREQ)
-    full_lag = full_lag.reshape(2, bands, nb, NLAG).transpose(1, 0, 2, 3)
-    lagged = jnp.einsum(
-        "gfuairbj,gufl->riabjl",
-        stacked,
-        full_lag,
-        precision=lax.Precision.HIGHEST,
-        preferred_element_type=jnp.float32,
-    )
+        lagged = to_lags(chosen, "gfuairbj,gufl->riabjl")
+    per_dev = lagged.shape[1]
     divisor = jnp.maximum(totals, 1.0)[:, :, None, None, :, None]
     lagged = lagged / divisor
     return lagged.reshape(rounds, per_dev, comp_count, comp_count * station_count, NLAG)

time: 68.4 us -> 68.6 us (level)
  the two profiles are of different devices: /device:TPU:16 before, /device:TPU:0 now
where the time goes in v16:
time: 68.6 us; the launch traced here: 67.3 us
  waiting for transfers between devices  21.3 us (31%)
  starting transfers between devices  17.1 us (25%)
  local copies, waits for them, and re-layouts  12.6 us (18%)
  other arithmetic  8.61 us (13%)
  matrix products  3.76 us (5%)
  Pallas kernels  3.47 us (5%)
    ppermute x3, waiting for transfers between devices, body(): held = lax.ppermute(flat, 'pair', [(p, p ^ k) for p in range(blocks)])  17.6 us
    ppermute x12, starting transfers between devices, exchange(): chunk = lax.ppermute(chunk.astype(jnp.bfloat16), ('win', 'band'), perm)  11.4 us
    ppermute x3, starting transfers between devices, body(): held = lax.ppermute(flat, 'pair', [(p, p ^ k) for p in range(blocks)])  5.71 us
    ppermute x12, waiting for transfers between devices, exchange(): chunk = lax.ppermute(chunk.astype(jnp.bfloat16), ('win', 'band'), perm)  3.71 us
    pallas_call x1, Pallas kernels, dft_whiten(): pl.pallas_call(dft_kernel, out_shape=jax.ShapeDtypeStruct((rows, 1 + nb,...  3.47 us
    reshape x3, local copies, waits for them, and re-layouts, body(): st, to = cross_with(held.reshape(1, xs, slots, lanes))  3.39 us
    unnamed x13, local copies, waits for them, and re-layouts  3.13 us
    another operation x10, other arithmetic, exchange(): return (jnp.stack(ordered, axis=0), by_offset[0])  2.66 us
  transfers between devices with their start and end apart: 15, of which 4 were waited for; matrix products, arithmetic and copies ran while one was open for 22% of the time, Pallas kernels for 0%

profile of v16, /device:TPU:0, one launch (start us, length us, event | category | flops | bytes accessed | tf_op | source)
XLA Modules:
  0.0 67.3 jit_solution(14052533718734544692)
XLA Ops:
  0.1 3.1 %copy.28 = bf16[64,3,8,512]{3,0,2,1:T(8,128)(2,1)} copy(bf16[64,3,8,512]{3,2,1,0:T(8,128)(2,1)} %param.3) | data formatting | bytes 3145728 | tf_op args[0]
  3.2 0.6 convert_bitcast_fusion.valid_ref
  3.8 0.6 multiply_convert_fusion
  4.4 0.7 maximum_bitcast_fusion.table_ref
  5.1 3.5 %shard_map.37 = f32[24,65,128]{2,1,0:T(8,128)} custom-call(bf16[24,64,512]{2,1,0:T(8,128)(2,1)} %bitcast.138, bf16[128,512]{1,0:T(8,128)(2,1)} %maximum_bitcast_fusion.table_ref, f32[8,64]{1,0:T(8,128)} %convert_bitcast_fusion.valid_ref), custom_call_target="tpu_custom_call" | custom-call | flops 201326592 | bytes 2502656 | tf_op jit(solution)/shard_map/pallas_call | solution.py:84
  8.5 1.2 %convert_element_type.107 = bf16[24,65,128]{2,1,0:T(8,128)(2,1)S(1)} convert(f32[24,65,128]{2,1,0:T(8,128)} %shard_map.37) | non-fusion elementwise | flops 199680 | bytes 1198080 | tf_op jit(solution)/shard_map/convert_element_type | solution.py:132
  9.8 0.1 reshape.125
  9.9 3.1 %collective-permute-start.3 = (bf16[1560,128]{1,0:T(8,128)(2,1)S(1)}, bf16[1560,128]{1,0:T(8,128)(2,1)}, u32[]{:S(2)}, u32[]{:S(2)}) collective-permute-start(bf16[1560,128]{1,0:T(8,128)(2,1)S(1)} %reshape.125), channel_id=1, source_target_pairs={{0,4},{4,0},{8,12},{12,8},{1,5},{5,1},{9,13},{13,9},{2,6},{6,2},{1... | collective-permute-start | bytes 1198088 | tf_op jit(solution)/shard_map/ppermute | solution.py:172
  13.0 2.6 %collective-permute-start.7 = (bf16[1560,128]{1,0:T(8,128)(2,1)S(1)}, bf16[1560,128]{1,0:T(8,128)(2,1)}, u32[]{:S(2)}, u32[]{:S(2)}) collective-permute-start(bf16[1560,128]{1,0:T(8,128)(2,1)S(1)} %reshape.125), channel_id=1, source_target_pairs={{0,8},{4,12},{8,0},{12,4},{1,9},{5,13},{9,1},{13,5},{2,10},{6,14},... | collective-permute-start | bytes 1198088 | tf_op jit(solution)/shard_map/ppermute | solution.py:172
  15.6 0.2 slice_bitcast_fusion.1
  15.8 0.1 convert_bitcast_fusion.2
  16.0 0.3 maximum_multiply_fusion
  16.3 0.1 pad_maximum_fusion
  16.3 0.5 fusion.9
  16.9 0.4 copy.31
  17.3 0.7 %dynamic-slice_convert_fusion.9 = (bf16[65,6,2,24]{0,3,2,1:T(8,128)(2,1)}, bf16[65,6,2,24]{0,3,2,1:T(8,128)(2,1)}, bf16[65,6,2,24]{0,3,2,1:T(8,128)(2,1)}) fusion(f32[65,6,8,24]{0,3,2,1:T(8,128)S(1)} %bitcast.139, s32[]{:T(128)S(6)} %select_n.157, s32[]{:T(128)S(6)} %select_n.153, s32[]{:T(128)S(6)} %select_n.151), kind=kLoop, calls=%fused_computation.72 | loop fusion | bytes 224652 | tf_op jit(solution)/shard_map/convert_element_type | solution.py:105
  18.0 1.7 %collective-permute-start.1 = (bf16[65,6,2,24]{0,3,2,1:T(8,128)(2,1)}, bf16[65,6,2,24]{0,3,2,1:T(8,128)(2,1)S(1)}, u32[]{:S(2)}, u32[]{:S(2)}) collective-permute-start(bf16[65,6,2,24]{0,3,2,1:T(8,128)(2,1)} %get-tuple-element.14), channel_id=1, source_target_pairs={{0,3},{1,0},{2,1},{3,2},{4,7},{5,4},{6,5},{7,6},{8,11},{9,8},{10,9... | collective-permute-start | bytes 112328 | tf_op jit(solution)/shard_map/ppermute | solution.py:105
  19.8 0.6 cosine_multiply_fusion
  20.4 0.7 %pad_maximum_fusion.6 = f32[256,256]{1,0:T(8,128)} fusion(f32[128,256]{1,0:T(8,128)S(1)} %get-tuple-element.30, f32[128,256]{1,0:T(8,128)S(1)} %get-tuple-element.29), kind=kLoop, calls=%fused_computation.35 | loop fusion | flops 65536 | bytes 524288 | tf_op jit(solution)/shard_map/concatenate | solution.py:36
  21.1 9.1 %collective-permute-done.3 = bf16[1560,128]{1,0:T(8,128)(2,1)} collective-permute-done((bf16[1560,128]{1,0:T(8,128)(2,1)S(1)}, bf16[1560,128]{1,0:T(8,128)(2,1)}, u32[]{:S(2)}, u32[]{:S(2)}) %collective-permute-start.3) | collective-permute-done | bytes 399392 | tf_op jit(solution)/shard_map/ppermute | solution.py:172
  30.2 1.7 %collective-permute-start.2 = (bf16[65,6,2,24]{0,3,2,1:T(8,128)(2,1)}, bf16[65,6,2,24]{0,3,2,1:T(8,128)(2,1)}, u32[]{:S(2)}, u32[]{:S(2)}) collective-permute-start(bf16[65,6,2,24]{0,3,2,1:T(8,128)(2,1)} %get-tuple-element.13), channel_id=1, source_target_pairs={{0,2},{1,3},{2,0},{3,1},{4,6},{5,7},{6,4},{7,5},{8,10},{9,11},{10,... | collective-permute-start | bytes 112328 | tf_op jit(solution)/shard_map/ppermute | solution.py:105
  31.8 1.1 %reshape.126 = bf16[1,24,65,128]{3,2,1,0:T(8,128)(2,1)S(1)} reshape(bf16[1560,128]{1,0:T(8,128)(2,1)} %collective-permute-done.3) | data formatting | bytes 798720 | tf_op jit(solution)/shard_map/reshape | solution.py:173
  33.0 0.5 fusion.4
  33.5 0.4 copy.35
  33.9 0.8 %dynamic-slice_convert_fusion.6 = (bf16[65,6,2,24]{0,3,2,1:T(8,128)(2,1)}, bf16[65,6,2,24]{0,3,2,1:T(8,128)(2,1)}, bf16[65,6,2,24]{0,3,2,1:T(8,128)(2,1)}) fusion(f32[65,6,8,24]{0,3,2,1:T(8,128)S(1)} %bitcast.145, s32[]{:T(128)S(6)} %select_n.157, s32[]{:T(128)S(6)} %select_n.153, s32[]{:T(128)S(6)} %select_n.151), kind=kLoop, calls=%fused_computation.65 | loop fusion | bytes 224652 | tf_op jit(solution)/shard_map/convert_element_type | solution.py:105
  34.7 8.6 %collective-permute-done.7 = bf16[1560,128]{1,0:T(8,128)(2,1)} collective-permute-done((bf16[1560,128]{1,0:T(8,128)(2,1)S(1)}, bf16[1560,128]{1,0:T(8,128)(2,1)}, u32[]{:S(2)}, u32[]{:S(2)}) %collective-permute-start.7) | collective-permute-done | bytes 399392 | tf_op jit(solution)/shard_map/ppermute | solution.py:172
  43.3 1.1 %reshape.130 = bf16[1,24,65,128]{3,2,1,0:T(8,128)(2,1)S(1)} reshape(bf16[1560,128]{1,0:T(8,128)(2,1)} %collective-permute-done.7) | data formatting | bytes 798720 | tf_op jit(solution)/shard_map/reshape | solution.py:173
  44.4 0.5 fusion.2
  44.9 0.4 copy.39
  45.3 1.8 %collective-permute-start.5 = (bf16[65,6,2,24]{0,3,2,1:T(8,128)(2,1)}, bf16[65,6,2,24]{0,3,2,1:T(8,128)(2,1)}, u32[]{:S(2)}, u32[]{:S(2)}) collective-permute-start(bf16[65,6,2,24]{0,3,2,1:T(8,128)(2,1)} %get-tuple-element.17), channel_id=1, source_target_pairs={{0,3},{1,0},{2,1},{3,2},{4,7},{5,4},{6,5},{7,6},{8,11},{9,8},{10,9... | collective-permute-start | bytes 112328 | tf_op jit(solution)/shard_map/ppermute | solution.py:105
  47.1 1.1 %reshape.134 = bf16[1,24,65,128]{3,2,1,0:T(8,128)(2,1)S(1)} reshape(bf16[1560,128]{1,0:T(8,128)(2,1)} %collective-permute-done.11) | data formatting | bytes 798720 | tf_op jit(solution)/shard_map/reshape | solution.py:173
  48.3 0.5 fusion
  48.8 0.7 %dynamic-slice_convert_fusion.3 = (bf16[65,6,2,24]{0,3,2,1:T(8,128)(2,1)}, bf16[65,6,2,24]{0,3,2,1:T(8,128)(2,1)S(1)}, bf16[65,6,2,24]{0,3,2,1:T(8,128)(2,1)S(1)}) fusion(f32[65,6,8,24]{0,3,2,1:T(8,128)S(1)} %bitcast.141, s32[]{:T(128)S(6)} %select_n.157, s32[]{:T(128)S(6)} %select_n.153, s32[]{:T(128)S(6)} %select_n.151), kind=kLoop, calls=%fused_computation.58 | loop fusion | bytes 224652 | tf_op jit(solution)/shard_map/convert_element_type | solution.py:105
  49.5 0.4 copy.43
  49.9 1.6 %collective-permute-start.6 = (bf16[65,6,2,24]{0,3,2,1:T(8,128)(2,1)S(1)}, bf16[65,6,2,24]{0,3,2,1:T(8,128)(2,1)S(1)}, u32[]{:S(2)}, u32[]{:S(2)}) collective-permute-start(bf16[65,6,2,24]{0,3,2,1:T(8,128)(2,1)S(1)} %copy-done.3), channel_id=1, source_target_pairs={{0,2},{1,3},{2,0},{3,1},{4,6},{5,7},{6,4},{7,5},{8,10},{9,11},{10,... | collective-permute-start | bytes 112328 | tf_op jit(solution)/shard_map/ppermute | solution.py:105
  51.5 0.6 collective-permute-start.10
  52.1 1.7 %collective-permute-start.9 = (bf16[65,6,2,24]{0,3,2,1:T(8,128)(2,1)S(1)}, bf16[65,6,2,24]{0,3,2,1:T(8,128)(2,1)S(1)}, u32[]{:S(2)}, u32[]{:S(2)}) collective-permute-start(bf16[65,6,2,24]{0,3,2,1:T(8,128)(2,1)S(1)} %get-tuple-element.20), channel_id=1, source_target_pairs={{0,3},{1,0},{2,1},{3,2},{4,7},{5,4},{6,5},{7,6},{8,11},{9,8},{10,9... | collective-permute-start | bytes 112328 | tf_op jit(solution)/shard_map/ppermute | solution.py:105
  53.9 0.9 %collective-permute-done.6 = bf16[65,6,2,24]{0,3,2,1:T(8,128)(2,1)S(1)} collective-permute-done((bf16[65,6,2,24]{0,3,2,1:T(8,128)(2,1)S(1)}, bf16[65,6,2,24]{0,3,2,1:T(8,128)(2,1)S(1)}, u32[]{:S(2)}, u32[]{:S(2)}) %collective-permute-start.6) | collective-permute-done | bytes 37472 | tf_op jit(solution)/shard_map/ppermute | solution.py:105
  54.8 0.8 %collective-permute-start.13 = (bf16[65,6,2,24]{0,3,2,1:T(8,128)(2,1)S(1)}, bf16[65,6,2,24]{0,3,2,1:T(8,128)(2,1)S(1)}, u32[]{:S(2)}, u32[]{:S(2)}) collective-permute-start(bf16[65,6,2,24]{0,3,2,1:T(8,128)(2,1)S(1)} %get-tuple-element.23), channel_id=1, source_target_pairs={{0,3},{1,0},{2,1},{3,2},{4,7},{5,4},{6,5},{7,6},{8,11},{9,8},{10,9... | collective-permute-start | bytes 112328 | tf_op jit(solution)/shard_map/ppermute | solution.py:105
  55.6 1.1 %select_bitcast_fusion.5 = (f32[1,65,6,2,24]{1,4,3,2,0:T(8,128)S(1)}, f32[65,6,2,24]{0,3,2,1:T(8,128)S(1)}, f32[1,65,6,2,24]{1,4,3,2,0:T(8,128)S(1)}, f32[65,6,2,24]{0,3,2,1:T(8,128)S(1)}) fusion(bf16[65,6,2,24]{0,3,2,1:T(8,128)(2,1)} %collective-permute-done.5, bf16[65,6,2,24]{0,3,2,1:T(8,128)(2,1)S(1)} %collective-permute-done.4, pred[]{:T(512)S(6)} %eq.41, ...), kind=kLoop, calls=%fused_computation.63 | loop fusion | flops 224640 | bytes 673925 | tf_op jit(solution)/shard_map/stack | solution.py:115
  56.7 0.1 pad_maximum_fusion.5
  56.9 0.4 convolution_bitcast_fusion.3
  57.3 0.9 %select_bitcast_fusion.4 = f32[1,65,6,2,24]{1,4,3,2,0:T(8,128)S(1)} fusion(f32[65,6,2,24]{0,3,2,1:T(8,128)S(1)} %get-tuple-element.8, bf16[65,6,2,24]{0,3,2,1:T(8,128)(2,1)} %collective-permute-done.5, bf16[65,6,2,24]{0,3,2,1:T(8,128)(2,1)S(1)} %collective-permute-done.4, pred[]{:T(512)S(6)} %eq.42), kind=kLoop, calls=%fused_computation.62 | loop fusion | flops 74880 | bytes 224641 | tf_op jit(solution)/shard_map/stack | solution.py:115
  58.2 0.1 pad_maximum_fusion.4
  58.4 0.4 convolution_bitcast_fusion.2
  58.8 0.1 slice_reduce_fusion.3
  58.9 1.5 %collective-permute-start.14 = (bf16[65,6,2,24]{0,3,2,1:T(8,128)(2,1)S(1)}, bf16[65,6,2,24]{0,3,2,1:T(8,128)(2,1)S(1)}, u32[]{:S(2)}, u32[]{:S(2)}) collective-permute-start(bf16[65,6,2,24]{0,3,2,1:T(8,128)(2,1)S(1)} %get-tuple-element.22), channel_id=1, source_target_pairs={{0,2},{1,3},{2,0},{3,1},{4,6},{5,7},{6,4},{7,5},{8,10},{9,11},{10,... | collective-permute-start | bytes 112328 | tf_op jit(solution)/shard_map/ppermute | solution.py:105
  60.4 0.1 slice_reduce_fusion.2
  60.5 2.7 %collective-permute-done.14 = bf16[65,6,2,24]{0,3,2,1:T(8,128)(2,1)S(1)} collective-permute-done((bf16[65,6,2,24]{0,3,2,1:T(8,128)(2,1)S(1)}, bf16[65,6,2,24]{0,3,2,1:T(8,128)(2,1)S(1)}, u32[]{:S(2)}, u32[]{:S(2)}) %collective-permute-start.14) | collective-permute-done | bytes 37472 | tf_op jit(solution)/shard_map/ppermute | solution.py:105
  63.3 0.1 select_bitcast_fusion.1
  63.3 0.1 slice_reduce_fusion.1
  63.5 0.1 pad_maximum_fusion.3
  63.6 0.4 convolution_bitcast_fusion.1
  64.0 0.1 slice_reduce_fusion
  64.1 0.1 pad_maximum_fusion.2
  64.3 0.4 convolution_bitcast_fusion
  64.7 0.1 reshape_squeeze.12
  64.8 0.1 reshape_squeeze.13
  64.9 0.1 reshape_squeeze.14
  65.0 0.1 reshape_squeeze.15
  65.1 0.6 gather_fusion
  65.7 0.6 gather_fusion.1
  66.3 0.1 div.14
  66.4 0.9 %copy_divide_fusion = f32[4,2,3,24,256]{4,3,2,1,0:T(8,128)} fusion(f32[4,2,24]{2,1,0:T(2,128)S(1)} %div.14, f32[4,2,3,3,8,256]{5,4,3,1,2,0:T(8,128)S(1)} %gather_fusion), kind=kLoop, calls=%fused_computation.8 | loop fusion | flops 147456 | bytes 1180416 | tf_op jit(solution)/shard_map/div | solution.py:187
  (47 shorter events, 0.4 us)
Async XLA Ops:
  0.1 3.1 %copy-start.4 = (s32[64,8]{0,1:T(8,128)S(1)}, s32[64,8]{0,1:T(8,128)}, u32[]{:S(2)}) copy-start(s32[64,8]{0,1:T(8,128)} %param.4) | copy-start | bytes 6148
  9.8 6.1 %copy-start = (f32[24,65,128]{2,1,0:T(8,128)S(1)}, f32[24,65,128]{2,1,0:T(8,128)}, u32[]{:S(2)}) copy-start(f32[24,65,128]{2,1,0:T(8,128)} %shard_map.37) | copy-start | bytes 2396164
  9.9 20.3 %collective-permute-start.3 = (bf16[1560,128]{1,0:T(8,128)(2,1)S(1)}, bf16[1560,128]{1,0:T(8,128)(2,1)}, u32[]{:S(2)}, u32[]{:S(2)}) collective-permute-start(bf16[1560,128]{1,0:T(8,128)(2,1)S(1)} %reshape.125), channel_id=1, source_target_pairs={{0,4},{4,0},{8,12},{12,8},{1,5},{5,1},{9,13},{13,9},{2,6},{6,2},{1... | collective-permute-start | bytes 1198088 | tf_op jit(solution)/shard_map/ppermute | solution.py:172
  13.0 30.2 %collective-permute-start.7 = (bf16[1560,128]{1,0:T(8,128)(2,1)S(1)}, bf16[1560,128]{1,0:T(8,128)(2,1)}, u32[]{:S(2)}, u32[]{:S(2)}) collective-permute-start(bf16[1560,128]{1,0:T(8,128)(2,1)S(1)} %reshape.125), channel_id=1, source_target_pairs={{0,8},{4,12},{8,0},{12,4},{1,9},{5,13},{9,1},{13,5},{2,10},{6,14},... | collective-permute-start | bytes 1198088 | tf_op jit(solution)/shard_map/ppermute | solution.py:172
  15.6 29.7 %collective-permute-start.11 = (bf16[1560,128]{1,0:T(8,128)(2,1)S(1)}, bf16[1560,128]{1,0:T(8,128)(2,1)}, u32[]{:S(2)}, u32[]{:S(2)}) collective-permute-start(bf16[1560,128]{1,0:T(8,128)(2,1)S(1)} %reshape.125), channel_id=1, source_target_pairs={{0,12},{4,8},{8,4},{12,0},{1,13},{5,9},{9,5},{13,1},{2,14},{6,10},... | collective-permute-start | bytes 1198088 | tf_op jit(solution)/shard_map/ppermute | solution.py:172
  16.9 4.2 %copy-start.5 = (s32[4]{0:T(128)S(1)}, s32[4]{0:T(128)}, u32[]{:S(2)}) copy-start(s32[4]{0:T(128)} %param.5) | copy-start | bytes 52
  18.0 31.9 %collective-permute-start = (bf16[65,6,2,24]{0,3,2,1:T(8,128)(2,1)}, bf16[65,6,2,24]{0,3,2,1:T(8,128)(2,1)S(1)}, u32[]{:S(2)}, u32[]{:S(2)}) collective-permute-start(bf16[65,6,2,24]{0,3,2,1:T(8,128)(2,1)} %get-tuple-element.15), channel_id=1, source_target_pairs={{0,1},{1,2},{2,3},{3,0},{4,5},{5,6},{6,7},{7,4},{8,9},{9,10},{10,1... | collective-permute-start | bytes 112328 | tf_op jit(solution)/shard_map/ppermute | solution.py:105
  18.0 33.5 %collective-permute-start.1 = (bf16[65,6,2,24]{0,3,2,1:T(8,128)(2,1)}, bf16[65,6,2,24]{0,3,2,1:T(8,128)(2,1)S(1)}, u32[]{:S(2)}, u32[]{:S(2)}) collective-permute-start(bf16[65,6,2,24]{0,3,2,1:T(8,128)(2,1)} %get-tuple-element.14), channel_id=1, source_target_pairs={{0,3},{1,0},{2,1},{3,2},{4,7},{5,4},{6,5},{7,6},{8,11},{9,8},{10,9... | collective-permute-start | bytes 112328 | tf_op jit(solution)/shard_map/ppermute | solution.py:105
  30.2 21.9 %collective-permute-start.2 = (bf16[65,6,2,24]{0,3,2,1:T(8,128)(2,1)}, bf16[65,6,2,24]{0,3,2,1:T(8,128)(2,1)}, u32[]{:S(2)}, u32[]{:S(2)}) collective-permute-start(bf16[65,6,2,24]{0,3,2,1:T(8,128)(2,1)} %get-tuple-element.13), channel_id=1, source_target_pairs={{0,2},{1,3},{2,0},{3,1},{4,6},{5,7},{6,4},{7,5},{8,10},{9,11},{10,... | collective-permute-start | bytes 112328 | tf_op jit(solution)/shard_map/ppermute | solution.py:105
  33.9 9.4 %copy-start.1 = (f32[65,48,24]{0,2,1:T(8,128)}, f32[65,48,24]{0,2,1:T(8,128)S(1)}, u32[]{:S(2)}) copy-start(f32[65,48,24]{0,2,1:T(8,128)S(1)} %copy.35) | copy-start | bytes 898564
  43.3 8.9 %collective-permute-start.4 = (bf16[65,6,2,24]{0,3,2,1:T(8,128)(2,1)}, bf16[65,6,2,24]{0,3,2,1:T(8,128)(2,1)S(1)}, u32[]{:S(2)}, u32[]{:S(2)}) collective-permute-start(bf16[65,6,2,24]{0,3,2,1:T(8,128)(2,1)} %get-tuple-element.18), channel_id=1, source_target_pairs={{0,1},{1,2},{2,3},{3,0},{4,5},{5,6},{6,7},{7,4},{8,9},{9,10},{10,1... | collective-permute-start | bytes 112328 | tf_op jit(solution)/shard_map/ppermute | solution.py:105
  45.3 8.5 %collective-permute-start.5 = (bf16[65,6,2,24]{0,3,2,1:T(8,128)(2,1)}, bf16[65,6,2,24]{0,3,2,1:T(8,128)(2,1)}, u32[]{:S(2)}, u32[]{:S(2)}) collective-permute-start(bf16[65,6,2,24]{0,3,2,1:T(8,128)(2,1)} %get-tuple-element.17), channel_id=1, source_target_pairs={{0,3},{1,0},{2,1},{3,2},{4,7},{5,4},{6,5},{7,6},{8,11},{9,8},{10,9... | collective-permute-start | bytes 112328 | tf_op jit(solution)/shard_map/ppermute | solution.py:105
  48.8 1.1 %copy-start.3 = (bf16[65,6,2,24]{0,3,2,1:T(8,128)(2,1)S(1)}, bf16[65,6,2,24]{0,3,2,1:T(8,128)(2,1)}, u32[]{:S(2)}) copy-start(bf16[65,6,2,24]{0,3,2,1:T(8,128)(2,1)} %get-tuple-element.16) | copy-start | bytes 112324
  49.9 7.0 %copy-start.2 = (f32[256,256]{1,0:T(8,128)S(1)}, f32[256,256]{1,0:T(8,128)}, u32[]{:S(2)}) copy-start(f32[256,256]{1,0:T(8,128)} %pad_maximum_fusion.6) | copy-start | bytes 786436
  49.9 4.9 %collective-permute-start.6 = (bf16[65,6,2,24]{0,3,2,1:T(8,128)(2,1)S(1)}, bf16[65,6,2,24]{0,3,2,1:T(8,128)(2,1)S(1)}, u32[]{:S(2)}, u32[]{:S(2)}) collective-permute-start(bf16[65,6,2,24]{0,3,2,1:T(8,128)(2,1)S(1)} %copy-done.3), channel_id=1, source_target_pairs={{0,2},{1,3},{2,0},{3,1},{4,6},{5,7},{6,4},{7,5},{8,10},{9,11},{10,... | collective-permute-start | bytes 112328 | tf_op jit(solution)/shard_map/ppermute | solution.py:105
  51.5 7.4 %collective-permute-start.10 = (bf16[65,6,2,24]{0,3,2,1:T(8,128)(2,1)}, bf16[65,6,2,24]{0,3,2,1:T(8,128)(2,1)S(1)}, u32[]{:S(2)}, u32[]{:S(2)}) collective-permute-start(bf16[65,6,2,24]{0,3,2,1:T(8,128)(2,1)} %get-tuple-element.19), channel_id=1, source_target_pairs={{0,2},{1,3},{2,0},{3,1},{4,6},{5,7},{6,4},{7,5},{8,10},{9,11},{10,... | collective-permute-start | bytes 112328 | tf_op jit(solution)/shard_map/ppermute | solution.py:105
  52.1 8.4 %collective-permute-start.8 = (bf16[65,6,2,24]{0,3,2,1:T(8,128)(2,1)S(1)}, bf16[65,6,2,24]{0,3,2,1:T(8,128)(2,1)S(1)}, u32[]{:S(2)}, u32[]{:S(2)}) collective-permute-start(bf16[65,6,2,24]{0,3,2,1:T(8,128)(2,1)S(1)} %get-tuple-element.21), channel_id=1, source_target_pairs={{0,1},{1,2},{2,3},{3,0},{4,5},{5,6},{6,7},{7,4},{8,9},{9,10},{10,1... | collective-permute-start | bytes 112328 | tf_op jit(solution)/shard_map/ppermute | solution.py:105
  52.1 8.4 %collective-permute-start.9 = (bf16[65,6,2,24]{0,3,2,1:T(8,128)(2,1)S(1)}, bf16[65,6,2,24]{0,3,2,1:T(8,128)(2,1)S(1)}, u32[]{:S(2)}, u32[]{:S(2)}) collective-permute-start(bf16[65,6,2,24]{0,3,2,1:T(8,128)(2,1)S(1)} %get-tuple-element.20), channel_id=1, source_target_pairs={{0,3},{1,0},{2,1},{3,2},{4,7},{5,4},{6,5},{7,6},{8,11},{9,8},{10,9... | collective-permute-start | bytes 112328 | tf_op jit(solution)/shard_map/ppermute | solution.py:105
  53.9 6.6 %collective-permute-start.12 = (bf16[65,6,2,24]{0,3,2,1:T(8,128)(2,1)S(1)}, bf16[65,6,2,24]{0,3,2,1:T(8,128)(2,1)S(1)}, u32[]{:S(2)}, u32[]{:S(2)}) collective-permute-start(bf16[65,6,2,24]{0,3,2,1:T(8,128)(2,1)S(1)} %get-tuple-element.24), channel_id=1, source_target_pairs={{0,1},{1,2},{2,3},{3,0},{4,5},{5,6},{6,7},{7,4},{8,9},{9,10},{10,1... | collective-permute-start | bytes 112328 | tf_op jit(solution)/shard_map/ppermute | solution.py:105
  54.8 5.7 %collective-permute-start.13 = (bf16[65,6,2,24]{0,3,2,1:T(8,128)(2,1)S(1)}, bf16[65,6,2,24]{0,3,2,1:T(8,128)(2,1)S(1)}, u32[]{:S(2)}, u32[]{:S(2)}) collective-permute-start(bf16[65,6,2,24]{0,3,2,1:T(8,128)(2,1)S(1)} %get-tuple-element.23), channel_id=1, source_target_pairs={{0,3},{1,0},{2,1},{3,2},{4,7},{5,4},{6,5},{7,6},{8,11},{9,8},{10,9... | collective-permute-start | bytes 112328 | tf_op jit(solution)/shard_map/ppermute | solution.py:105
  58.9 4.4 %collective-permute-start.14 = (bf16[65,6,2,24]{0,3,2,1:T(8,128)(2,1)S(1)}, bf16[65,6,2,24]{0,3,2,1:T(8,128)(2,1)S(1)}, u32[]{:S(2)}, u32[]{:S(2)}) collective-permute-start(bf16[65,6,2,24]{0,3,2,1:T(8,128)(2,1)S(1)} %get-tuple-element.22), channel_id=1, source_target_pairs={{0,2},{1,3},{2,0},{3,1},{4,6},{5,7},{6,4},{7,5},{8,10},{9,11},{10,... | collective-permute-start | bytes 112328 | tf_op jit(solution)/shard_map/ppermute | solution.py:105
